TPU v7x, 128 devices: a whole 4x4x4 slice. The times are simulated.
128 devices in a mesh: group: 4 (over z), dev: 32 (over y, x, core).
Axes of the slice: x: 4, y: 4, z: 4, core: 2. Of those that a mesh axis runs over, the one named last changes fastest.
Arguments:
- tokens: bfloat16 [16384, 3584], P(('group', 'dev')), may hold values from -1.5 to 1.5
- out_grad: bfloat16 [16384, 3584], P(('group', 'dev')), may hold values from -0.59765625 to 0.59765625
- gate_weights: bfloat16 [16384, 8], P(('group', 'dev')), may hold values from 0.099609375 to 1
- expert_ids: int32 [16384, 8], P(('group', 'dev')), may hold values from 0 to 127, as said below
- slot_ids: int32 [16384, 8], P(('group', 'dev')), may hold values from 0 to 9, as said below
- up_weight: bfloat16 [128, 3584, 1024], P(('group', 'dev')), may hold values from -0.40039062 to 0.40039062
- down_weight: bfloat16 [128, 1024, 3584], P(('group', 'dev')), may hold values from -0.1875 to 0.1875
Outputs:
- token_grad: bfloat16 [16384, 3584], P(('group', 'dev'))
- gate_grad: bfloat16 [16384, 8], P(('group', 'dev'))
Inputs may be any that keep to these rules, and one draw needn't show every extreme that they name: `expert_ids`: expert e lies in group e // 32 and on the device of index e along group+dev. Each token names 8 different experts, 4 in each of exactly 2 groups. In the rows of one device no expert is named more than 10 times and some expert exactly 10 times; no group is named by more than 80 rows and some group by exactly 80. `slot_ids`: in the rows of one device, two entries that name the same expert have different slots.
All inputs are finite; a program needn't handle non-finite values.
Results may differ from a plain program's by a relative error of at most 0.009.
Values may be sent and summed in bfloat16 or wider, within the bound.
No kernel may reach another device: no remote copies, remote signals or barrier semaphores. Data moves between devices by JAX's collectives and lax.ppermute only.
A program may use at most 192 MiB of HBM per device.

v0:
```python
import jax
import jax.numpy as jnp
from jax import lax
from jax.sharding import PartitionSpec as P

TOPK = 8


def silu_slope(values):
    sigmoid_up = jax.nn.sigmoid(values)
    return sigmoid_up * (1.0 + values * (1.0 - sigmoid_up))


def expert_rows(token_rows, grad_rows, gate_rows, up_matrix, down_matrix):
    raised = jnp.dot(token_rows, up_matrix, preferred_element_type=jnp.float32)
    backward = lax.dot_general(
        grad_rows, down_matrix, (((1,), (1,)), ((), ())), preferred_element_type=jnp.float32
    )
    gate_grad = jnp.sum(jax.nn.silu(raised) * backward, axis=1).astype(jnp.bfloat16)
    inner_grad = (gate_rows.astype(jnp.float32)[:, None] * backward * silu_slope(raised)).astype(
        jnp.bfloat16
    )
    contrib = lax.dot_general(
        inner_grad, up_matrix, (((1,), (1,)), ((), ())), preferred_element_type=jnp.float32
    ).astype(jnp.bfloat16)
    return (contrib, gate_grad)


def shards(tokens, out_grad, gate_weights, expert_ids, slot_ids, up_weight, down_weight):
    rows_dev = tokens.shape[0]
    features = tokens.shape[1]
    groups = lax.axis_size("group")
    per_group = lax.axis_size("dev")
    experts = groups * per_group
    capacity = 5 * rows_dev * TOPK // (4 * experts)
    slots_all = experts * capacity
    entries = rows_dev * TOPK
    up_matrix = up_weight[0]
    down_matrix = down_weight[0]
    group_of = expert_ids // per_group
    zero_row = jnp.zeros((1, features), jnp.bfloat16)
    token_pad = jnp.concatenate([tokens, zero_row])
    grad_pad = jnp.concatenate([out_grad, zero_row])
    gate_flat = jnp.concatenate([gate_weights.reshape(-1), jnp.zeros((1,), jnp.bfloat16)])
    target = (expert_ids * capacity + slot_ids).reshape(-1)
    slot_table = (
        jnp.full((slots_all,), entries, jnp.int32)
        .at[target]
        .set(jnp.arange(entries, dtype=jnp.int32))
    )
    anchor = slot_table // TOPK
    arrived = (
        lax.all_to_all(
            token_pad[anchor].reshape(experts, capacity, features),
            ("group", "dev"),
            split_axis=0,
            concat_axis=0,
            tiled=True,
        ),
        lax.all_to_all(
            grad_pad[anchor].reshape(experts, capacity, features),
            ("group", "dev"),
            split_axis=0,
            concat_axis=0,
            tiled=True,
        ),
        lax.all_to_all(
            gate_flat[slot_table].reshape(experts, capacity),
            ("group", "dev"),
            split_axis=0,
            concat_axis=0,
            tiled=True,
        ),
    )
    contrib, gate_rows = expert_rows(
        arrived[0].reshape(slots_all, features),
        arrived[1].reshape(slots_all, features),
        arrived[2].reshape(slots_all),
        up_matrix,
        down_matrix,
    )
    returned_rows = (
        lax.all_to_all(
            contrib.reshape(experts, capacity, features),
            ("group", "dev"),
            split_axis=0,
            concat_axis=0,
            tiled=True,
        ),
        lax.all_to_all(
            gate_rows.reshape(experts, capacity),
            ("group", "dev"),
            split_axis=0,
            concat_axis=0,
            tiled=True,
        ),
    )
    gathered = (
        returned_rows[0].reshape(slots_all, features)[target].reshape(rows_dev, TOPK, features)
    )
    gate_grad = returned_rows[1].reshape(-1)[target].reshape(rows_dev, TOPK)
    same_group = group_of == group_of[:, :1]
    selector = jnp.stack([same_group, jnp.logical_not(same_group)], axis=1).astype(jnp.bfloat16)
    halves = jnp.einsum(
        "tpk,tkd->tpd", selector, gathered, preferred_element_type=jnp.float32
    ).astype(jnp.bfloat16)
    token_grad = jnp.sum(halves.astype(jnp.float32), axis=1).astype(jnp.bfloat16)
    return (token_grad, gate_grad)


def solution(mesh):
    in_specs = (
        P(("group", "dev"), None),
        P(("group", "dev"), None),
        P(("group", "dev"), None),
        P(("group", "dev"), None),
        P(("group", "dev"), None),
        P(("group", "dev"), None, None),
        P(("group", "dev"), None, None),
    )
    out_specs = (P(("group", "dev"), None), P(("group", "dev"), None))
    return jax.shard_map(shards, mesh=mesh, in_specs=in_specs, out_specs=out_specs, check_vma=False)
```

profile of v0, /device:TPU:84, one launch (start us, length us, event | category | flops | bytes accessed | tf_op | source)
XLA Modules:
  0.0 809.4 jit_solution(9729953009175875647)
XLA Ops:
  0.6 1.3 multiply_add_fusion
  1.9 0.1 copy.29
  2.0 0.1 reshape.95
  2.1 0.0 copy-start.1
  2.2 4.3 scatter_custom_fusion
  6.5 0.0 copy-done.1
  6.5 0.8 copy.28
  7.3 0.1 reshape.94
  7.4 8.0 gather_fusion
  15.4 0.8 all_to_all.25
  16.2 9.9 %all-to-all-start = ((bf16[128,1,10]{2,1,0:T(2,128)(2,1)}), bf16[128,1,10]{2,1,0:T(2,128)(2,1)S(1)}, u32[]{:S(2)}, u32[]{:S(2)}) async-start(bf16[128,1,10]{2,1,0:T(2,128)(2,1)} %all_to_all.25), calls=%async_computation | async-start | bytes 131072 | tf_op jit(solution)/shard_map/all_to_all | solution.py:67
  26.2 1.2 concatenate.11
  27.4 7.9 gather_fusion.2
  35.3 14.2 %reshape.98 = bf16[128,10,3584]{2,1,0:T(8,128)(2,1)} reshape(bf16[1280,3584]{1,0:T(8,128)(2,1)} %gather_fusion.2) | data formatting | bytes 18350080 | tf_op jit(solution)/shard_map/reshape | solution.py:54
  49.6 0.0 copy-start
  49.6 0.0 all-to-all-done
  49.6 10.2 %all-to-all-start.2 = ((bf16[128,10,3584]{2,1,0:T(8,128)(2,1)}), bf16[128,10,3584]{2,1,0:T(8,128)(2,1)}, u32[]{:S(2)}, u32[]{:S(2)}) async-start(bf16[128,10,3584]{2,1,0:T(8,128)(2,1)} %reshape.98), calls=%async_computation.2 | async-start | bytes 29360128 | tf_op jit(solution)/shard_map/all_to_all | solution.py:53
  59.7 0.0 copy-done
  59.7 0.1 concatenate.10
  59.8 7.8 gather_fusion.1
  67.6 14.2 %reshape.96 = bf16[128,10,3584]{2,1,0:T(8,128)(2,1)} reshape(bf16[1280,3584]{1,0:T(8,128)(2,1)} %gather_fusion.1) | data formatting | bytes 18350080 | tf_op jit(solution)/shard_map/reshape | solution.py:61
  81.8 175.6 %all-to-all-done.2 = bf16[128,10,3584]{2,1,0:T(8,128)(2,1)} async-done(((bf16[128,10,3584]{2,1,0:T(8,128)(2,1)}), bf16[128,10,3584]{2,1,0:T(8,128)(2,1)}, u32[]{:S(2)}, u32[]{:S(2)}) %all-to-all-start.2) | async-done | bytes 9175072 | tf_op jit(solution)/shard_map/all_to_all | solution.py:53
  257.4 12.5 %all-to-all-start.1 = ((bf16[128,10,3584]{2,1,0:T(8,128)(2,1)}), bf16[128,10,3584]{2,1,0:T(8,128)(2,1)}, u32[]{:S(2)}, u32[]{:S(2)}) async-start(bf16[128,10,3584]{2,1,0:T(8,128)(2,1)} %reshape.96), calls=%async_computation.1 | async-start | bytes 29360128 | tf_op jit(solution)/shard_map/all_to_all | solution.py:60
  269.9 0.2 convert_reduce_fusion
  270.1 0.1 reshape.105
  270.2 14.7 %reshape.99 = bf16[1280,3584]{1,0:T(8,128)(2,1)} reshape(bf16[128,10,3584]{2,1,0:T(8,128)(2,1)} %all-to-all-done.2) | data formatting | bytes 18350080 | tf_op jit(solution)/shard_map/reshape | solution.py:76
  284.9 15.7 %fusion.3 = f32[1280,1024]{0,1:T(8,128)} fusion(bf16[1280,3584]{1,0:T(8,128)(2,1)} %reshape.99, bf16[1,3584,1024]{2,1,0:T(8,128)(2,1)} %param.12), kind=kOutput, calls=%fused_computation.10 | convolution fusion | flops 9395240960 | bytes 21757952 | tf_op jit(solution)/shard_map/dot_general | solution.py:15
  300.6 174.5 %all-to-all-done.1 = bf16[128,10,3584]{2,1,0:T(8,128)(2,1)} async-done(((bf16[128,10,3584]{2,1,0:T(8,128)(2,1)}), bf16[128,10,3584]{2,1,0:T(8,128)(2,1)}, u32[]{:S(2)}, u32[]{:S(2)}) %all-to-all-start.1) | async-done | bytes 9175072 | tf_op jit(solution)/shard_map/all_to_all | solution.py:60
  475.1 14.7 %reshape.97 = bf16[1280,3584]{1,0:T(8,128)(2,1)} reshape(bf16[128,10,3584]{2,1,0:T(8,128)(2,1)} %all-to-all-done.1) | data formatting | bytes 18350080 | tf_op jit(solution)/shard_map/reshape | solution.py:77
  489.8 17.2 %multiply_reduce_fusion = (bf16[1280]{0:T(1024)(128)(2,1)S(1)}, f32[1280,1024]{0,1:T(8,128)}) fusion(f32[1280,1024]{0,1:T(8,128)} %fusion.3, bf16[1280,3584]{1,0:T(8,128)(2,1)} %reshape.97, bf16[1,1024,3584]{2,1,0:T(8,128)(2,1)} %param.13), kind=kOutput, calls=%fused_computation.14 | convolution fusion | flops 9403104256 | bytes 27003392 | tf_op jit(solution)/shard_map/dot_general | solution.py:16
  507.0 0.8 convert_element_type.44
  507.8 9.8 %all-to-all-start.4 = ((bf16[128,1,10]{2,1,0:T(2,128)(2,1)}), bf16[128,1,10]{2,1,0:T(2,128)(2,1)S(1)}, u32[]{:S(2)}, u32[]{:S(2)}) async-start(bf16[128,1,10]{2,1,0:T(2,128)(2,1)} %convert_element_type.44), calls=%async_computation.4 | async-start | bytes 131072 | tf_op jit(solution)/shard_map/all_to_all | solution.py:90
  517.5 20.3 %convolution_convert_fusion = bf16[1280,3584]{1,0:T(8,128)(2,1)} fusion(bf16[1,3584,1024]{2,1,0:T(8,128)(2,1)} %param.12, f32[1280,1024]{0,1:T(8,128)} %fusion.3, f32[1280,1024]{0,1:T(8,128)} %get-tuple-element.15, f32[1280]{0:T(1024)S(1)} %reshape.105), kind=kOutput, calls=%fused_computation.6 | convolution fusion | flops 9412935680 | bytes 27005952 | tf_op jit(solution)/shard_map/dot_general | solution.py:23
  537.9 14.2 %reshape.100 = bf16[128,10,3584]{2,1,0:T(8,128)(2,1)} reshape(bf16[1280,3584]{1,0:T(8,128)(2,1)} %convolution_convert_fusion) | data formatting | bytes 18350080 | tf_op jit(solution)/shard_map/reshape | solution.py:84
  552.1 0.0 copy-start.3
  552.1 0.0 copy-start.2
  552.1 0.0 all-to-all-done.4
  552.1 10.2 %all-to-all-start.3 = ((bf16[128,10,3584]{2,1,0:T(8,128)(2,1)}), bf16[128,10,3584]{2,1,0:T(8,128)(2,1)}, u32[]{:S(2)}, u32[]{:S(2)}) async-start(bf16[128,10,3584]{2,1,0:T(8,128)(2,1)} %reshape.100), calls=%async_computation.3 | async-start | bytes 29360128 | tf_op jit(solution)/shard_map/all_to_all | solution.py:83
  562.3 0.0 copy-done.3
  562.4 0.2 copy.31
  562.5 0.0 copy-done.2
  562.6 0.2 reduce.2
  562.8 0.1 reshape.103
  562.9 6.8 gather_fusion.4
  569.7 0.1 reshape.104
  569.8 0.7 copy.33
  570.5 197.1 %all-to-all-done.3 = bf16[128,10,3584]{2,1,0:T(8,128)(2,1)} async-done(((bf16[128,10,3584]{2,1,0:T(8,128)(2,1)}), bf16[128,10,3584]{2,1,0:T(8,128)(2,1)}, u32[]{:S(2)}, u32[]{:S(2)}) %all-to-all-start.3) | async-done | bytes 9175072 | tf_op jit(solution)/shard_map/all_to_all | solution.py:83
  767.6 14.6 %reshape.101 = bf16[1280,3584]{1,0:T(8,128)(2,1)} reshape(bf16[128,10,3584]{2,1,0:T(8,128)(2,1)} %all-to-all-done.3) | data formatting | bytes 18350080 | tf_op jit(solution)/shard_map/reshape | solution.py:99
  782.2 18.6 %gather_fusion.3 = bf16[1024,3584]{1,0:T(8,128)(2,1)} fusion(bf16[1280,3584]{1,0:T(8,128)(2,1)} %reshape.101, s32[1024]{0:T(1024)S(1)} %broadcast_clamp_fusion), kind=kCustom, calls=%fused_computation.3 | custom fusion | bytes 14684160 | tf_op jit(solution)/shard_map/gather | solution.py:99
  800.8 8.7 %fusion.12 = bf16[128,3584]{1,0:T(8,128)(2,1)} fusion(pred[128,2,8]{2,1,0:T(4,128)(4,1)S(1)} %copy.31, bf16[1024,3584]{1,0:T(8,128)(2,1)} %gather_fusion.3), kind=kOutput, calls=%fused_computation.20 | convolution fusion | flops 16056320 | bytes 8259584 | tf_op jit(solution)/shard_map/tpk,tkd->tpd/dot_general | solution.py:104
  (9 shorter events, 0.1 us)
Async XLA Ops:
  2.1 4.3 copy-start.1
  16.2 33.3 %all-to-all-start = ((bf16[128,1,10]{2,1,0:T(2,128)(2,1)}), bf16[128,1,10]{2,1,0:T(2,128)(2,1)S(1)}, u32[]{:S(2)}, u32[]{:S(2)}) async-start(bf16[128,1,10]{2,1,0:T(2,128)(2,1)} %all_to_all.25), calls=%async_computation | async-start | bytes 131072 | tf_op jit(solution)/shard_map/all_to_all | solution.py:67
  49.6 10.2 %copy-start = (bf16[128,3584]{1,0:T(8,128)(2,1)S(1)}, bf16[128,3584]{1,0:T(8,128)(2,1)}, u32[]{:S(2)}) copy-start(bf16[128,3584]{1,0:T(8,128)(2,1)} %param.8) | copy-start | bytes 2752516
  49.6 207.8 %all-to-all-start.2 = ((bf16[128,10,3584]{2,1,0:T(8,128)(2,1)}), bf16[128,10,3584]{2,1,0:T(8,128)(2,1)}, u32[]{:S(2)}, u32[]{:S(2)}) async-start(bf16[128,10,3584]{2,1,0:T(8,128)(2,1)} %reshape.98), calls=%async_computation.2 | async-start | bytes 29360128 | tf_op jit(solution)/shard_map/all_to_all | solution.py:53
  257.4 217.7 %all-to-all-start.1 = ((bf16[128,10,3584]{2,1,0:T(8,128)(2,1)}), bf16[128,10,3584]{2,1,0:T(8,128)(2,1)}, u32[]{:S(2)}, u32[]{:S(2)}) async-start(bf16[128,10,3584]{2,1,0:T(8,128)(2,1)} %reshape.96), calls=%async_computation.1 | async-start | bytes 29360128 | tf_op jit(solution)/shard_map/all_to_all | solution.py:60
  507.8 44.4 %all-to-all-start.4 = ((bf16[128,1,10]{2,1,0:T(2,128)(2,1)}), bf16[128,1,10]{2,1,0:T(2,128)(2,1)S(1)}, u32[]{:S(2)}, u32[]{:S(2)}) async-start(bf16[128,1,10]{2,1,0:T(2,128)(2,1)} %convert_element_type.44), calls=%async_computation.4 | async-start | bytes 131072 | tf_op jit(solution)/shard_map/all_to_all | solution.py:90
  552.1 10.2 %copy-start.3 = (s32[128,8]{0,1:T(8,128)S(1)}, s32[128,8]{0,1:T(8,128)}, u32[]{:S(2)}) copy-start(s32[128,8]{0,1:T(8,128)} %get-tuple-element.13) | copy-start | bytes 12292
  552.1 10.4 %copy-start.2 = (s32[1024,1]{0,1:T(1,128)S(1)}, s32[1024,1]{0,1:T(1,128)}, u32[]{:S(2)}) copy-start(s32[1024,1]{0,1:T(1,128)} %copy-done.1) | copy-start | bytes 12292
  552.1 215.4 %all-to-all-start.3 = ((bf16[128,10,3584]{2,1,0:T(8,128)(2,1)}), bf16[128,10,3584]{2,1,0:T(8,128)(2,1)}, u32[]{:S(2)}, u32[]{:S(2)}) async-start(bf16[128,10,3584]{2,1,0:T(8,128)(2,1)} %reshape.100), calls=%async_computation.3 | async-start | bytes 29360128 | tf_op jit(solution)/shard_map/all_to_all | solution.py:83
where the time goes:
time: 812 us; the launch traced here: 809 us
  waiting for transfers between devices  547 us (67%)
  local copies, waits for them, and re-layouts  145 us (18%)
  matrix products  61.9 us (8%)
  starting transfers between devices  52.5 us (6%)
    all_to_all x1, waiting for transfers between devices, shards(): lax.all_to_all(contrib.reshape(experts, capacity, features), ('group', 'd...  197 us
    all_to_all x1, waiting for transfers between devices, shards(): lax.all_to_all(token_pad[anchor].reshape(experts, capacity, features), ('...  176 us
    all_to_all x1, waiting for transfers between devices, shards(): lax.all_to_all(grad_pad[anchor].reshape(experts, capacity, features), ('g...  175 us
    dot_general x1, matrix products, expert_rows(): lax.dot_general(inner_grad, up_matrix, (((1,), (1,)), ((), ())), preferre...  20.3 us
    gather x1, local copies, waits for them, and re-layouts, shards(): returned_rows[0].reshape(slots_all, features)[target]  18.6 us
    dot_general x1, matrix products, expert_rows(): lax.dot_general(grad_rows, down_matrix, (((1,), (1,)), ((), ())), preferr...  17.2 us
  transfers between devices with their start and end apart: 5, of which 3 were waited for; matrix products, arithmetic and copies ran while one was open for 15% of the time, Pallas kernels for 0%

commit v1 on v0

--- a/solution.py
+++ b/solution.py
@@ -4,6 +4,7 @@
 from jax.sharding import PartitionSpec as P
 
 TOPK = 8
+LANES = 128
 
 
 def silu_slope(values):
@@ -26,6 +27,10 @@
     return (contrib, gate_grad)
 
 
+def exchange(x):
+    return lax.all_to_all(x, ("group", "dev"), split_axis=0, concat_axis=0, tiled=True)
+
+
 def shards(tokens, out_grad, gate_weights, expert_ids, slot_ids, up_weight, down_weight):
     rows_dev = tokens.shape[0]
     features = tokens.shape[1]
@@ -38,9 +43,11 @@
     up_matrix = up_weight[0]
     down_matrix = down_weight[0]
     group_of = expert_ids // per_group
-    zero_row = jnp.zeros((1, features), jnp.bfloat16)
-    token_pad = jnp.concatenate([tokens, zero_row])
-    grad_pad = jnp.concatenate([out_grad, zero_row])
+    both = 2 * features
+    blocks = both // LANES
+    joined = jnp.concatenate(
+        [jnp.concatenate([tokens, out_grad], axis=1), jnp.zeros((1, both), jnp.bfloat16)]
+    ).reshape(rows_dev + 1, blocks, LANES)
     gate_flat = jnp.concatenate([gate_weights.reshape(-1), jnp.zeros((1,), jnp.bfloat16)])
     target = (expert_ids * capacity + slot_ids).reshape(-1)
     slot_table = (
@@ -49,56 +56,21 @@
         .set(jnp.arange(entries, dtype=jnp.int32))
     )
     anchor = slot_table // TOPK
-    arrived = (
-        lax.all_to_all(
-            token_pad[anchor].reshape(experts, capacity, features),
-            ("group", "dev"),
-            split_axis=0,
-            concat_axis=0,
-            tiled=True,
-        ),
-        lax.all_to_all(
-            grad_pad[anchor].reshape(experts, capacity, features),
-            ("group", "dev"),
-            split_axis=0,
-            concat_axis=0,
-            tiled=True,
-        ),
-        lax.all_to_all(
-            gate_flat[slot_table].reshape(experts, capacity),
-            ("group", "dev"),
-            split_axis=0,
-            concat_axis=0,
-            tiled=True,
-        ),
-    )
+    sent = joined[anchor].reshape(experts, capacity * blocks, LANES)
+    arrived = exchange(sent).reshape(slots_all, both)
+    gate_in = exchange(gate_flat[slot_table].reshape(experts, capacity))
     contrib, gate_rows = expert_rows(
-        arrived[0].reshape(slots_all, features),
-        arrived[1].reshape(slots_all, features),
-        arrived[2].reshape(slots_all),
+        arrived[:, :features],
+        arrived[:, features:],
+        gate_in.reshape(slots_all),
         up_matrix,
         down_matrix,
     )
-    returned_rows = (
-        lax.all_to_all(
-            contrib.reshape(experts, capacity, features),
-            ("group", "dev"),
-            split_axis=0,
-            concat_axis=0,
-            tiled=True,
-        ),
-        lax.all_to_all(
-            gate_rows.reshape(experts, capacity),
-            ("group", "dev"),
-            split_axis=0,
-            concat_axis=0,
-            tiled=True,
-        ),
-    )
-    gathered = (
-        returned_rows[0].reshape(slots_all, features)[target].reshape(rows_dev, TOPK, features)
-    )
-    gate_grad = returned_rows[1].reshape(-1)[target].reshape(rows_dev, TOPK)
+    half_blocks = capacity // 2 * both // LANES
+    returned = exchange(contrib.reshape(experts, half_blocks, LANES)).reshape(slots_all, features)
+    gate_back = exchange(gate_rows.reshape(experts, capacity))
+    gathered = returned[target].reshape(rows_dev, TOPK, features)
+    gate_grad = gate_back.reshape(-1)[target].reshape(rows_dev, TOPK)
     same_group = group_of == group_of[:, :1]
     selector = jnp.stack([same_group, jnp.logical_not(same_group)], axis=1).astype(jnp.bfloat16)
     halves = jnp.einsum(

time: 812 us -> 585 us (0.72)
  waiting for transfers between devices: 547 us -> 362 us
  local copies, waits for them, and re-layouts: 145 us -> 111 us
  starting transfers between devices: 52.5 us -> 42.5 us
    all_to_all x5 -> x4, waiting for transfers between devices: 547 us -> 362 us  [exchange(): lax.all_to_all(x, ('group', 'dev'), split_axis=0, concat_axis=0, tiled=True)]
    reshape x8 -> x6, local copies, waits for them, and re-layouts: 86.9 us -> 61.3 us  [the longest x1 26.3 us: shards(): arrived = exchange(sent).reshape(slots_all, both)]
    all_to_all x5 -> x4, starting transfers between devices: 52.5 us -> 42.5 us  [exchange(): lax.all_to_all(x, ('group', 'dev'), split_axis=0, concat_axis=0, tiled=True)]
    gather x5 -> x4, local copies, waits for them, and re-layouts: 49.1 us -> 41.8 us  [the longest x1 18.6 us: shards(): gathered = returned[target].reshape(rows_dev, TOPK, features)]
  transfers between devices with their start and end apart: 5 -> 4, of which waited for: 3 -> 2; matrix products, arithmetic and copies ran while one was open for 15% -> 10% of each run, Pallas kernels for 0% -> 0%
where the time goes in v1:
time: 585 us; the launch traced here: 580 us
  waiting for transfers between devices  362 us (62%)
  local copies, waits for them, and re-layouts  111 us (19%)
  matrix products  62.1 us (11%)
  starting transfers between devices  42.5 us (7%)
    all_to_all x4, waiting for transfers between devices, exchange(): lax.all_to_all(x, ('group', 'dev'), split_axis=0, concat_axis=0, tiled=True)  362 us
    all_to_all x4, starting transfers between devices, exchange(): lax.all_to_all(x, ('group', 'dev'), split_axis=0, concat_axis=0, tiled=True)  42.5 us
    reshape x1, local copies, waits for them, and re-layouts, shards(): arrived = exchange(sent).reshape(slots_all, both)  26.3 us
    dot_general x1, matrix products, expert_rows(): lax.dot_general(inner_grad, up_matrix, (((1,), (1,)), ((), ())), preferre...  20.4 us
    gather x1, local copies, waits for them, and re-layouts, shards(): gathered = returned[target].reshape(rows_dev, TOPK, features)  18.6 us
    dot_general x1, matrix products, expert_rows(): lax.dot_general(grad_rows, down_matrix, (((1,), (1,)), ((), ())), preferr...  18.3 us
    reshape x1, local copies, waits for them, and re-layouts, shards(): contrib.reshape(experts, half_blocks, LANES)  17.6 us
    reshape x1, local copies, waits for them, and re-layouts, shards(): exchange(contrib.reshape(experts, half_blocks, LANES))  16.9 us
  transfers between devices with their start and end apart: 4, of which 2 were waited for; matrix products, arithmetic and copies ran while one was open for 10% of the time, Pallas kernels for 0%

profile of v1, /device:TPU:84, one launch (start us, length us, event | category | flops | bytes accessed | tf_op | source)
XLA Modules:
  0.0 580.1 jit_solution(10802313233600870386)
XLA Ops:
  0.6 0.0 copy-start.1
  0.6 0.0 copy-start
  0.7 0.8 multiply_add_fusion
  1.5 0.1 copy.29
  1.6 0.1 reshape.92
  1.7 4.3 scatter_custom_fusion
  6.1 0.8 copy.28
  6.9 0.1 reshape.91
  7.0 8.0 %gather_fusion = bf16[1280]{0:T(1024)(128)(2,1)S(1)} fusion(bf16[1025]{0:T(1024)(128)(2,1)S(1)} %pad_maximum_fusion, s32[2048]{0:T(1024)S(1)} %get-tuple-element.17), kind=kCustom, calls=%fused_computation | custom fusion | bytes 10240 | tf_op jit(solution)/shard_map/gather | solution.py:61
  15.0 0.8 all_to_all.21
  15.8 9.9 %all-to-all-start = ((bf16[128,1,10]{2,1,0:T(2,128)(2,1)}), bf16[128,1,10]{2,1,0:T(2,128)(2,1)S(1)}, u32[]{:S(2)}, u32[]{:S(2)}) async-start(bf16[128,1,10]{2,1,0:T(2,128)(2,1)} %all_to_all.21), calls=%async_computation | async-start | bytes 131072 | tf_op jit(solution)/shard_map/all_to_all | solution.py:31
  25.7 0.0 copy-done.1
  25.7 0.0 copy-done
  25.7 0.2 fusion.16
  25.9 0.4 copy.34
  26.3 0.3 slice.22
  26.7 8.4 %gather_fusion.1 = bf16[1280,56,128]{2,1,0:T(8,128)(2,1)} fusion(bf16[129,56,128]{2,1,0:T(8,128)(2,1)S(1)} %slice.22, s32[2048]{0:T(1024)S(1)} %get-tuple-element.16), kind=kCustom, calls=%fused_computation.1 | custom fusion | bytes 36705280 | tf_op jit(solution)/shard_map/gather | solution.py:59
  35.1 0.0 all-to-all-done
  35.1 10.2 %all-to-all-start.1 = ((bf16[128,560,128]{2,1,0:T(8,128)(2,1)}), bf16[128,560,128]{2,1,0:T(8,128)(2,1)}, u32[]{:S(2)}, u32[]{:S(2)}) async-start(bf16[128,560,128]{2,1,0:T(8,128)(2,1)} %bitcast.28), calls=%async_computation.1 | async-start | bytes 36700160 | tf_op jit(solution)/shard_map/all_to_all | solution.py:31
  45.2 0.2 convert_reduce_fusion
  45.4 0.1 reshape.101
  45.6 261.5 %all-to-all-done.1 = bf16[128,560,128]{2,1,0:T(8,128)(2,1)} async-done(((bf16[128,560,128]{2,1,0:T(8,128)(2,1)}), bf16[128,560,128]{2,1,0:T(8,128)(2,1)}, u32[]{:S(2)}, u32[]{:S(2)}) %all-to-all-start.1) | async-done | bytes 18350112 | tf_op jit(solution)/shard_map/all_to_all | solution.py:31
  307.0 26.3 %reshape.95 = bf16[1280,7168]{1,0:T(8,128)(2,1)} reshape(bf16[128,560,128]{2,1,0:T(8,128)(2,1)} %all-to-all-done.1) | data formatting | bytes 36700160 | tf_op jit(solution)/shard_map/reshape | solution.py:60
  333.3 14.7 %fusion = f32[1280,1024]{0,1:T(8,128)S(1)} fusion(bf16[1280,7168]{1,0:T(8,128)(2,1)} %reshape.95, bf16[1,3584,1024]{2,1,0:T(8,128)(2,1)} %param.12), kind=kOutput, calls=%fused_computation.6 | convolution fusion | flops 9395240960 | bytes 21757952 | tf_op jit(solution)/shard_map/dot_general | solution.py:16
  348.1 0.0 copy-start.2
  348.1 18.3 %multiply_reduce_fusion = (bf16[1280]{0:T(1024)(128)(2,1)S(1)}, f32[1280,1024]{0,1:T(8,128)}) fusion(f32[1280,1024]{0,1:T(8,128)S(1)} %fusion, bf16[1,1024,3584]{2,1,0:T(8,128)(2,1)} %param.13, bf16[1280,7168]{1,0:T(8,128)(2,1)} %reshape.95), kind=kOutput, calls=%fused_computation.15 | convolution fusion | flops 9403104256 | bytes 27003392 | tf_op jit(solution)/shard_map/dot_general | solution.py:17
  366.4 0.0 copy-done.2
  366.4 0.8 convert_element_type.44
  367.2 12.2 %all-to-all-start.3 = ((bf16[128,1,10]{2,1,0:T(2,128)(2,1)}), bf16[128,1,10]{2,1,0:T(2,128)(2,1)S(1)}, u32[]{:S(2)}, u32[]{:S(2)}) async-start(bf16[128,1,10]{2,1,0:T(2,128)(2,1)} %convert_element_type.44), calls=%async_computation.3 | async-start | bytes 131072 | tf_op jit(solution)/shard_map/all_to_all | solution.py:31
  379.4 20.4 %convolution_convert_fusion = bf16[1280,3584]{1,0:T(8,128)(2,1)} fusion(bf16[1,3584,1024]{2,1,0:T(8,128)(2,1)} %param.12, f32[1280,1024]{0,1:T(8,128)} %copy-done.2, f32[1280,1024]{0,1:T(8,128)} %get-tuple-element.15, f32[1280]{0:T(1024)S(1)} %reshape.101), kind=kOutput, calls=%fused_computation.5 | convolution fusion | flops 9412935680 | bytes 27005952 | tf_op jit(solution)/shard_map/dot_general | solution.py:24
  399.8 17.6 %reshape.96 = bf16[128,280,128]{2,1,0:T(8,128)(2,1)} reshape(bf16[1280,3584]{1,0:T(8,128)(2,1)} %convolution_convert_fusion) | data formatting | bytes 18350080 | tf_op jit(solution)/shard_map/reshape | solution.py:70
  417.4 0.0 all-to-all-done.3
  417.4 10.2 %all-to-all-start.2 = ((bf16[128,280,128]{2,1,0:T(8,128)(2,1)}), bf16[128,280,128]{2,1,0:T(8,128)(2,1)}, u32[]{:S(2)}, u32[]{:S(2)}) async-start(bf16[128,280,128]{2,1,0:T(8,128)(2,1)} %reshape.96), calls=%async_computation.2 | async-start | bytes 18350080 | tf_op jit(solution)/shard_map/all_to_all | solution.py:31
  427.6 0.2 copy.31
  427.8 0.2 reduce.2
  428.0 0.1 reshape.99
  428.1 6.8 %gather_fusion.3 = bf16[1024]{0:T(1024)(128)(2,1)S(1)} fusion(bf16[1280]{0:T(1024)(128)(2,1)S(1)} %reshape.99, s32[1024]{0:T(1024)S(1)} %broadcast_clamp_fusion), kind=kCustom, calls=%fused_computation.3 | custom fusion | bytes 8192 | tf_op jit(solution)/shard_map/gather | solution.py:73
  434.9 0.1 reshape.100
  435.0 0.7 copy.33
  435.7 100.3 %all-to-all-done.2 = bf16[128,280,128]{2,1,0:T(8,128)(2,1)} async-done(((bf16[128,280,128]{2,1,0:T(8,128)(2,1)}), bf16[128,280,128]{2,1,0:T(8,128)(2,1)}, u32[]{:S(2)}, u32[]{:S(2)}) %all-to-all-start.2) | async-done | bytes 9175072 | tf_op jit(solution)/shard_map/all_to_all | solution.py:31
  536.0 16.9 %reshape.97 = bf16[1280,3584]{1,0:T(8,128)(2,1)} reshape(bf16[128,280,128]{2,1,0:T(8,128)(2,1)} %all-to-all-done.2) | data formatting | bytes 18350080 | tf_op jit(solution)/shard_map/reshape | solution.py:70
  552.8 18.6 %gather_fusion.2 = bf16[1024,3584]{1,0:T(8,128)(2,1)} fusion(bf16[1280,3584]{1,0:T(8,128)(2,1)} %reshape.97, s32[1024]{0:T(1024)S(1)} %broadcast_clamp_fusion), kind=kCustom, calls=%fused_computation.2 | custom fusion | bytes 14684160 | tf_op jit(solution)/shard_map/gather | solution.py:72
  571.4 8.7 %fusion.17 = bf16[128,3584]{1,0:T(8,128)(2,1)} fusion(pred[128,2,8]{2,1,0:T(4,128)(4,1)S(1)} %copy.31, bf16[1024,3584]{1,0:T(8,128)(2,1)} %gather_fusion.2), kind=kOutput, calls=%fused_computation.25 | convolution fusion | flops 16056320 | bytes 8259584 | tf_op jit(solution)/shard_map/tpk,tkd->tpd/dot_general | solution.py:76
  (9 shorter events, 0.1 us)
Async XLA Ops:
  0.6 25.1 %copy-start.1 = (bf16[128,3584]{1,0:T(8,128)(2,1)S(1)}, bf16[128,3584]{1,0:T(8,128)(2,1)}, u32[]{:S(2)}) copy-start(bf16[128,3584]{1,0:T(8,128)(2,1)} %param.7) | copy-start | bytes 2752516
  0.6 25.1 %copy-start = (bf16[128,3584]{1,0:T(8,128)(2,1)S(1)}, bf16[128,3584]{1,0:T(8,128)(2,1)}, u32[]{:S(2)}) copy-start(bf16[128,3584]{1,0:T(8,128)(2,1)} %param.8) | copy-start | bytes 2752516
  15.8 19.3 %all-to-all-start = ((bf16[128,1,10]{2,1,0:T(2,128)(2,1)}), bf16[128,1,10]{2,1,0:T(2,128)(2,1)S(1)}, u32[]{:S(2)}, u32[]{:S(2)}) async-start(bf16[128,1,10]{2,1,0:T(2,128)(2,1)} %all_to_all.21), calls=%async_computation | async-start | bytes 131072 | tf_op jit(solution)/shard_map/all_to_all | solution.py:31
  35.1 272.0 %all-to-all-start.1 = ((bf16[128,560,128]{2,1,0:T(8,128)(2,1)}), bf16[128,560,128]{2,1,0:T(8,128)(2,1)}, u32[]{:S(2)}, u32[]{:S(2)}) async-start(bf16[128,560,128]{2,1,0:T(8,128)(2,1)} %bitcast.28), calls=%async_computation.1 | async-start | bytes 36700160 | tf_op jit(solution)/shard_map/all_to_all | solution.py:31
  348.1 18.3 %copy-start.2 = (f32[1280,1024]{0,1:T(8,128)}, f32[1280,1024]{0,1:T(8,128)S(1)}, u32[]{:S(2)}) copy-start(f32[1280,1024]{0,1:T(8,128)S(1)} %fusion) | copy-start | bytes 15728644
  367.2 50.2 %all-to-all-start.3 = ((bf16[128,1,10]{2,1,0:T(2,128)(2,1)}), bf16[128,1,10]{2,1,0:T(2,128)(2,1)S(1)}, u32[]{:S(2)}, u32[]{:S(2)}) async-start(bf16[128,1,10]{2,1,0:T(2,128)(2,1)} %convert_element_type.44), calls=%async_computation.3 | async-start | bytes 131072 | tf_op jit(solution)/shard_map/all_to_all | solution.py:31
  417.4 118.6 %all-to-all-start.2 = ((bf16[128,280,128]{2,1,0:T(8,128)(2,1)}), bf16[128,280,128]{2,1,0:T(8,128)(2,1)}, u32[]{:S(2)}, u32[]{:S(2)}) async-start(bf16[128,280,128]{2,1,0:T(8,128)(2,1)} %reshape.96), calls=%async_computation.2 | async-start | bytes 18350080 | tf_op jit(solution)/shard_map/all_to_all | solution.py:31

commit v2 on v1

--- a/solution.py
+++ b/solution.py
@@ -5,6 +5,8 @@
 
 TOPK = 8
 LANES = 128
+CHUNKS = 2
+BACK_ROWS = 4
 
 
 def silu_slope(values):
@@ -31,7 +33,12 @@
     return lax.all_to_all(x, ("group", "dev"), split_axis=0, concat_axis=0, tiled=True)
 
 
-def shards(tokens, out_grad, gate_weights, expert_ids, slot_ids, up_weight, down_weight):
+def side_block(values, rows):
+    n = values.shape[1]
+    return jnp.pad(values[:, None, :], ((0, 0), (0, rows - 1), (0, LANES - n)))
+
+
+def layer(tokens, out_grad, gate_weights, expert_ids, slot_ids, up_weight, down_weight):
     rows_dev = tokens.shape[0]
     features = tokens.shape[1]
     groups = lax.axis_size("group")
@@ -45,6 +52,8 @@
     group_of = expert_ids // per_group
     both = 2 * features
     blocks = both // LANES
+    part = capacity // CHUNKS
+    part_rows = experts * part
     joined = jnp.concatenate(
         [jnp.concatenate([tokens, out_grad], axis=1), jnp.zeros((1, both), jnp.bfloat16)]
     ).reshape(rows_dev + 1, blocks, LANES)
@@ -54,23 +63,37 @@
         jnp.full((slots_all,), entries, jnp.int32)
         .at[target]
         .set(jnp.arange(entries, dtype=jnp.int32))
-    )
-    anchor = slot_table // TOPK
-    sent = joined[anchor].reshape(experts, capacity * blocks, LANES)
-    arrived = exchange(sent).reshape(slots_all, both)
-    gate_in = exchange(gate_flat[slot_table].reshape(experts, capacity))
-    contrib, gate_rows = expert_rows(
-        arrived[:, :features],
-        arrived[:, features:],
-        gate_in.reshape(slots_all),
-        up_matrix,
-        down_matrix,
-    )
-    half_blocks = capacity // 2 * both // LANES
-    returned = exchange(contrib.reshape(experts, half_blocks, LANES)).reshape(slots_all, features)
-    gate_back = exchange(gate_rows.reshape(experts, capacity))
-    gathered = returned[target].reshape(rows_dev, TOPK, features)
-    gate_grad = gate_back.reshape(-1)[target].reshape(rows_dev, TOPK)
+    ).reshape(experts, capacity)
+    gate_all = exchange(gate_flat[slot_table])
+    contribs = []
+    gate_backs = []
+    for c in range(CHUNKS):
+        table = slot_table[:, c * part:(c + 1) * part]
+        sent = joined[table // TOPK].reshape(experts, part * blocks, LANES)
+        arrived = exchange(sent)
+        data = arrived.reshape(part_rows, both)
+        gate_in = gate_all[:, c * part:(c + 1) * part].reshape(part_rows)
+        contrib, gate_rows = expert_rows(
+            data[:, :features], data[:, features:], gate_in, up_matrix, down_matrix
+        )
+        back_blocks = part * features // LANES
+        back = jnp.concatenate(
+            [
+                contrib.reshape(experts, back_blocks, LANES),
+                side_block(gate_rows.reshape(experts, part), BACK_ROWS),
+            ],
+            axis=1,
+        )
+        returned = exchange(back)
+        contribs.append(returned[:, :back_blocks, :].reshape(part_rows, features))
+        gate_backs.append(returned[:, back_blocks, :part])
+    all_contrib = jnp.concatenate(contribs, axis=0)
+    all_gate = jnp.concatenate(gate_backs, axis=1)
+    slot_flat = slot_ids.reshape(-1)
+    expert_flat = expert_ids.reshape(-1)
+    where = (slot_flat // part) * part_rows + expert_flat * part + slot_flat % part
+    gathered = all_contrib[where].reshape(rows_dev, TOPK, features)
+    gate_grad = all_gate.reshape(-1)[target].reshape(rows_dev, TOPK)
     same_group = group_of == group_of[:, :1]
     selector = jnp.stack([same_group, jnp.logical_not(same_group)], axis=1).astype(jnp.bfloat16)
     halves = jnp.einsum(
@@ -91,4 +114,4 @@
         P(("group", "dev"), None, None),
     )
     out_specs = (P(("group", "dev"), None), P(("group", "dev"), None))
-    return jax.shard_map(shards, mesh=mesh, in_specs=in_specs, out_specs=out_specs, check_vma=False)
+    return jax.shard_map(layer, mesh=mesh, in_specs=in_specs, out_specs=out_specs, check_vma=False)

time: 585 us -> 474 us (0.81)
  the two profiles are of different devices: /device:TPU:84 before, /device:TPU:1 now
where the time goes in v2:
time: 474 us; the launch traced here: 467 us
  waiting for transfers between devices  199 us (42%)
  local copies, waits for them, and re-layouts  122 us (26%)
  matrix products  72.2 us (15%)
  starting transfers between devices  53.9 us (11%)
  other arithmetic  18.7 us (4%)
    all_to_all x5, waiting for transfers between devices, exchange(): lax.all_to_all(x, ('group', 'dev'), split_axis=0, concat_axis=0, tiled=True)  199 us
    all_to_all x5, starting transfers between devices, exchange(): lax.all_to_all(x, ('group', 'dev'), split_axis=0, concat_axis=0, tiled=True)  53.9 us
    reshape x2, local copies, waits for them, and re-layouts, layer(): data = arrived.reshape(part_rows, both)  27.6 us
    dot_general x2, matrix products, expert_rows(): lax.dot_general(inner_grad, up_matrix, (((1,), (1,)), ((), ())), preferre...  25 us
    dot_general x2, matrix products, expert_rows(): lax.dot_general(grad_rows, down_matrix, (((1,), (1,)), ((), ())), preferr...  21.3 us
    reshape x2, local copies, waits for them, and re-layouts, layer(): contrib.reshape(experts, back_blocks, LANES)  19.2 us
    gather x1, local copies, waits for them, and re-layouts, layer(): gathered = all_contrib[where].reshape(rows_dev, TOPK, features)  18.6 us
    reshape x2, local copies, waits for them, and re-layouts, layer(): contribs.append(returned[:, :back_blocks, :].reshape(part_rows, features))  18.1 us
  transfers between devices with their start and end apart: 5, of which 4 were waited for; matrix products, arithmetic and copies ran while one was open for 31% of the time, Pallas kernels for 0%

profile of v2, /device:TPU:1, one launch (start us, length us, event | category | flops | bytes accessed | tf_op | source)
XLA Modules:
  0.0 466.9 jit_solution(18010660078925677924)
XLA Ops:
  0.6 0.8 copy.57
  1.4 0.1 reshape.241
  1.5 0.7 broadcast_divide_fusion
  2.3 0.1 copy.58
  2.4 0.1 reshape.242
  2.5 4.3 scatter_custom_fusion
  6.8 0.1 reshape.243
  7.0 0.1 reshape.261
  7.1 8.0 %gather_fusion = bf16[1280]{0:T(1024)(128)(2,1)S(1)} fusion(bf16[1025]{0:T(1024)(128)(2,1)S(1)} %pad_maximum_fusion.1, s32[2048]{0:T(1024)S(1)} %pad_clamp_fusion), kind=kCustom, calls=%fused_computation | custom fusion | bytes 10240 | tf_op jit(solution)/shard_map/gather | solution.py:67
  15.1 0.8 all_to_all.27
  15.9 11.5 %all-to-all-start = ((bf16[128,1,10]{2,1,0:T(2,128)(2,1)}), bf16[128,1,10]{2,1,0:T(2,128)(2,1)S(1)}, u32[]{:S(2)}, u32[]{:S(2)}) async-start(bf16[128,1,10]{2,1,0:T(2,128)(2,1)} %all_to_all.27), calls=%async_computation | async-start | bytes 131072 | tf_op jit(solution)/shard_map/all_to_all | solution.py:33
  27.4 0.1 reshape.245
  27.5 0.1 compare_select_fusion.1
  27.7 0.2 reshape.277
  27.9 0.2 fusion.33
  28.1 0.4 copy.74
  28.5 0.3 slice.74
  28.9 5.2 %gather_fusion.2 = bf16[640,56,128]{2,1,0:T(8,128)(2,1)} fusion(bf16[129,56,128]{2,1,0:T(8,128)(2,1)S(1)} %slice.74, s32[1024]{0:T(1024)S(1)} %pad_clamp_fusion.1), kind=kCustom, calls=%fused_computation.2 | custom fusion | bytes 18352640 | tf_op jit(solution)/shard_map/gather | solution.py:72
  34.1 2.9 all-to-all-done
  37.0 7.3 %all-to-all-start.3 = ((bf16[128,280,128]{2,1,0:T(8,128)(2,1)}), bf16[128,280,128]{2,1,0:T(8,128)(2,1)}, u32[]{:S(2)}, u32[]{:S(2)}) async-start(bf16[128,280,128]{2,1,0:T(8,128)(2,1)} %bitcast.51), calls=%async_computation.3 | async-start | bytes 18350080 | tf_op jit(solution)/shard_map/all_to_all | solution.py:33
  44.3 0.2 reshape.269
  44.5 5.2 %gather_fusion.1 = bf16[640,56,128]{2,1,0:T(8,128)(2,1)} fusion(bf16[129,56,128]{2,1,0:T(8,128)(2,1)S(1)} %slice.74, s32[1024]{0:T(1024)S(1)} %pad_clamp_fusion.2), kind=kCustom, calls=%fused_computation.1 | custom fusion | bytes 18352640 | tf_op jit(solution)/shard_map/gather | solution.py:72
  49.7 102.6 %all-to-all-done.3 = bf16[128,280,128]{2,1,0:T(8,128)(2,1)} async-done(((bf16[128,280,128]{2,1,0:T(8,128)(2,1)}), bf16[128,280,128]{2,1,0:T(8,128)(2,1)}, u32[]{:S(2)}, u32[]{:S(2)}) %all-to-all-start.3) | async-done | bytes 9175072 | tf_op jit(solution)/shard_map/all_to_all | solution.py:33
  152.3 12.6 %all-to-all-start.1 = ((bf16[128,280,128]{2,1,0:T(8,128)(2,1)}), bf16[128,280,128]{2,1,0:T(8,128)(2,1)}, u32[]{:S(2)}, u32[]{:S(2)}) async-start(bf16[128,280,128]{2,1,0:T(8,128)(2,1)} %bitcast.50), calls=%async_computation.1 | async-start | bytes 18350080 | tf_op jit(solution)/shard_map/all_to_all | solution.py:33
  165.0 0.1 copy.61
  165.1 0.2 reshape.257
  165.3 0.1 copy.63
  165.5 0.2 reshape.258
  165.7 13.8 %reshape.251 = bf16[640,7168]{1,0:T(8,128)(2,1)} reshape(bf16[128,280,128]{2,1,0:T(8,128)(2,1)} %all-to-all-done.3) | data formatting | bytes 18350080 | tf_op jit(solution)/shard_map/reshape | solution.py:74
  179.4 8.6 %fusion.6 = f32[640,1024]{1,0:T(8,128)S(1)} fusion(bf16[1,3584,1024]{2,1,0:T(8,128)(2,1)} %param.12, bf16[640,7168]{1,0:T(8,128)(2,1)} %reshape.251), kind=kOutput, calls=%fused_computation.14 | convolution fusion | flops 4697620480 | bytes 14548992 | tf_op jit(solution)/shard_map/dot_general | solution.py:18
  188.1 10.6 %multiply_reduce_fusion = (bf16[640]{0:T(1024)(128)(2,1)S(1)}, f32[640,1024]{1,0:T(8,128)}) fusion(f32[640,1024]{1,0:T(8,128)S(1)} %fusion.6, bf16[1,1024,3584]{2,1,0:T(8,128)(2,1)} %param.13, bf16[640,7168]{1,0:T(8,128)(2,1)S(1)} %copy-done), kind=kOutput, calls=%fused_computation.36 | convolution fusion | flops 4701552128 | bytes 17171712 | tf_op jit(solution)/shard_map/dot_general | solution.py:19
  198.7 0.2 convert_element_type.83
  199.0 12.5 %fusion.19 = bf16[640,3584]{1,0:T(8,128)(2,1)} fusion(bf16[1,3584,1024]{2,1,0:T(8,128)(2,1)} %param.12, f32[640,1024]{1,0:T(8,128)} %copy-done.5, f32[640,1024]{1,0:T(8,128)} %get-tuple-element.20, f32[640]{0:T(1024)S(1)} %reshape.258), kind=kOutput, calls=%fused_computation.25 | convolution fusion | flops 4706467840 | bytes 17172992 | tf_op jit(solution)/shard_map/dot_general | solution.py:26
  211.5 9.6 %reshape.252 = bf16[128,140,128]{2,1,0:T(8,128)(2,1)} reshape(bf16[640,3584]{1,0:T(8,128)(2,1)} %fusion.19) | data formatting | bytes 9175040 | tf_op jit(solution)/shard_map/reshape | solution.py:82
  221.0 5.0 %fusion.26 = bf16[128,144,128]{2,1,0:T(8,128)(2,1)} fusion(bf16[128,1,5]{2,1,0:T(2,128)(2,1)S(1)} %convert_element_type.83, bf16[128,140,128]{2,1,0:T(8,128)(2,1)} %reshape.252), kind=kLoop, calls=%fused_computation.28 | loop fusion | flops 14155776 | bytes 9307392 | tf_op jit(solution)/shard_map/concatenate | solution.py:80
  226.1 46.7 %all-to-all-done.1 = bf16[128,280,128]{2,1,0:T(8,128)(2,1)} async-done(((bf16[128,280,128]{2,1,0:T(8,128)(2,1)}), bf16[128,280,128]{2,1,0:T(8,128)(2,1)}, u32[]{:S(2)}, u32[]{:S(2)}) %all-to-all-start.1) | async-done | bytes 9175072 | tf_op jit(solution)/shard_map/all_to_all | solution.py:33
  272.7 12.0 %all-to-all-start.4 = ((bf16[128,144,128]{2,1,0:T(8,128)(2,1)}), bf16[128,144,128]{2,1,0:T(8,128)(2,1)}, u32[]{:S(2)}, u32[]{:S(2)}) async-start(bf16[128,144,128]{2,1,0:T(8,128)(2,1)} %fusion.26), calls=%async_computation.4 | async-start | bytes 9437184 | tf_op jit(solution)/shard_map/all_to_all | solution.py:33
  284.7 13.8 %reshape.247 = bf16[640,7168]{1,0:T(8,128)(2,1)} reshape(bf16[128,280,128]{2,1,0:T(8,128)(2,1)} %all-to-all-done.1) | data formatting | bytes 18350080 | tf_op jit(solution)/shard_map/reshape | solution.py:74
  298.6 8.6 %fusion.10 = f32[640,1024]{1,0:T(8,128)S(1)} fusion(bf16[1,3584,1024]{2,1,0:T(8,128)(2,1)} %param.12, bf16[640,7168]{1,0:T(8,128)(2,1)} %reshape.247), kind=kOutput, calls=%fused_computation.18 | convolution fusion | flops 4697620480 | bytes 14548992 | tf_op jit(solution)/shard_map/dot_general | solution.py:18
  307.2 10.7 %multiply_reduce_fusion.1 = (bf16[640]{0:T(1024)(128)(2,1)S(1)}, f32[640,1024]{1,0:T(8,128)}) fusion(f32[640,1024]{1,0:T(8,128)S(1)} %fusion.10, bf16[1,1024,3584]{2,1,0:T(8,128)(2,1)} %param.13, bf16[640,7168]{1,0:T(8,128)(2,1)S(1)} %copy-done.1), kind=kOutput, calls=%fused_computation.39 | convolution fusion | flops 4701552128 | bytes 17171712 | tf_op jit(solution)/shard_map/dot_general | solution.py:19
  317.9 0.2 convert_element_type.82
  318.1 12.4 %fusion.16 = bf16[640,3584]{1,0:T(8,128)(2,1)} fusion(bf16[1,3584,1024]{2,1,0:T(8,128)(2,1)} %param.12, f32[640,1024]{1,0:T(8,128)} %copy-done.6, f32[640,1024]{1,0:T(8,128)} %get-tuple-element.22, f32[640]{0:T(1024)S(1)} %reshape.257), kind=kOutput, calls=%fused_computation.24 | convolution fusion | flops 4706467840 | bytes 17172992 | tf_op jit(solution)/shard_map/dot_general | solution.py:26
  330.6 9.6 %reshape.248 = bf16[128,140,128]{2,1,0:T(8,128)(2,1)} reshape(bf16[640,3584]{1,0:T(8,128)(2,1)} %fusion.16) | data formatting | bytes 9175040 | tf_op jit(solution)/shard_map/reshape | solution.py:82
  340.2 4.9 %fusion.25 = bf16[128,144,128]{2,1,0:T(8,128)(2,1)} fusion(bf16[128,1,5]{2,1,0:T(2,128)(2,1)S(1)} %convert_element_type.82, bf16[128,140,128]{2,1,0:T(8,128)(2,1)} %reshape.248), kind=kLoop, calls=%fused_computation.27 | loop fusion | flops 14155776 | bytes 9307392 | tf_op jit(solution)/shard_map/concatenate | solution.py:80
  345.1 10.6 %all-to-all-start.2 = ((bf16[128,144,128]{2,1,0:T(8,128)(2,1)}), bf16[128,144,128]{2,1,0:T(8,128)(2,1)}, u32[]{:S(2)}, u32[]{:S(2)}) async-start(bf16[128,144,128]{2,1,0:T(8,128)(2,1)} %fusion.25), calls=%async_computation.2 | async-start | bytes 9437184 | tf_op jit(solution)/shard_map/all_to_all | solution.py:33
  355.7 0.1 copy.65
  355.8 0.1 ne.88
  356.0 0.1 copy.67
  356.1 0.1 div.71
  356.2 0.2 copy.69
  356.4 0.1 copy.68
  356.6 0.1 copy.66
  356.8 1.0 slice.73
  357.9 9.1 %reshape.253 = bf16[640,3584]{1,0:T(8,128)(2,1)} reshape(bf16[128,140,128]{2,1,0:T(8,128)(2,1)} %bitcast.47) | data formatting | bytes 9175040 | tf_op jit(solution)/shard_map/reshape | solution.py:88
  367.0 46.8 %all-to-all-done.2 = bf16[128,144,128]{2,1,0:T(8,128)(2,1)} async-done(((bf16[128,144,128]{2,1,0:T(8,128)(2,1)}), bf16[128,144,128]{2,1,0:T(8,128)(2,1)}, u32[]{:S(2)}, u32[]{:S(2)}) %all-to-all-start.2) | async-done | bytes 4718624 | tf_op jit(solution)/shard_map/all_to_all | solution.py:33
  413.8 1.0 slice.72
  414.9 0.1 copy.72
  415.1 0.2 reshape.255
  415.2 6.8 %gather_fusion.4 = bf16[1024]{0:T(1024)(128)(2,1)S(1)} fusion(bf16[1280]{0:T(1024)(128)(2,1)S(1)} %reshape.255, s32[1024]{0:T(1024)S(1)} %broadcast_clamp_fusion), kind=kCustom, calls=%fused_computation.4 | custom fusion | bytes 8192 | tf_op jit(solution)/shard_map/gather | solution.py:96
  422.1 0.7 copy.73
  422.8 9.1 %reshape.249 = bf16[640,3584]{1,0:T(8,128)(2,1)} reshape(bf16[128,140,128]{2,1,0:T(8,128)(2,1)} %bitcast.48) | data formatting | bytes 9175040 | tf_op jit(solution)/shard_map/reshape | solution.py:88
  431.9 7.6 %pad_maximum_fusion = bf16[1280,3584]{1,0:T(8,128)(2,1)} fusion(bf16[640,3584]{1,0:T(8,128)(2,1)} %reshape.253, bf16[640,3584]{1,0:T(8,128)(2,1)} %reshape.249), kind=kLoop, calls=%fused_computation.9 | loop fusion | flops 18350080 | bytes 18350080 | tf_op jit(solution)/shard_map/concatenate | solution.py:90
  439.4 18.6 %gather_fusion.3 = bf16[1024,3584]{1,0:T(8,128)(2,1)} fusion(bf16[1280,3584]{1,0:T(8,128)(2,1)} %pad_maximum_fusion, s32[1024]{0:T(1024)S(1)} %broadcast_clamp_fusion.1), kind=kCustom, calls=%fused_computation.3 | custom fusion | bytes 14684160 | tf_op jit(solution)/shard_map/gather | solution.py:95
  458.0 8.7 %fusion.38 = bf16[128,3584]{1,0:T(8,128)(2,1)} fusion(pred[128,2,8]{2,1,0:T(4,128)(4,1)S(1)} %copy.69, bf16[1024,3584]{1,0:T(8,128)(2,1)} %gather_fusion.3), kind=kOutput, calls=%fused_computation.47 | convolution fusion | flops 16056320 | bytes 8259584 | tf_op jit(solution)/shard_map/tpk,tkd->tpd/dot_general | solution.py:99
  (37 shorter events, 0.7 us)
Async XLA Ops:
  7.1 20.8 %copy-start.2 = (bf16[128,3584]{1,0:T(8,128)(2,1)S(1)}, bf16[128,3584]{1,0:T(8,128)(2,1)}, u32[]{:S(2)}) copy-start(bf16[128,3584]{1,0:T(8,128)(2,1)} %param.8) | copy-start | bytes 2752516
  7.1 20.8 %copy-start.3 = (bf16[128,3584]{1,0:T(8,128)(2,1)S(1)}, bf16[128,3584]{1,0:T(8,128)(2,1)}, u32[]{:S(2)}) copy-start(bf16[128,3584]{1,0:T(8,128)(2,1)} %param.7) | copy-start | bytes 2752516
  15.9 21.1 %all-to-all-start = ((bf16[128,1,10]{2,1,0:T(2,128)(2,1)}), bf16[128,1,10]{2,1,0:T(2,128)(2,1)S(1)}, u32[]{:S(2)}, u32[]{:S(2)}) async-start(bf16[128,1,10]{2,1,0:T(2,128)(2,1)} %all_to_all.27), calls=%async_computation | async-start | bytes 131072 | tf_op jit(solution)/shard_map/all_to_all | solution.py:33
  37.0 115.4 %all-to-all-start.3 = ((bf16[128,280,128]{2,1,0:T(8,128)(2,1)}), bf16[128,280,128]{2,1,0:T(8,128)(2,1)}, u32[]{:S(2)}, u32[]{:S(2)}) async-start(bf16[128,280,128]{2,1,0:T(8,128)(2,1)} %bitcast.51), calls=%async_computation.3 | async-start | bytes 18350080 | tf_op jit(solution)/shard_map/all_to_all | solution.py:33
  152.3 120.4 %all-to-all-start.1 = ((bf16[128,280,128]{2,1,0:T(8,128)(2,1)}), bf16[128,280,128]{2,1,0:T(8,128)(2,1)}, u32[]{:S(2)}, u32[]{:S(2)}) async-start(bf16[128,280,128]{2,1,0:T(8,128)(2,1)} %bitcast.50), calls=%async_computation.1 | async-start | bytes 18350080 | tf_op jit(solution)/shard_map/all_to_all | solution.py:33
  179.4 8.6 %copy-start = (bf16[640,7168]{1,0:T(8,128)(2,1)S(1)}, bf16[640,7168]{1,0:T(8,128)(2,1)}, u32[]{:S(2)}) copy-start(bf16[640,7168]{1,0:T(8,128)(2,1)} %reshape.251) | copy-start | bytes 27525124
  188.1 10.6 %copy-start.5 = (f32[640,1024]{1,0:T(8,128)}, f32[640,1024]{1,0:T(8,128)S(1)}, u32[]{:S(2)}) copy-start(f32[640,1024]{1,0:T(8,128)S(1)} %fusion.6) | copy-start | bytes 7864324
  272.7 72.4 %all-to-all-start.4 = ((bf16[128,144,128]{2,1,0:T(8,128)(2,1)}), bf16[128,144,128]{2,1,0:T(8,128)(2,1)}, u32[]{:S(2)}, u32[]{:S(2)}) async-start(bf16[128,144,128]{2,1,0:T(8,128)(2,1)} %fusion.26), calls=%async_computation.4 | async-start | bytes 9437184 | tf_op jit(solution)/shard_map/all_to_all | solution.py:33
  298.6 8.6 %copy-start.1 = (bf16[640,7168]{1,0:T(8,128)(2,1)S(1)}, bf16[640,7168]{1,0:T(8,128)(2,1)}, u32[]{:S(2)}) copy-start(bf16[640,7168]{1,0:T(8,128)(2,1)} %reshape.247) | copy-start | bytes 27525124
  307.2 10.7 %copy-start.6 = (f32[640,1024]{1,0:T(8,128)}, f32[640,1024]{1,0:T(8,128)S(1)}, u32[]{:S(2)}) copy-start(f32[640,1024]{1,0:T(8,128)S(1)} %fusion.10) | copy-start | bytes 7864324
  345.1 10.6 %copy-start.4 = (s32[128,8]{0,1:T(8,128)S(1)}, s32[128,8]{0,1:T(8,128)}, u32[]{:S(2)}) copy-start(s32[128,8]{0,1:T(8,128)} %param.11) | copy-start | bytes 12292
  345.1 68.7 %all-to-all-start.2 = ((bf16[128,144,128]{2,1,0:T(8,128)(2,1)}), bf16[128,144,128]{2,1,0:T(8,128)(2,1)}, u32[]{:S(2)}, u32[]{:S(2)}) async-start(bf16[128,144,128]{2,1,0:T(8,128)(2,1)} %fusion.25), calls=%async_computation.2 | async-start | bytes 9437184 | tf_op jit(solution)/shard_map/all_to_all | solution.py:33

commit v3 on v2

--- a/solution.py
+++ b/solution.py
@@ -14,15 +14,13 @@
     return sigmoid_up * (1.0 + values * (1.0 - sigmoid_up))
 
 
-def expert_rows(token_rows, grad_rows, gate_rows, up_matrix, down_matrix):
+def expert_rows(token_rows, grad_rows, up_matrix, down_matrix):
     raised = jnp.dot(token_rows, up_matrix, preferred_element_type=jnp.float32)
     backward = lax.dot_general(
         grad_rows, down_matrix, (((1,), (1,)), ((), ())), preferred_element_type=jnp.float32
     )
     gate_grad = jnp.sum(jax.nn.silu(raised) * backward, axis=1).astype(jnp.bfloat16)
-    inner_grad = (gate_rows.astype(jnp.float32)[:, None] * backward * silu_slope(raised)).astype(
-        jnp.bfloat16
-    )
+    inner_grad = (backward * silu_slope(raised)).astype(jnp.bfloat16)
     contrib = lax.dot_general(
         inner_grad, up_matrix, (((1,), (1,)), ((), ())), preferred_element_type=jnp.float32
     ).astype(jnp.bfloat16)
@@ -57,24 +55,26 @@
     joined = jnp.concatenate(
         [jnp.concatenate([tokens, out_grad], axis=1), jnp.zeros((1, both), jnp.bfloat16)]
     ).reshape(rows_dev + 1, blocks, LANES)
-    gate_flat = jnp.concatenate([gate_weights.reshape(-1), jnp.zeros((1,), jnp.bfloat16)])
     target = (expert_ids * capacity + slot_ids).reshape(-1)
     slot_table = (
         jnp.full((slots_all,), entries, jnp.int32)
         .at[target]
         .set(jnp.arange(entries, dtype=jnp.int32))
     ).reshape(experts, capacity)
-    gate_all = exchange(gate_flat[slot_table])
-    contribs = []
+    slot_flat = slot_ids.reshape(-1)
+    expert_flat = expert_ids.reshape(-1)
+    same_group = group_of == group_of[:, :1]
+    selector = jnp.stack([same_group, jnp.logical_not(same_group)], axis=1)
+    gate_rowwise = gate_weights.reshape(rows_dev, 1, TOPK)
+    summed = None
     gate_backs = []
     for c in range(CHUNKS):
         table = slot_table[:, c * part:(c + 1) * part]
         sent = joined[table // TOPK].reshape(experts, part * blocks, LANES)
         arrived = exchange(sent)
         data = arrived.reshape(part_rows, both)
-        gate_in = gate_all[:, c * part:(c + 1) * part].reshape(part_rows)
         contrib, gate_rows = expert_rows(
-            data[:, :features], data[:, features:], gate_in, up_matrix, down_matrix
+            data[:, :features], data[:, features:], up_matrix, down_matrix
         )
         back_blocks = part * features // LANES
         back = jnp.concatenate(
@@ -85,20 +85,19 @@
             axis=1,
         )
         returned = exchange(back)
-        contribs.append(returned[:, :back_blocks, :].reshape(part_rows, features))
+        rows_back = returned[:, :back_blocks, :].reshape(part_rows, features)
         gate_backs.append(returned[:, back_blocks, :part])
-    all_contrib = jnp.concatenate(contribs, axis=0)
+        in_chunk = (slot_flat // part == c).reshape(rows_dev, 1, TOPK)
+        where = jnp.clip(expert_flat * part + slot_flat - c * part, 0, part_rows - 1)
+        gathered = rows_back[where].reshape(rows_dev, TOPK, features)
+        pick = jnp.where(jnp.logical_and(selector, in_chunk), gate_rowwise, jnp.bfloat16(0))
+        partial = jnp.einsum(
+            "tpk,tkd->tpd", pick, gathered, preferred_element_type=jnp.float32
+        )
+        summed = partial if summed is None else summed + partial
     all_gate = jnp.concatenate(gate_backs, axis=1)
-    slot_flat = slot_ids.reshape(-1)
-    expert_flat = expert_ids.reshape(-1)
-    where = (slot_flat // part) * part_rows + expert_flat * part + slot_flat % part
-    gathered = all_contrib[where].reshape(rows_dev, TOPK, features)
     gate_grad = all_gate.reshape(-1)[target].reshape(rows_dev, TOPK)
-    same_group = group_of == group_of[:, :1]
-    selector = jnp.stack([same_group, jnp.logical_not(same_group)], axis=1).astype(jnp.bfloat16)
-    halves = jnp.einsum(
-        "tpk,tkd->tpd", selector, gathered, preferred_element_type=jnp.float32
-    ).astype(jnp.bfloat16)
+    halves = summed.astype(jnp.bfloat16)
     token_grad = jnp.sum(halves.astype(jnp.float32), axis=1).astype(jnp.bfloat16)
     return (token_grad, gate_grad)
 

time: 474 us -> 471 us (level)
  matrix products: 72.2 us -> 80 us
  starting transfers between devices: 53.9 us -> 47 us
  other arithmetic: 18.7 us -> 12.5 us
    dot_general x1 -> x2, matrix products: 8.68 us -> 17.1 us  [layer(): jnp.einsum('tpk,tkd->tpd', pick, gathered, preferred_element_type=jnp.flo...]
    concatenate x2 -> x0, other arithmetic: 7.57 us -> none  [the longest x1 7.56 us: layer(): all_contrib = jnp.concatenate(contribs, axis=0)]
    gather x2, local copies, waits for them, and re-layouts: 26.6 us -> 33.6 us  [layer(): gathered = rows_back[where].reshape(rows_dev, TOPK, features)]
    all_to_all x5 -> x4, starting transfers between devices: 53.9 us -> 47 us  [exchange(): lax.all_to_all(x, ('group', 'dev'), split_axis=0, concat_axis=0, tiled=True)]
    all_to_all x5 -> x4, waiting for transfers between devices: 199 us -> 197 us  [exchange(): lax.all_to_all(x, ('group', 'dev'), split_axis=0, concat_axis=0, tiled=True)]
    reshape x3 -> x2, local copies, waits for them, and re-layouts: 18.2 us -> 18.2 us  [layer(): rows_back = returned[:, :back_blocks, :].reshape(part_rows, features)]
  transfers between devices with their start and end apart: 5 -> 4, of which waited for: 4 -> 3; matrix products, arithmetic and copies ran while one was open for 31% -> 29% of each run, Pallas kernels for 0% -> 0%
where the time goes in v3:
time: 471 us; the launch traced here: 464 us
  waiting for transfers between devices  197 us (42%)
  local copies, waits for them, and re-layouts  126 us (27%)
  matrix products  80 us (17%)
  starting transfers between devices  47 us (10%)
  other arithmetic  12.5 us (3%)
    all_to_all x4, waiting for transfers between devices, exchange(): lax.all_to_all(x, ('group', 'dev'), split_axis=0, concat_axis=0, tiled=True)  197 us
    all_to_all x4, starting transfers between devices, exchange(): lax.all_to_all(x, ('group', 'dev'), split_axis=0, concat_axis=0, tiled=True)  47 us
    gather x2, local copies, waits for them, and re-layouts, layer(): gathered = rows_back[where].reshape(rows_dev, TOPK, features)  33.6 us
    reshape x2, local copies, waits for them, and re-layouts, layer(): data = arrived.reshape(part_rows, both)  27.6 us
    dot_general x2, matrix products, expert_rows(): lax.dot_general(inner_grad, up_matrix, (((1,), (1,)), ((), ())), preferre...  24.4 us
    dot_general x2, matrix products, expert_rows(): lax.dot_general(grad_rows, down_matrix, (((1,), (1,)), ((), ())), preferr...  21.3 us
    reshape x2, local copies, waits for them, and re-layouts, layer(): contrib.reshape(experts, back_blocks, LANES)  19.2 us
    reshape x2, local copies, waits for them, and re-layouts, layer(): rows_back = returned[:, :back_blocks, :].reshape(part_rows, features)  18.2 us
  transfers between devices with their start and end apart: 4, of which 3 were waited for; matrix products, arithmetic and copies ran while one was open for 29% of the time, Pallas kernels for 0%

profile of v3, /device:TPU:1, one launch (start us, length us, event | category | flops | bytes accessed | tf_op | source)
XLA Modules:
  0.0 464.1 jit_solution(3712533320986897971)
XLA Ops:
  0.6 0.7 broadcast_clamp_fusion.3
  1.3 0.1 copy.23
  1.4 0.1 reshape.186
  1.6 4.3 scatter_custom_fusion
  5.9 0.1 reshape.187
  6.0 0.1 compare_select_fusion.1
  6.2 0.2 reshape.218
  6.4 1.6 fusion.38
  8.0 0.4 copy.34
  8.4 0.3 slice.64
  8.8 5.2 %gather_fusion.2 = bf16[640,56,128]{2,1,0:T(8,128)(2,1)} fusion(bf16[129,56,128]{2,1,0:T(8,128)(2,1)S(1)} %slice.64, s32[1024]{0:T(1024)S(1)} %pad_clamp_fusion), kind=kCustom, calls=%fused_computation.2 | custom fusion | bytes 18352640 | tf_op jit(solution)/shard_map/gather | solution.py:73
  14.0 11.9 %all-to-all-start.2 = ((bf16[128,280,128]{2,1,0:T(8,128)(2,1)}), bf16[128,280,128]{2,1,0:T(8,128)(2,1)}, u32[]{:S(2)}, u32[]{:S(2)}) async-start(bf16[128,280,128]{2,1,0:T(8,128)(2,1)} %bitcast.55), calls=%async_computation.2 | async-start | bytes 18350080 | tf_op jit(solution)/shard_map/all_to_all | solution.py:31
  25.9 0.2 reshape.202
  26.1 5.2 %gather_fusion = bf16[640,56,128]{2,1,0:T(8,128)(2,1)} fusion(bf16[129,56,128]{2,1,0:T(8,128)(2,1)S(1)} %slice.64, s32[1024]{0:T(1024)S(1)} %pad_clamp_fusion.1), kind=kCustom, calls=%fused_computation | custom fusion | bytes 18352640 | tf_op jit(solution)/shard_map/gather | solution.py:73
  31.3 102.6 %all-to-all-done.2 = bf16[128,280,128]{2,1,0:T(8,128)(2,1)} async-done(((bf16[128,280,128]{2,1,0:T(8,128)(2,1)}), bf16[128,280,128]{2,1,0:T(8,128)(2,1)}, u32[]{:S(2)}, u32[]{:S(2)}) %all-to-all-start.2) | async-done | bytes 9175072 | tf_op jit(solution)/shard_map/all_to_all | solution.py:31
  134.0 12.6 %all-to-all-start = ((bf16[128,280,128]{2,1,0:T(8,128)(2,1)}), bf16[128,280,128]{2,1,0:T(8,128)(2,1)}, u32[]{:S(2)}, u32[]{:S(2)}) async-start(bf16[128,280,128]{2,1,0:T(8,128)(2,1)} %bitcast.54), calls=%async_computation | async-start | bytes 18350080 | tf_op jit(solution)/shard_map/all_to_all | solution.py:31
  146.6 13.8 %reshape.194 = bf16[640,7168]{1,0:T(8,128)(2,1)} reshape(bf16[128,280,128]{2,1,0:T(8,128)(2,1)} %all-to-all-done.2) | data formatting | bytes 18350080 | tf_op jit(solution)/shard_map/reshape | solution.py:75
  160.4 8.6 %fusion.8 = f32[640,1024]{1,0:T(8,128)S(1)} fusion(bf16[1,3584,1024]{2,1,0:T(8,128)(2,1)} %param.12, bf16[640,7168]{1,0:T(8,128)(2,1)} %reshape.194), kind=kOutput, calls=%fused_computation.15 | convolution fusion | flops 4697620480 | bytes 14548992 | tf_op jit(solution)/shard_map/dot_general | solution.py:18
  169.0 0.0 copy-done
  169.0 0.0 copy-start.4
  169.1 10.6 %multiply_reduce_fusion = (bf16[640]{0:T(1024)(128)(2,1)S(1)}, f32[640,1024]{1,0:T(8,128)}) fusion(f32[640,1024]{1,0:T(8,128)S(1)} %fusion.8, bf16[1,1024,3584]{2,1,0:T(8,128)(2,1)} %param.13, bf16[640,7168]{1,0:T(8,128)(2,1)S(1)} %copy-done), kind=kOutput, calls=%fused_computation.38 | convolution fusion | flops 4701552128 | bytes 17171712 | tf_op jit(solution)/shard_map/dot_general | solution.py:19
  179.7 0.0 copy-done.4
  179.7 0.2 convert_element_type.56
  179.9 12.2 %fusion.21 = bf16[640,3584]{1,0:T(8,128)(2,1)} fusion(bf16[1,3584,1024]{2,1,0:T(8,128)(2,1)} %param.12, f32[640,1024]{1,0:T(8,128)} %get-tuple-element.19, f32[640,1024]{1,0:T(8,128)} %copy-done.4), kind=kOutput, calls=%fused_computation.26 | convolution fusion | flops 4705812480 | bytes 17170432 | tf_op jit(solution)/shard_map/dot_general | solution.py:24
  192.1 9.6 %reshape.195 = bf16[128,140,128]{2,1,0:T(8,128)(2,1)} reshape(bf16[640,3584]{1,0:T(8,128)(2,1)} %fusion.21) | data formatting | bytes 9175040 | tf_op jit(solution)/shard_map/reshape | solution.py:82
  201.7 5.0 %fusion.31 = bf16[128,144,128]{2,1,0:T(8,128)(2,1)} fusion(bf16[128,1,5]{2,1,0:T(2,128)(2,1)S(1)} %convert_element_type.56, bf16[128,140,128]{2,1,0:T(8,128)(2,1)} %reshape.195), kind=kLoop, calls=%fused_computation.30 | loop fusion | flops 14155776 | bytes 9307392 | tf_op jit(solution)/shard_map/concatenate | solution.py:80
  206.7 47.7 %all-to-all-done = bf16[128,280,128]{2,1,0:T(8,128)(2,1)} async-done(((bf16[128,280,128]{2,1,0:T(8,128)(2,1)}), bf16[128,280,128]{2,1,0:T(8,128)(2,1)}, u32[]{:S(2)}, u32[]{:S(2)}) %all-to-all-start) | async-done | bytes 9175072 | tf_op jit(solution)/shard_map/all_to_all | solution.py:31
  254.4 12.0 %all-to-all-start.3 = ((bf16[128,144,128]{2,1,0:T(8,128)(2,1)}), bf16[128,144,128]{2,1,0:T(8,128)(2,1)}, u32[]{:S(2)}, u32[]{:S(2)}) async-start(bf16[128,144,128]{2,1,0:T(8,128)(2,1)} %fusion.31), calls=%async_computation.3 | async-start | bytes 9437184 | tf_op jit(solution)/shard_map/all_to_all | solution.py:31
  266.4 13.8 %reshape.189 = bf16[640,7168]{1,0:T(8,128)(2,1)} reshape(bf16[128,280,128]{2,1,0:T(8,128)(2,1)} %all-to-all-done) | data formatting | bytes 18350080 | tf_op jit(solution)/shard_map/reshape | solution.py:75
  280.2 8.6 %fusion.12 = f32[640,1024]{1,0:T(8,128)S(1)} fusion(bf16[1,3584,1024]{2,1,0:T(8,128)(2,1)} %param.12, bf16[640,7168]{1,0:T(8,128)(2,1)} %reshape.189), kind=kOutput, calls=%fused_computation.19 | convolution fusion | flops 4697620480 | bytes 14548992 | tf_op jit(solution)/shard_map/dot_general | solution.py:18
  288.9 0.0 copy-done.1
  288.9 0.0 copy-start.5
  288.9 10.7 %multiply_reduce_fusion.1 = (bf16[640]{0:T(1024)(128)(2,1)S(1)}, f32[640,1024]{1,0:T(8,128)}) fusion(f32[640,1024]{1,0:T(8,128)S(1)} %fusion.12, bf16[1,1024,3584]{2,1,0:T(8,128)(2,1)} %param.13, bf16[640,7168]{1,0:T(8,128)(2,1)S(1)} %copy-done.1), kind=kOutput, calls=%fused_computation.41 | convolution fusion | flops 4701552128 | bytes 17171712 | tf_op jit(solution)/shard_map/dot_general | solution.py:19
  299.6 0.0 copy-done.5
  299.6 0.2 convert_element_type.55
  299.8 12.2 %fusion.18 = bf16[640,3584]{1,0:T(8,128)(2,1)} fusion(bf16[1,3584,1024]{2,1,0:T(8,128)(2,1)} %param.12, f32[640,1024]{1,0:T(8,128)} %get-tuple-element.21, f32[640,1024]{1,0:T(8,128)} %copy-done.5), kind=kOutput, calls=%fused_computation.25 | convolution fusion | flops 4705812480 | bytes 17170432 | tf_op jit(solution)/shard_map/dot_general | solution.py:24
  312.0 9.6 %reshape.190 = bf16[128,140,128]{2,1,0:T(8,128)(2,1)} reshape(bf16[640,3584]{1,0:T(8,128)(2,1)} %fusion.18) | data formatting | bytes 9175040 | tf_op jit(solution)/shard_map/reshape | solution.py:82
  321.6 4.9 %fusion.30 = bf16[128,144,128]{2,1,0:T(8,128)(2,1)} fusion(bf16[128,1,5]{2,1,0:T(2,128)(2,1)S(1)} %convert_element_type.55, bf16[128,140,128]{2,1,0:T(8,128)(2,1)} %reshape.190), kind=kLoop, calls=%fused_computation.29 | loop fusion | flops 14155776 | bytes 9307392 | tf_op jit(solution)/shard_map/concatenate | solution.py:80
  326.5 0.0 all-to-all-done.3
  326.5 10.5 %all-to-all-start.1 = ((bf16[128,144,128]{2,1,0:T(8,128)(2,1)}), bf16[128,144,128]{2,1,0:T(8,128)(2,1)}, u32[]{:S(2)}, u32[]{:S(2)}) async-start(bf16[128,144,128]{2,1,0:T(8,128)(2,1)} %fusion.30), calls=%async_computation.1 | async-start | bytes 9437184 | tf_op jit(solution)/shard_map/all_to_all | solution.py:31
  337.1 0.0 copy-done.2
  337.1 0.0 copy-done.3
  337.2 0.1 copy.26
  337.3 0.1 copy.25
  337.4 0.1 min.18
  337.5 0.1 copy.29
  337.6 0.1 copy.28
  337.7 0.1 min.20
  337.9 1.0 slice.63
  338.9 0.1 copy.31
  339.0 9.1 %reshape.196 = bf16[640,3584]{1,0:T(8,128)(2,1)} reshape(bf16[128,140,128]{2,1,0:T(8,128)(2,1)} %bitcast.51) | data formatting | bytes 9175040 | tf_op jit(solution)/shard_map/reshape | solution.py:88
  348.1 47.1 %all-to-all-done.1 = bf16[128,144,128]{2,1,0:T(8,128)(2,1)} async-done(((bf16[128,144,128]{2,1,0:T(8,128)(2,1)}), bf16[128,144,128]{2,1,0:T(8,128)(2,1)}, u32[]{:S(2)}, u32[]{:S(2)}) %all-to-all-start.1) | async-done | bytes 4718624 | tf_op jit(solution)/shard_map/all_to_all | solution.py:31
  395.2 1.0 slice.62
  396.2 0.1 copy.30
  396.3 0.1 copy.32
  396.5 0.2 reshape.198
  396.6 6.8 %gather_fusion.4 = bf16[1024]{0:T(1024)(128)(2,1)S(1)} fusion(bf16[1280]{0:T(1024)(128)(2,1)S(1)} %reshape.198, s32[1024]{0:T(1024)S(1)} %broadcast_clamp_fusion), kind=kCustom, calls=%fused_computation.4 | custom fusion | bytes 8192 | tf_op jit(solution)/shard_map/gather | solution.py:99
  403.4 0.1 reshape.199
  403.5 0.7 copy.33
  404.2 9.1 %reshape.191 = bf16[640,3584]{1,0:T(8,128)(2,1)} reshape(bf16[128,140,128]{2,1,0:T(8,128)(2,1)} %bitcast.52) | data formatting | bytes 9175040 | tf_op jit(solution)/shard_map/reshape | solution.py:88
  413.2 16.7 %gather_fusion.3 = bf16[1024,3584]{1,0:T(8,128)(2,1)} fusion(bf16[640,3584]{1,0:T(8,128)(2,1)} %reshape.196, s32[1024]{0:T(1024)S(1)} %broadcast_clamp_fusion.1), kind=kCustom, calls=%fused_computation.3 | custom fusion | bytes 14684160 | tf_op jit(solution)/shard_map/gather | solution.py:92
  429.9 6.9 %fusion.2 = f32[128,2,3584]{2,1,0:T(2,128)} fusion(bf16[128,2,8]{2,1,0:T(2,128)(2,1)S(1)} %copy.29, bf16[1024,3584]{1,0:T(8,128)(2,1)} %gather_fusion.3), kind=kOutput, calls=%fused_computation.9 | convolution fusion | flops 14680064 | bytes 11014144 | tf_op jit(solution)/shard_map/tpk,tkd->tpd/dot_general | solution.py:94
  436.8 16.9 %gather_fusion.1 = bf16[1024,3584]{1,0:T(8,128)(2,1)} fusion(bf16[640,3584]{1,0:T(8,128)(2,1)} %reshape.191, s32[1024]{0:T(1024)S(1)} %broadcast_clamp_fusion.2), kind=kCustom, calls=%fused_computation.1 | custom fusion | bytes 14684160 | tf_op jit(solution)/shard_map/gather | solution.py:92
  453.7 10.2 %fusion.39 = bf16[128,3584]{1,0:T(8,128)(2,1)} fusion(f32[128,2,3584]{2,1,0:T(2,128)} %fusion.2, bf16[128,2,8]{2,1,0:T(2,128)(2,1)S(1)} %copy.26, bf16[1024,3584]{1,0:T(8,128)(2,1)} %gather_fusion.1), kind=kOutput, calls=%fused_computation.45 | convolution fusion | flops 16973824 | bytes 11931648 | tf_op jit(solution)/shard_map/tpk,tkd->tpd/dot_general | solution.py:94
  (17 shorter events, 0.1 us)
Async XLA Ops:
  14.0 120.0 %all-to-all-start.2 = ((bf16[128,280,128]{2,1,0:T(8,128)(2,1)}), bf16[128,280,128]{2,1,0:T(8,128)(2,1)}, u32[]{:S(2)}, u32[]{:S(2)}) async-start(bf16[128,280,128]{2,1,0:T(8,128)(2,1)} %bitcast.55), calls=%async_computation.2 | async-start | bytes 18350080 | tf_op jit(solution)/shard_map/all_to_all | solution.py:31
  134.0 120.5 %all-to-all-start = ((bf16[128,280,128]{2,1,0:T(8,128)(2,1)}), bf16[128,280,128]{2,1,0:T(8,128)(2,1)}, u32[]{:S(2)}, u32[]{:S(2)}) async-start(bf16[128,280,128]{2,1,0:T(8,128)(2,1)} %bitcast.54), calls=%async_computation | async-start | bytes 18350080 | tf_op jit(solution)/shard_map/all_to_all | solution.py:31
  160.4 8.6 %copy-start = (bf16[640,7168]{1,0:T(8,128)(2,1)S(1)}, bf16[640,7168]{1,0:T(8,128)(2,1)}, u32[]{:S(2)}) copy-start(bf16[640,7168]{1,0:T(8,128)(2,1)} %reshape.194) | copy-start | bytes 27525124
  169.0 10.6 %copy-start.4 = (f32[640,1024]{1,0:T(8,128)}, f32[640,1024]{1,0:T(8,128)S(1)}, u32[]{:S(2)}) copy-start(f32[640,1024]{1,0:T(8,128)S(1)} %fusion.8) | copy-start | bytes 7864324
  254.4 72.1 %all-to-all-start.3 = ((bf16[128,144,128]{2,1,0:T(8,128)(2,1)}), bf16[128,144,128]{2,1,0:T(8,128)(2,1)}, u32[]{:S(2)}, u32[]{:S(2)}) async-start(bf16[128,144,128]{2,1,0:T(8,128)(2,1)} %fusion.31), calls=%async_computation.3 | async-start | bytes 9437184 | tf_op jit(solution)/shard_map/all_to_all | solution.py:31
  280.2 8.6 %copy-start.1 = (bf16[640,7168]{1,0:T(8,128)(2,1)S(1)}, bf16[640,7168]{1,0:T(8,128)(2,1)}, u32[]{:S(2)}) copy-start(bf16[640,7168]{1,0:T(8,128)(2,1)} %reshape.189) | copy-start | bytes 27525124
  288.9 10.7 %copy-start.5 = (f32[640,1024]{1,0:T(8,128)}, f32[640,1024]{1,0:T(8,128)S(1)}, u32[]{:S(2)}) copy-start(f32[640,1024]{1,0:T(8,128)S(1)} %fusion.12) | copy-start | bytes 7864324
  326.5 10.6 %copy-start.2 = (s32[128,8]{0,1:T(8,128)S(1)}, s32[128,8]{0,1:T(8,128)}, u32[]{:S(2)}) copy-start(s32[128,8]{0,1:T(8,128)} %param.11) | copy-start | bytes 12292
  326.5 10.6 %copy-start.3 = (bf16[128,8]{0,1:T(8,128)(2,1)S(1)}, bf16[128,8]{0,1:T(8,128)(2,1)}, u32[]{:S(2)}) copy-start(bf16[128,8]{0,1:T(8,128)(2,1)} %param.9) | copy-start | bytes 6148
  326.5 68.7 %all-to-all-start.1 = ((bf16[128,144,128]{2,1,0:T(8,128)(2,1)}), bf16[128,144,128]{2,1,0:T(8,128)(2,1)}, u32[]{:S(2)}, u32[]{:S(2)}) async-start(bf16[128,144,128]{2,1,0:T(8,128)(2,1)} %fusion.30), calls=%async_computation.1 | async-start | bytes 9437184 | tf_op jit(solution)/shard_map/all_to_all | solution.py:31

commit v4 on v3

--- a/solution.py
+++ b/solution.py
@@ -65,9 +65,9 @@
     expert_flat = expert_ids.reshape(-1)
     same_group = group_of == group_of[:, :1]
     selector = jnp.stack([same_group, jnp.logical_not(same_group)], axis=1)
-    gate_rowwise = gate_weights.reshape(rows_dev, 1, TOPK)
+    pick = jnp.where(selector, gate_weights.reshape(rows_dev, 1, TOPK), jnp.bfloat16(0))
     summed = None
-    gate_backs = []
+    gate_sum = None
     for c in range(CHUNKS):
         table = slot_table[:, c * part:(c + 1) * part]
         sent = joined[table // TOPK].reshape(experts, part * blocks, LANES)
@@ -86,17 +86,22 @@
         )
         returned = exchange(back)
         rows_back = returned[:, :back_blocks, :].reshape(part_rows, features)
-        gate_backs.append(returned[:, back_blocks, :part])
-        in_chunk = (slot_flat // part == c).reshape(rows_dev, 1, TOPK)
-        where = jnp.clip(expert_flat * part + slot_flat - c * part, 0, part_rows - 1)
-        gathered = rows_back[where].reshape(rows_dev, TOPK, features)
-        pick = jnp.where(jnp.logical_and(selector, in_chunk), gate_rowwise, jnp.bfloat16(0))
-        partial = jnp.einsum(
-            "tpk,tkd->tpd", pick, gathered, preferred_element_type=jnp.float32
-        )
+        gates_back = returned[:, back_blocks, :part].reshape(part_rows)
+        in_chunk = slot_flat // part == c
+        spot = jnp.where(in_chunk, expert_flat * part + slot_flat - c * part, -1)
+        onehot = (
+            spot.reshape(rows_dev, TOPK, 1) == jnp.arange(part_rows, dtype=jnp.int32)
+        ).astype(jnp.bfloat16)
+        chooser = jnp.einsum(
+            "tpk,tkj->tpj", pick, onehot, preferred_element_type=jnp.float32
+        ).astype(jnp.bfloat16)
+        partial = jnp.einsum("tpj,jd->tpd", chooser, rows_back, preferred_element_type=jnp.float32)
+        gate_part = jnp.einsum("tkj,j->tk", onehot, gates_back, preferred_element_type=jnp.float32)
+        if c < CHUNKS - 1:
+            partial, gate_part = lax.optimization_barrier((partial, gate_part))
         summed = partial if summed is None else summed + partial
-    all_gate = jnp.concatenate(gate_backs, axis=1)
-    gate_grad = all_gate.reshape(-1)[target].reshape(rows_dev, TOPK)
+        gate_sum = gate_part if gate_sum is None else gate_sum + gate_part
+    gate_grad = gate_sum.astype(jnp.bfloat16)
     halves = summed.astype(jnp.bfloat16)
     token_grad = jnp.sum(halves.astype(jnp.float32), axis=1).astype(jnp.bfloat16)
     return (token_grad, gate_grad)

time: 471 us -> 412 us (0.87); the launches traced: 464 us -> 410 us
  local copies, waits for them, and re-layouts: 126 us -> 85 us
  matrix products: 80 us -> 73.1 us
    gather x3 -> x0, local copies, waits for them, and re-layouts: 40.4 us -> none  [the longest x2 33.6 us: layer(): gathered = rows_back[where].reshape(rows_dev, TOPK, features)]
    dot_general x2, matrix products: 21.3 us -> 15.3 us  [expert_rows(): lax.dot_general(grad_rows, down_matrix, (((1,), (1,)), ((), ())), preferr...]
    dot_general x2 -> x6, matrix products: 17.1 us -> 20.4 us  [the longest x2 11.9 us: layer(): jnp.einsum('tpj,jd->tpd', chooser, rows_back, preferred_element_type=jnp....]
  transfers between devices with their start and end apart: 4 -> 4, of which waited for: 3 -> 4; matrix products, arithmetic and copies ran while one was open for 29% -> 33% of each run, Pallas kernels for 0% -> 0%
where the time goes in v4:
time: 412 us; the launch traced here: 410 us
  waiting for transfers between devices  196 us (48%)
  local copies, waits for them, and re-layouts  85 us (21%)
  matrix products  73.1 us (18%)
  starting transfers between devices  42.5 us (10%)
  other arithmetic  13 us (3%)
    all_to_all x4, waiting for transfers between devices, exchange(): lax.all_to_all(x, ('group', 'dev'), split_axis=0, concat_axis=0, tiled=True)  196 us
    all_to_all x4, starting transfers between devices, exchange(): lax.all_to_all(x, ('group', 'dev'), split_axis=0, concat_axis=0, tiled=True)  42.5 us
    reshape x2, local copies, waits for them, and re-layouts, layer(): data = arrived.reshape(part_rows, both)  27.7 us
    dot_general x2, matrix products, expert_rows(): lax.dot_general(inner_grad, up_matrix, (((1,), (1,)), ((), ())), preferre...  20.1 us
    reshape x2, local copies, waits for them, and re-layouts, layer(): contrib.reshape(experts, back_blocks, LANES)  19.3 us
    reshape x2, local copies, waits for them, and re-layouts, layer(): rows_back = returned[:, :back_blocks, :].reshape(part_rows, features)  18.2 us
    dot_general x2, matrix products, expert_rows(): raised = jnp.dot(token_rows, up_matrix, preferred_element_type=jnp.float32)  17.3 us
    dot_general x2, matrix products, expert_rows(): lax.dot_general(grad_rows, down_matrix, (((1,), (1,)), ((), ())), preferr...  15.3 us
  transfers between devices with their start and end apart: 4, of which 4 were waited for; matrix products, arithmetic and copies ran while one was open for 33% of the time, Pallas kernels for 0%

profile of v4, /device:TPU:1, one launch (start us, length us, event | category | flops | bytes accessed | tf_op | source)
XLA Modules:
  0.0 410.1 jit_solution(12744854065409838561)
XLA Ops:
  0.6 0.7 add_select_fusion.5
  1.3 0.1 copy.12
  1.5 0.1 reshape.115
  1.6 4.3 %scatter_custom_fusion = s32[1280]{0:T(1024)S(1)} fusion(s32[1024]{0:T(1024)S(1)} %bitcast.51, s32[1024]{0:T(1024)S(1)} %iota.8, s32[]{:T(128)} %constant.64.clone.1), kind=kCustom, calls=%fused_computation.86 | custom fusion | bytes 5124 | tf_op jit(solution)/shard_map/scatter | solution.py:62
  5.9 0.1 reshape.116
  6.0 0.1 compare_select_fusion
  6.2 0.2 reshape.127
  6.4 1.6 fusion.33
  8.0 0.4 copy.21
  8.4 0.3 slice.58
  8.8 5.2 %gather_fusion = bf16[640,56,128]{2,1,0:T(8,128)(2,1)} fusion(bf16[129,56,128]{2,1,0:T(8,128)(2,1)S(1)} %slice.58, s32[1024]{0:T(1024)S(1)} %pad_clamp_fusion.1), kind=kCustom, calls=%fused_computation | custom fusion | bytes 18352640 | tf_op jit(solution)/shard_map/gather | solution.py:73
  14.0 11.9 %all-to-all-start = ((bf16[128,280,128]{2,1,0:T(8,128)(2,1)}), bf16[128,280,128]{2,1,0:T(8,128)(2,1)}, u32[]{:S(2)}, u32[]{:S(2)}) async-start(bf16[128,280,128]{2,1,0:T(8,128)(2,1)} %bitcast.47), calls=%async_computation | async-start | bytes 18350080 | tf_op jit(solution)/shard_map/all_to_all | solution.py:31
  25.9 0.2 reshape.135
  26.1 5.2 %gather_fusion.1 = bf16[640,56,128]{2,1,0:T(8,128)(2,1)} fusion(bf16[129,56,128]{2,1,0:T(8,128)(2,1)S(1)} %slice.58, s32[1024]{0:T(1024)S(1)} %pad_clamp_fusion), kind=kCustom, calls=%fused_computation.1 | custom fusion | bytes 18352640 | tf_op jit(solution)/shard_map/gather | solution.py:73
  31.3 102.6 %all-to-all-done = bf16[128,280,128]{2,1,0:T(8,128)(2,1)} async-done(((bf16[128,280,128]{2,1,0:T(8,128)(2,1)}), bf16[128,280,128]{2,1,0:T(8,128)(2,1)}, u32[]{:S(2)}, u32[]{:S(2)}) %all-to-all-start) | async-done | bytes 9175072 | tf_op jit(solution)/shard_map/all_to_all | solution.py:31
  134.0 11.9 %all-to-all-start.2 = ((bf16[128,280,128]{2,1,0:T(8,128)(2,1)}), bf16[128,280,128]{2,1,0:T(8,128)(2,1)}, u32[]{:S(2)}, u32[]{:S(2)}) async-start(bf16[128,280,128]{2,1,0:T(8,128)(2,1)} %bitcast.46), calls=%async_computation.2 | async-start | bytes 18350080 | tf_op jit(solution)/shard_map/all_to_all | solution.py:31
  145.9 13.9 %reshape.118 = bf16[640,7168]{1,0:T(8,128)(2,1)} reshape(bf16[128,280,128]{2,1,0:T(8,128)(2,1)} %all-to-all-done) | data formatting | bytes 18350080 | tf_op jit(solution)/shard_map/reshape | solution.py:75
  159.8 0.0 copy-start
  159.8 8.6 %fusion.8 = f32[640,1024]{1,0:T(8,128)S(1)} fusion(bf16[1,3584,1024]{2,1,0:T(8,128)(2,1)} %param.12, bf16[640,7168]{1,0:T(8,128)(2,1)} %reshape.118), kind=kOutput, calls=%fused_computation.12 | convolution fusion | flops 4697620480 | bytes 14548992 | tf_op jit(solution)/shard_map/dot_general | solution.py:18
  168.4 0.0 copy-done
  168.4 7.6 %multiply_reduce_fusion.1 = (bf16[640]{0:T(1024)(128)(2,1)S(1)}, f32[640,1024]{1,0:T(8,128)S(1)}) fusion(f32[640,1024]{1,0:T(8,128)S(1)} %fusion.8, bf16[1,1024,3584]{2,1,0:T(8,128)(2,1)} %param.13, bf16[640,7168]{1,0:T(8,128)(2,1)S(1)} %copy-done), kind=kOutput, calls=%fused_computation.37 | convolution fusion | flops 4701552128 | bytes 17171712 | tf_op jit(solution)/shard_map/dot_general | solution.py:19
  176.1 10.1 %fusion.14 = bf16[640,3584]{1,0:T(8,128)(2,1)} fusion(bf16[1,3584,1024]{2,1,0:T(8,128)(2,1)} %param.12, f32[640,1024]{1,0:T(8,128)S(1)} %get-tuple-element.15, f32[640,1024]{1,0:T(8,128)S(1)} %fusion.8), kind=kOutput, calls=%fused_computation.18 | convolution fusion | flops 4705812480 | bytes 17170432 | tf_op jit(solution)/shard_map/dot_general | solution.py:24
  186.2 9.6 %reshape.119 = bf16[128,140,128]{2,1,0:T(8,128)(2,1)} reshape(bf16[640,3584]{1,0:T(8,128)(2,1)} %fusion.14) | data formatting | bytes 9175040 | tf_op jit(solution)/shard_map/reshape | solution.py:82
  195.8 0.2 convert_element_type.69
  196.0 5.0 %fusion.21 = bf16[128,144,128]{2,1,0:T(8,128)(2,1)} fusion(bf16[128,1,5]{2,1,0:T(2,128)(2,1)S(1)} %convert_element_type.69, bf16[128,140,128]{2,1,0:T(8,128)(2,1)} %reshape.119), kind=kLoop, calls=%fused_computation.22 | loop fusion | flops 14155776 | bytes 9307392 | tf_op jit(solution)/shard_map/concatenate | solution.py:80
  201.0 52.9 %all-to-all-done.2 = bf16[128,280,128]{2,1,0:T(8,128)(2,1)} async-done(((bf16[128,280,128]{2,1,0:T(8,128)(2,1)}), bf16[128,280,128]{2,1,0:T(8,128)(2,1)}, u32[]{:S(2)}, u32[]{:S(2)}) %all-to-all-start.2) | async-done | bytes 9175072 | tf_op jit(solution)/shard_map/all_to_all | solution.py:31
  254.0 11.8 %all-to-all-start.1 = ((bf16[128,144,128]{2,1,0:T(8,128)(2,1)}), bf16[128,144,128]{2,1,0:T(8,128)(2,1)}, u32[]{:S(2)}, u32[]{:S(2)}) async-start(bf16[128,144,128]{2,1,0:T(8,128)(2,1)} %fusion.21), calls=%async_computation.1 | async-start | bytes 9437184 | tf_op jit(solution)/shard_map/all_to_all | solution.py:31
  265.8 13.8 %reshape.122 = bf16[640,7168]{1,0:T(8,128)(2,1)} reshape(bf16[128,280,128]{2,1,0:T(8,128)(2,1)} %all-to-all-done.2) | data formatting | bytes 18350080 | tf_op jit(solution)/shard_map/reshape | solution.py:75
  279.6 0.0 copy-start.1
  279.6 8.6 %fusion.4 = f32[640,1024]{1,0:T(8,128)S(1)} fusion(bf16[1,3584,1024]{2,1,0:T(8,128)(2,1)} %param.12, bf16[640,7168]{1,0:T(8,128)(2,1)} %reshape.122), kind=kOutput, calls=%fused_computation.8 | convolution fusion | flops 4697620480 | bytes 14548992 | tf_op jit(solution)/shard_map/dot_general | solution.py:18
  288.2 0.0 copy-done.1
  288.3 7.6 %multiply_reduce_fusion = (bf16[640]{0:T(1024)(128)(2,1)S(1)}, f32[640,1024]{1,0:T(8,128)S(1)}) fusion(f32[640,1024]{1,0:T(8,128)S(1)} %fusion.4, bf16[1,1024,3584]{2,1,0:T(8,128)(2,1)} %param.13, bf16[640,7168]{1,0:T(8,128)(2,1)S(1)} %copy-done.1), kind=kOutput, calls=%fused_computation.31 | convolution fusion | flops 4701552128 | bytes 17171712 | tf_op jit(solution)/shard_map/dot_general | solution.py:19
  295.9 10.0 %fusion.17 = bf16[640,3584]{1,0:T(8,128)(2,1)} fusion(bf16[1,3584,1024]{2,1,0:T(8,128)(2,1)} %param.12, f32[640,1024]{1,0:T(8,128)S(1)} %get-tuple-element.17, f32[640,1024]{1,0:T(8,128)S(1)} %fusion.4), kind=kOutput, calls=%fused_computation.19 | convolution fusion | flops 4705812480 | bytes 17170432 | tf_op jit(solution)/shard_map/dot_general | solution.py:24
  305.9 9.7 %reshape.123 = bf16[128,140,128]{2,1,0:T(8,128)(2,1)} reshape(bf16[640,3584]{1,0:T(8,128)(2,1)} %fusion.17) | data formatting | bytes 9175040 | tf_op jit(solution)/shard_map/reshape | solution.py:82
  315.6 0.2 convert_element_type.70
  315.8 4.9 %fusion.22 = bf16[128,144,128]{2,1,0:T(8,128)(2,1)} fusion(bf16[128,1,5]{2,1,0:T(2,128)(2,1)S(1)} %convert_element_type.70, bf16[128,140,128]{2,1,0:T(8,128)(2,1)} %reshape.123), kind=kLoop, calls=%fused_computation.23 | loop fusion | flops 14155776 | bytes 9307392 | tf_op jit(solution)/shard_map/concatenate | solution.py:80
  320.8 0.0 copy-start.2
  320.8 3.3 all-to-all-done.1
  324.0 6.9 %all-to-all-start.3 = ((bf16[128,144,128]{2,1,0:T(8,128)(2,1)}), bf16[128,144,128]{2,1,0:T(8,128)(2,1)}, u32[]{:S(2)}, u32[]{:S(2)}) async-start(bf16[128,144,128]{2,1,0:T(8,128)(2,1)} %fusion.22), calls=%async_computation.3 | async-start | bytes 9437184 | tf_op jit(solution)/shard_map/all_to_all | solution.py:31
  331.0 0.0 copy-done.2
  331.0 0.1 copy.16
  331.1 0.1 copy.11
  331.2 0.1 copy.14
  331.3 0.6 fusion.32
  332.0 0.6 fusion.30
  332.6 9.1 %reshape.155 = bf16[640,3584,1]{1,0,2:T(8,128)(2,1)} reshape(bf16[128,140,128]{2,1,0:T(8,128)(2,1)} %bitcast.44) | data formatting | bytes 9175040 | tf_op jit(solution)/shard_map/reshape | solution.py:88
  341.7 1.2 slice_reduce_fusion.1
  342.9 0.2 reshape.156
  343.1 3.6 fusion.31
  346.7 0.1 copy.18
  346.8 5.7 %fusion.41 = f32[128,2,3584]{2,0,1:T(8,128)} fusion(bf16[640,3584,1]{1,0,2:T(8,128)(2,1)} %reshape.155, bf16[128,2,640]{2,1,0:T(2,128)(2,1)S(1)} %fusion.32), kind=kOutput, calls=%fused_computation.53 | convolution fusion | flops 1174405120 | bytes 8585216 | tf_op jit(solution)/shard_map/tpj,jd->tpd/dot_general | solution.py:98
  352.5 36.7 %all-to-all-done.3 = bf16[128,144,128]{2,1,0:T(8,128)(2,1)} async-done(((bf16[128,144,128]{2,1,0:T(8,128)(2,1)}), bf16[128,144,128]{2,1,0:T(8,128)(2,1)}, u32[]{:S(2)}, u32[]{:S(2)}) %all-to-all-start.3) | async-done | bytes 4718624 | tf_op jit(solution)/shard_map/all_to_all | solution.py:31
  389.2 1.2 slice_reduce_fusion
  390.4 0.2 reshape.159
  390.6 3.6 fusion.29
  394.2 0.1 copy.20
  394.3 9.1 %reshape.158 = bf16[640,3584,1]{1,0,2:T(8,128)(2,1)} reshape(bf16[128,140,128]{2,1,0:T(8,128)(2,1)} %bitcast.45) | data formatting | bytes 9175040 | tf_op jit(solution)/shard_map/reshape | solution.py:88
  403.3 0.6 fusion.47
  403.9 6.2 %fusion.34 = bf16[128,3584]{1,0:T(8,128)(2,1)} fusion(f32[128,2,3584]{2,0,1:T(8,128)} %fusion.41, bf16[640,3584,1]{1,0,2:T(8,128)(2,1)} %reshape.158, bf16[128,2,640]{2,1,0:T(2,128)(2,1)S(1)} %fusion.30), kind=kOutput, calls=%fused_computation.44 | convolution fusion | flops 1176698880 | bytes 9502720 | tf_op jit(solution)/shard_map/tpj,jd->tpd/dot_general | solution.py:98
  (7 shorter events, 0.0 us)
Async XLA Ops:
  14.0 120.0 %all-to-all-start = ((bf16[128,280,128]{2,1,0:T(8,128)(2,1)}), bf16[128,280,128]{2,1,0:T(8,128)(2,1)}, u32[]{:S(2)}, u32[]{:S(2)}) async-start(bf16[128,280,128]{2,1,0:T(8,128)(2,1)} %bitcast.47), calls=%async_computation | async-start | bytes 18350080 | tf_op jit(solution)/shard_map/all_to_all | solution.py:31
  134.0 120.0 %all-to-all-start.2 = ((bf16[128,280,128]{2,1,0:T(8,128)(2,1)}), bf16[128,280,128]{2,1,0:T(8,128)(2,1)}, u32[]{:S(2)}, u32[]{:S(2)}) async-start(bf16[128,280,128]{2,1,0:T(8,128)(2,1)} %bitcast.46), calls=%async_computation.2 | async-start | bytes 18350080 | tf_op jit(solution)/shard_map/all_to_all | solution.py:31
  159.8 8.6 %copy-start = (bf16[640,7168]{1,0:T(8,128)(2,1)S(1)}, bf16[640,7168]{1,0:T(8,128)(2,1)}, u32[]{:S(2)}) copy-start(bf16[640,7168]{1,0:T(8,128)(2,1)} %reshape.118) | copy-start | bytes 27525124
  254.0 70.1 %all-to-all-start.1 = ((bf16[128,144,128]{2,1,0:T(8,128)(2,1)}), bf16[128,144,128]{2,1,0:T(8,128)(2,1)}, u32[]{:S(2)}, u32[]{:S(2)}) async-start(bf16[128,144,128]{2,1,0:T(8,128)(2,1)} %fusion.21), calls=%async_computation.1 | async-start | bytes 9437184 | tf_op jit(solution)/shard_map/all_to_all | solution.py:31
  279.6 8.6 %copy-start.1 = (bf16[640,7168]{1,0:T(8,128)(2,1)S(1)}, bf16[640,7168]{1,0:T(8,128)(2,1)}, u32[]{:S(2)}) copy-start(bf16[640,7168]{1,0:T(8,128)(2,1)} %reshape.122) | copy-start | bytes 27525124
  320.8 10.2 %copy-start.2 = (bf16[128,8]{0,1:T(8,128)(2,1)S(1)}, bf16[128,8]{0,1:T(8,128)(2,1)}, u32[]{:S(2)}) copy-start(bf16[128,8]{0,1:T(8,128)(2,1)} %param.9) | copy-start | bytes 6148
  324.0 65.1 %all-to-all-start.3 = ((bf16[128,144,128]{2,1,0:T(8,128)(2,1)}), bf16[128,144,128]{2,1,0:T(8,128)(2,1)}, u32[]{:S(2)}, u32[]{:S(2)}) async-start(bf16[128,144,128]{2,1,0:T(8,128)(2,1)} %fusion.22), calls=%async_computation.3 | async-start | bytes 9437184 | tf_op jit(solution)/shard_map/all_to_all | solution.py:31

commit v5 on v4

--- a/solution.py
+++ b/solution.py
@@ -5,8 +5,6 @@
 
 TOPK = 8
 LANES = 128
-CHUNKS = 2
-BACK_ROWS = 4
 
 
 def silu_slope(values):
@@ -50,8 +48,9 @@
     group_of = expert_ids // per_group
     both = 2 * features
     blocks = both // LANES
-    part = capacity // CHUNKS
-    part_rows = experts * part
+    first = (3 * capacity + 4) // 5
+    sizes = (first, capacity - first)
+    starts = (0, first)
     joined = jnp.concatenate(
         [jnp.concatenate([tokens, out_grad], axis=1), jnp.zeros((1, both), jnp.bfloat16)]
     ).reshape(rows_dev + 1, blocks, LANES)
@@ -68,8 +67,9 @@
     pick = jnp.where(selector, gate_weights.reshape(rows_dev, 1, TOPK), jnp.bfloat16(0))
     summed = None
     gate_sum = None
-    for c in range(CHUNKS):
-        table = slot_table[:, c * part:(c + 1) * part]
+    for c, (begin, part) in enumerate(zip(starts, sizes)):
+        part_rows = experts * part
+        table = slot_table[:, begin:begin + part]
         sent = joined[table // TOPK].reshape(experts, part * blocks, LANES)
         arrived = exchange(sent)
         data = arrived.reshape(part_rows, both)
@@ -77,18 +77,19 @@
             data[:, :features], data[:, features:], up_matrix, down_matrix
         )
         back_blocks = part * features // LANES
+        side_rows = 8 - back_blocks % 8
         back = jnp.concatenate(
             [
                 contrib.reshape(experts, back_blocks, LANES),
-                side_block(gate_rows.reshape(experts, part), BACK_ROWS),
+                side_block(gate_rows.reshape(experts, part), side_rows),
             ],
             axis=1,
         )
         returned = exchange(back)
         rows_back = returned[:, :back_blocks, :].reshape(part_rows, features)
         gates_back = returned[:, back_blocks, :part].reshape(part_rows)
-        in_chunk = slot_flat // part == c
-        spot = jnp.where(in_chunk, expert_flat * part + slot_flat - c * part, -1)
+        in_chunk = jnp.logical_and(slot_flat >= begin, slot_flat < begin + part)
+        spot = jnp.where(in_chunk, expert_flat * part + slot_flat - begin, -1)
         onehot = (
             spot.reshape(rows_dev, TOPK, 1) == jnp.arange(part_rows, dtype=jnp.int32)
         ).astype(jnp.bfloat16)
@@ -97,7 +98,7 @@
         ).astype(jnp.bfloat16)
         partial = jnp.einsum("tpj,jd->tpd", chooser, rows_back, preferred_element_type=jnp.float32)
         gate_part = jnp.einsum("tkj,j->tk", onehot, gates_back, preferred_element_type=jnp.float32)
-        if c < CHUNKS - 1:
+        if c < len(sizes) - 1:
             partial, gate_part = lax.optimization_barrier((partial, gate_part))
         summed = partial if summed is None else summed + partial
         gate_sum = gate_part if gate_sum is None else gate_sum + gate_part

time: 412 us -> 440 us (1.068)
  waiting for transfers between devices: 196 us -> 216 us
  local copies, waits for them, and re-layouts: 85 us -> 94.3 us
  matrix products: 73.1 us -> 66.5 us
  starting transfers between devices: 42.5 us -> 48.1 us
    all_to_all x4, waiting for transfers between devices: 196 us -> 216 us  [exchange(): lax.all_to_all(x, ('group', 'dev'), split_axis=0, concat_axis=0, tiled=True)]
    slice x0 -> x2, local copies, waits for them, and re-layouts: none -> 9.47 us  [layer(): rows_back = returned[:, :back_blocks, :].reshape(part_rows, features)]
    all_to_all x4, starting transfers between devices: 42.5 us -> 48.1 us  [exchange(): lax.all_to_all(x, ('group', 'dev'), split_axis=0, concat_axis=0, tiled=True)]
    dot_general x2, matrix products: 11.9 us -> 6.38 us  [layer(): jnp.einsum('tpj,jd->tpd', chooser, rows_back, preferred_element_type=jnp....]
  transfers between devices with their start and end apart: 4 -> 4, of which waited for: 4 -> 3; matrix products, arithmetic and copies ran while one was open for 33% -> 30% of each run, Pallas kernels for 0% -> 0%
where the time goes in v5:
time: 440 us; the launch traced here: 438 us
  waiting for transfers between devices  216 us (49%)
  local copies, waits for them, and re-layouts  94.3 us (21%)
  matrix products  66.5 us (15%)
  starting transfers between devices  48.1 us (11%)
  other arithmetic  12.3 us (3%)
    all_to_all x4, waiting for transfers between devices, exchange(): lax.all_to_all(x, ('group', 'dev'), split_axis=0, concat_axis=0, tiled=True)  216 us
    all_to_all x4, starting transfers between devices, exchange(): lax.all_to_all(x, ('group', 'dev'), split_axis=0, concat_axis=0, tiled=True)  48.1 us
    reshape x2, local copies, waits for them, and re-layouts, layer(): data = arrived.reshape(part_rows, both)  28.1 us
    dot_general x2, matrix products, expert_rows(): lax.dot_general(inner_grad, up_matrix, (((1,), (1,)), ((), ())), preferre...  20.2 us
    reshape x2, local copies, waits for them, and re-layouts, layer(): contrib.reshape(experts, back_blocks, LANES)  19.1 us
    reshape x2, local copies, waits for them, and re-layouts, layer(): rows_back = returned[:, :back_blocks, :].reshape(part_rows, features)  18.3 us
    dot_general x2, matrix products, expert_rows(): raised = jnp.dot(token_rows, up_matrix, preferred_element_type=jnp.float32)  17.3 us
    dot_general x2, matrix products, expert_rows(): lax.dot_general(grad_rows, down_matrix, (((1,), (1,)), ((), ())), preferr...  15.3 us
  transfers between devices with their start and end apart: 4, of which 3 were waited for; matrix products, arithmetic and copies ran while one was open for 30% of the time, Pallas kernels for 0%

profile of v5, /device:TPU:1, one launch (start us, length us, event | category | flops | bytes accessed | tf_op | source)
XLA Modules:
  0.0 438.1 jit_solution(12214298133746646489)
XLA Ops:
  0.6 0.7 add_select_fusion.4
  1.3 0.1 copy.20
  1.4 0.1 reshape.113
  1.6 4.3 scatter_custom_fusion
  5.9 0.1 reshape.114
  6.0 1.6 fusion.33
  7.7 0.4 copy.31
  8.1 0.3 slice.58
  8.4 0.1 compare_select_fusion
  8.5 0.1 reshape.133
  8.7 4.6 %gather_fusion.1 = bf16[512,56,128]{2,1,0:T(8,128)(2,1)} fusion(bf16[129,56,128]{2,1,0:T(8,128)(2,1)S(1)} %slice.58, s32[1024]{0:T(1024)S(1)} %pad_clamp_fusion), kind=kCustom, calls=%fused_computation.1 | custom fusion | bytes 14682112 | tf_op jit(solution)/shard_map/gather | solution.py:73
  13.3 11.9 %all-to-all-start.2 = ((bf16[128,224,128]{2,1,0:T(8,128)(2,1)}), bf16[128,224,128]{2,1,0:T(8,128)(2,1)}, u32[]{:S(2)}, u32[]{:S(2)}) async-start(bf16[128,224,128]{2,1,0:T(8,128)(2,1)} %bitcast.45), calls=%async_computation.2 | async-start | bytes 14680064 | tf_op jit(solution)/shard_map/all_to_all | solution.py:29
  25.2 0.1 reshape.125
  25.4 5.8 %gather_fusion = bf16[768,56,128]{2,1,0:T(8,128)(2,1)} fusion(bf16[129,56,128]{2,1,0:T(8,128)(2,1)S(1)} %slice.58, s32[1024]{0:T(1024)S(1)} %pad_clamp_fusion.1), kind=kCustom, calls=%fused_computation | custom fusion | bytes 22023168 | tf_op jit(solution)/shard_map/gather | solution.py:73
  31.2 81.0 %all-to-all-done.2 = bf16[128,224,128]{2,1,0:T(8,128)(2,1)} async-done(((bf16[128,224,128]{2,1,0:T(8,128)(2,1)}), bf16[128,224,128]{2,1,0:T(8,128)(2,1)}, u32[]{:S(2)}, u32[]{:S(2)}) %all-to-all-start.2) | async-done | bytes 7340064 | tf_op jit(solution)/shard_map/all_to_all | solution.py:29
  112.2 8.6 %all-to-all-start = ((bf16[128,336,128]{2,1,0:T(8,128)(2,1)}), bf16[128,336,128]{2,1,0:T(8,128)(2,1)}, u32[]{:S(2)}, u32[]{:S(2)}) async-start(bf16[128,336,128]{2,1,0:T(8,128)(2,1)} %bitcast.44), calls=%async_computation | async-start | bytes 22020096 | tf_op jit(solution)/shard_map/all_to_all | solution.py:29
  120.8 11.6 %reshape.120 = bf16[512,7168]{1,0:T(8,128)(2,1)} reshape(bf16[128,224,128]{2,1,0:T(8,128)(2,1)} %all-to-all-done.2) | data formatting | bytes 14680064 | tf_op jit(solution)/shard_map/reshape | solution.py:75
  132.4 0.0 copy-start.2
  132.4 7.4 %fusion.4 = f32[512,1024]{1,0:T(8,128)S(1)} fusion(bf16[1,3584,1024]{2,1,0:T(8,128)(2,1)} %param.12, bf16[512,7168]{1,0:T(8,128)(2,1)} %reshape.120), kind=kOutput, calls=%fused_computation.9 | convolution fusion | flops 3758096384 | bytes 13107200 | tf_op jit(solution)/shard_map/dot_general | solution.py:16
  139.8 0.0 copy-done.2
  139.8 6.6 %multiply_reduce_fusion.1 = (bf16[512]{0:T(512)(128)(2,1)S(1)}, f32[512,1024]{1,0:T(8,128)S(1)}) fusion(f32[512,1024]{1,0:T(8,128)S(1)} %fusion.4, bf16[1,1024,3584]{2,1,0:T(8,128)(2,1)} %param.13, bf16[512,7168]{1,0:T(8,128)(2,1)S(1)} %copy-done.2), kind=kOutput, calls=%fused_computation.38 | convolution fusion | flops 3761241600 | bytes 15205376 | tf_op jit(solution)/shard_map/dot_general | solution.py:17
  146.5 8.9 %fusion.17 = bf16[512,3584]{1,0:T(8,128)(2,1)} fusion(bf16[1,3584,1024]{2,1,0:T(8,128)(2,1)} %param.12, f32[512,1024]{1,0:T(8,128)S(1)} %get-tuple-element.15, f32[512,1024]{1,0:T(8,128)S(1)} %fusion.4), kind=kOutput, calls=%fused_computation.20 | convolution fusion | flops 3764649984 | bytes 15204352 | tf_op jit(solution)/shard_map/dot_general | solution.py:22
  155.3 7.9 %reshape.121 = bf16[128,112,128]{2,1,0:T(8,128)(2,1)} reshape(bf16[512,3584]{1,0:T(8,128)(2,1)} %fusion.17) | data formatting | bytes 7340032 | tf_op jit(solution)/shard_map/reshape | solution.py:83
  163.3 0.1 convert_element_type.71
  163.4 3.6 fusion.24
  167.0 83.0 %all-to-all-done = bf16[128,336,128]{2,1,0:T(8,128)(2,1)} async-done(((bf16[128,336,128]{2,1,0:T(8,128)(2,1)}), bf16[128,336,128]{2,1,0:T(8,128)(2,1)}, u32[]{:S(2)}, u32[]{:S(2)}) %all-to-all-start) | async-done | bytes 11010080 | tf_op jit(solution)/shard_map/all_to_all | solution.py:29
  250.0 17.4 %all-to-all-start.3 = ((bf16[128,120,128]{2,1,0:T(8,128)(2,1)}), bf16[128,120,128]{2,1,0:T(8,128)(2,1)}, u32[]{:S(2)}, u32[]{:S(2)}) async-start(bf16[128,120,128]{2,1,0:T(8,128)(2,1)} %fusion.24), calls=%async_computation.3 | async-start | bytes 7864320 | tf_op jit(solution)/shard_map/all_to_all | solution.py:29
  267.4 16.5 %reshape.116 = bf16[768,7168]{1,0:T(8,128)(2,1)} reshape(bf16[128,336,128]{2,1,0:T(8,128)(2,1)} %all-to-all-done) | data formatting | bytes 22020096 | tf_op jit(solution)/shard_map/reshape | solution.py:75
  284.0 0.0 copy-start.1
  284.0 9.8 %fusion.8 = f32[768,1024]{1,0:T(8,128)S(1)} fusion(bf16[1,3584,1024]{2,1,0:T(8,128)(2,1)} %param.12, bf16[768,7168]{1,0:T(8,128)(2,1)} %reshape.116), kind=kOutput, calls=%fused_computation.13 | convolution fusion | flops 5637144576 | bytes 15990784 | tf_op jit(solution)/shard_map/dot_general | solution.py:16
  293.8 0.0 copy-done.1
  293.8 8.7 %multiply_reduce_fusion = (bf16[768]{0:T(1024)(128)(2,1)S(1)}, f32[768,1024]{1,0:T(8,128)S(1)}) fusion(f32[768,1024]{1,0:T(8,128)S(1)} %fusion.8, bf16[1,1024,3584]{2,1,0:T(8,128)(2,1)} %param.13, bf16[768,7168]{1,0:T(8,128)(2,1)S(1)} %copy-done.1), kind=kOutput, calls=%fused_computation.32 | convolution fusion | flops 5641862144 | bytes 19138048 | tf_op jit(solution)/shard_map/dot_general | solution.py:17
  302.5 11.4 %fusion.14 = bf16[768,3584]{1,0:T(8,128)(2,1)} fusion(bf16[1,3584,1024]{2,1,0:T(8,128)(2,1)} %param.12, f32[768,1024]{1,0:T(8,128)S(1)} %get-tuple-element.13, f32[768,1024]{1,0:T(8,128)S(1)} %fusion.8), kind=kOutput, calls=%fused_computation.19 | convolution fusion | flops 5646974976 | bytes 19136512 | tf_op jit(solution)/shard_map/dot_general | solution.py:22
  313.8 11.1 %reshape.117 = bf16[128,168,128]{2,1,0:T(8,128)(2,1)} reshape(bf16[768,3584]{1,0:T(8,128)(2,1)} %fusion.14) | data formatting | bytes 11010048 | tf_op jit(solution)/shard_map/reshape | solution.py:83
  325.0 0.2 convert_element_type.70
  325.1 5.6 %fusion.20 = bf16[128,176,128]{2,1,0:T(8,128)(2,1)} fusion(bf16[128,1,6]{2,1,0:T(2,128)(2,1)S(1)} %convert_element_type.70, bf16[128,168,128]{2,1,0:T(8,128)(2,1)} %reshape.117), kind=kLoop, calls=%fused_computation.21 | loop fusion | flops 17301504 | bytes 11273728 | tf_op jit(solution)/shard_map/concatenate | solution.py:81
  330.7 0.0 copy-start.3
  330.7 0.0 all-to-all-done.3
  330.7 10.2 %all-to-all-start.1 = ((bf16[128,176,128]{2,1,0:T(8,128)(2,1)}), bf16[128,176,128]{2,1,0:T(8,128)(2,1)}, u32[]{:S(2)}, u32[]{:S(2)}) async-start(bf16[128,176,128]{2,1,0:T(8,128)(2,1)} %fusion.20), calls=%async_computation.1 | async-start | bytes 11534336 | tf_op jit(solution)/shard_map/all_to_all | solution.py:29
  340.9 0.0 copy-done.3
  340.9 0.1 copy.19
  341.1 0.1 copy.18
  341.2 0.1 copy.23
  341.3 0.6 fusion.39
  341.8 0.8 fusion.38
  342.6 1.1 slice_reduce_fusion
  343.7 0.1 reshape.157
  343.9 2.5 fusion.31
  346.3 0.1 copy.28
  346.4 4.2 slice.56
  350.6 7.7 %reshape.156 = bf16[512,3584,1]{1,0,2:T(8,128)(2,1)} reshape(bf16[128,112,128]{2,1,0:T(8,128)(2,1)} %slice.56) | data formatting | bytes 7340032 | tf_op jit(solution)/shard_map/reshape | solution.py:89
  358.2 52.0 %all-to-all-done.1 = bf16[128,176,128]{2,1,0:T(8,128)(2,1)} async-done(((bf16[128,176,128]{2,1,0:T(8,128)(2,1)}), bf16[128,176,128]{2,1,0:T(8,128)(2,1)}, u32[]{:S(2)}, u32[]{:S(2)}) %all-to-all-start.1) | async-done | bytes 5767200 | tf_op jit(solution)/shard_map/all_to_all | solution.py:29
  410.2 5.3 %slice.51 = bf16[128,168,128]{2,1,0:T(8,128)(2,1)} slice(bf16[128,176,128]{2,1,0:T(8,128)(2,1)} %all-to-all-done.1), slice={[0:128], [0:168], [0:128]} | slice | bytes 11010048 | tf_op jit(solution)/shard_map/slice | solution.py:89
  415.5 10.6 %reshape.153 = bf16[768,3584,1]{1,0,2:T(8,128)(2,1)} reshape(bf16[128,168,128]{2,1,0:T(8,128)(2,1)} %slice.51) | data formatting | bytes 11010048 | tf_op jit(solution)/shard_map/reshape | solution.py:89
  426.2 1.1 slice_reduce_fusion.1
  427.3 0.1 reshape.154
  427.5 3.6 fusion.29
  431.1 0.1 copy.27
  431.1 0.0 copy-start
  431.1 4.3 fusion.43
  435.5 0.6 fusion.51
  436.1 0.0 copy-done
  436.1 2.1 fusion.37
  (8 shorter events, 0.1 us)
Async XLA Ops:
  13.3 98.9 %all-to-all-start.2 = ((bf16[128,224,128]{2,1,0:T(8,128)(2,1)}), bf16[128,224,128]{2,1,0:T(8,128)(2,1)}, u32[]{:S(2)}, u32[]{:S(2)}) async-start(bf16[128,224,128]{2,1,0:T(8,128)(2,1)} %bitcast.45), calls=%async_computation.2 | async-start | bytes 14680064 | tf_op jit(solution)/shard_map/all_to_all | solution.py:29
  112.2 137.8 %all-to-all-start = ((bf16[128,336,128]{2,1,0:T(8,128)(2,1)}), bf16[128,336,128]{2,1,0:T(8,128)(2,1)}, u32[]{:S(2)}, u32[]{:S(2)}) async-start(bf16[128,336,128]{2,1,0:T(8,128)(2,1)} %bitcast.44), calls=%async_computation | async-start | bytes 22020096 | tf_op jit(solution)/shard_map/all_to_all | solution.py:29
  132.4 7.4 %copy-start.2 = (bf16[512,7168]{1,0:T(8,128)(2,1)S(1)}, bf16[512,7168]{1,0:T(8,128)(2,1)}, u32[]{:S(2)}) copy-start(bf16[512,7168]{1,0:T(8,128)(2,1)} %reshape.120) | copy-start | bytes 22020100
  250.0 80.7 %all-to-all-start.3 = ((bf16[128,120,128]{2,1,0:T(8,128)(2,1)}), bf16[128,120,128]{2,1,0:T(8,128)(2,1)}, u32[]{:S(2)}, u32[]{:S(2)}) async-start(bf16[128,120,128]{2,1,0:T(8,128)(2,1)} %fusion.24), calls=%async_computation.3 | async-start | bytes 7864320 | tf_op jit(solution)/shard_map/all_to_all | solution.py:29
  284.0 9.8 %copy-start.1 = (bf16[768,7168]{1,0:T(8,128)(2,1)S(1)}, bf16[768,7168]{1,0:T(8,128)(2,1)}, u32[]{:S(2)}) copy-start(bf16[768,7168]{1,0:T(8,128)(2,1)} %reshape.116) | copy-start | bytes 33030148
  330.7 10.2 %copy-start.3 = (bf16[128,8]{0,1:T(8,128)(2,1)S(1)}, bf16[128,8]{0,1:T(8,128)(2,1)}, u32[]{:S(2)}) copy-start(bf16[128,8]{0,1:T(8,128)(2,1)} %param.9) | copy-start | bytes 6148
  330.7 79.5 %all-to-all-start.1 = ((bf16[128,176,128]{2,1,0:T(8,128)(2,1)}), bf16[128,176,128]{2,1,0:T(8,128)(2,1)}, u32[]{:S(2)}, u32[]{:S(2)}) async-start(bf16[128,176,128]{2,1,0:T(8,128)(2,1)} %fusion.20), calls=%async_computation.1 | async-start | bytes 11534336 | tf_op jit(solution)/shard_map/all_to_all | solution.py:29
  431.1 4.9 %copy-start = (bf16[512,3584,1]{1,0,2:T(8,128)(2,1)S(1)}, bf16[512,3584,1]{1,0,2:T(8,128)(2,1)}, u32[]{:S(2)}) copy-start(bf16[512,3584,1]{1,0,2:T(8,128)(2,1)} %reshape.156) | copy-start | bytes 11010052

commit v6 on v4

--- a/solution.py
+++ b/solution.py
@@ -28,7 +28,7 @@
 
 
 def exchange(x):
-    return lax.all_to_all(x, ("group", "dev"), split_axis=0, concat_axis=0, tiled=True)
+    return lax.all_to_all(x, ("dev", "group"), split_axis=0, concat_axis=0, tiled=True)
 
 
 def side_block(values, rows):
@@ -61,8 +61,11 @@
         .at[target]
         .set(jnp.arange(entries, dtype=jnp.int32))
     ).reshape(experts, capacity)
+    position = jnp.arange(experts, dtype=jnp.int32)
+    slot_table = slot_table[(position % groups) * per_group + position // groups]
     slot_flat = slot_ids.reshape(-1)
-    expert_flat = expert_ids.reshape(-1)
+    expert_flat = (expert_ids % per_group) * groups + expert_ids // per_group
+    expert_flat = expert_flat.reshape(-1)
     same_group = group_of == group_of[:, :1]
     selector = jnp.stack([same_group, jnp.logical_not(same_group)], axis=1)
     pick = jnp.where(selector, gate_weights.reshape(rows_dev, 1, TOPK), jnp.bfloat16(0))

time: 412 us -> 416 us (level)
  waiting for transfers between devices: 196 us -> 205 us
  starting transfers between devices: 42.5 us -> 36.8 us
    all_to_all x4, waiting for transfers between devices: 196 us -> 205 us  [exchange(): lax.all_to_all(x, ('dev', 'group'), split_axis=0, concat_axis=0, tiled=True)]
    all_to_all x4, starting transfers between devices: 42.5 us -> 36.8 us  [exchange(): lax.all_to_all(x, ('dev', 'group'), split_axis=0, concat_axis=0, tiled=True)]
where the time goes in v6:
time: 416 us; the launch traced here: 414 us
  waiting for transfers between devices  205 us (49%)
  local copies, waits for them, and re-layouts  85.6 us (21%)
  matrix products  73.1 us (18%)
  starting transfers between devices  36.8 us (9%)
  other arithmetic  13 us (3%)
    all_to_all x4, waiting for transfers between devices, exchange(): lax.all_to_all(x, ('dev', 'group'), split_axis=0, concat_axis=0, tiled=True)  205 us
    all_to_all x4, starting transfers between devices, exchange(): lax.all_to_all(x, ('dev', 'group'), split_axis=0, concat_axis=0, tiled=True)  36.8 us
    reshape x2, local copies, waits for them, and re-layouts, layer(): data = arrived.reshape(part_rows, both)  27.6 us
    dot_general x2, matrix products, expert_rows(): lax.dot_general(inner_grad, up_matrix, (((1,), (1,)), ((), ())), preferre...  20.2 us
    reshape x2, local copies, waits for them, and re-layouts, layer(): contrib.reshape(experts, back_blocks, LANES)  19.2 us
    reshape x2, local copies, waits for them, and re-layouts, layer(): rows_back = returned[:, :back_blocks, :].reshape(part_rows, features)  18.1 us
    dot_general x2, matrix products, expert_rows(): raised = jnp.dot(token_rows, up_matrix, preferred_element_type=jnp.float32)  17.3 us
    dot_general x2, matrix products, expert_rows(): lax.dot_general(grad_rows, down_matrix, (((1,), (1,)), ((), ())), preferr...  15.3 us
  transfers between devices with their start and end apart: 4, of which 4 were waited for; matrix products, arithmetic and copies ran while one was open for 33% of the time, Pallas kernels for 0%

profile of v6, /device:TPU:1, one launch (start us, length us, event | category | flops | bytes accessed | tf_op | source)
XLA Modules:
  0.0 414.3 jit_solution(7904949870932983924)
XLA Ops:
  0.6 0.7 add_select_fusion.6
  1.4 0.1 copy.12
  1.5 0.1 reshape.179
  1.6 4.3 %scatter_custom_fusion = s32[1280]{0:T(1024)S(1)} fusion(s32[1024]{0:T(1024)S(1)} %bitcast.53, s32[1024]{0:T(1024)S(1)} %iota.12, s32[]{:T(128)} %constant.108.clone.1), kind=kCustom, calls=%fused_computation.92 | custom fusion | bytes 5124 | tf_op jit(solution)/shard_map/scatter | solution.py:62
  5.9 0.1 reshape.180
  6.1 0.6 gather_fusion
  6.7 0.1 compare_select_fusion
  6.8 0.2 reshape.199
  7.1 1.6 fusion.33
  8.7 0.4 copy.21
  9.1 0.3 slice.60
  9.4 5.2 %gather_fusion.1 = bf16[640,56,128]{2,1,0:T(8,128)(2,1)} fusion(bf16[129,56,128]{2,1,0:T(8,128)(2,1)S(1)} %slice.60, s32[1024]{0:T(1024)S(1)} %pad_clamp_fusion.1), kind=kCustom, calls=%fused_computation.1 | custom fusion | bytes 18352640 | tf_op jit(solution)/shard_map/gather | solution.py:76
  14.7 11.9 %all-to-all-start = ((bf16[128,280,128]{2,1,0:T(8,128)(2,1)}), bf16[128,280,128]{2,1,0:T(8,128)(2,1)}, u32[]{:S(2)}, u32[]{:S(2)}) async-start(bf16[128,280,128]{2,1,0:T(8,128)(2,1)} %bitcast.49), calls=%async_computation | async-start | bytes 18350080 | tf_op jit(solution)/shard_map/all_to_all | solution.py:31
  26.6 0.2 reshape.207
  26.8 5.2 %gather_fusion.2 = bf16[640,56,128]{2,1,0:T(8,128)(2,1)} fusion(bf16[129,56,128]{2,1,0:T(8,128)(2,1)S(1)} %slice.60, s32[1024]{0:T(1024)S(1)} %pad_clamp_fusion), kind=kCustom, calls=%fused_computation.2 | custom fusion | bytes 18352640 | tf_op jit(solution)/shard_map/gather | solution.py:76
  32.0 107.3 %all-to-all-done = bf16[128,280,128]{2,1,0:T(8,128)(2,1)} async-done(((bf16[128,280,128]{2,1,0:T(8,128)(2,1)}), bf16[128,280,128]{2,1,0:T(8,128)(2,1)}, u32[]{:S(2)}, u32[]{:S(2)}) %all-to-all-start) | async-done | bytes 9175072 | tf_op jit(solution)/shard_map/all_to_all | solution.py:31
  139.3 8.4 %all-to-all-start.2 = ((bf16[128,280,128]{2,1,0:T(8,128)(2,1)}), bf16[128,280,128]{2,1,0:T(8,128)(2,1)}, u32[]{:S(2)}, u32[]{:S(2)}) async-start(bf16[128,280,128]{2,1,0:T(8,128)(2,1)} %bitcast.48), calls=%async_computation.2 | async-start | bytes 18350080 | tf_op jit(solution)/shard_map/all_to_all | solution.py:31
  147.8 13.8 %reshape.182 = bf16[640,7168]{1,0:T(8,128)(2,1)} reshape(bf16[128,280,128]{2,1,0:T(8,128)(2,1)} %all-to-all-done) | data formatting | bytes 18350080 | tf_op jit(solution)/shard_map/reshape | solution.py:78
  161.6 0.0 copy-start
  161.6 8.6 %fusion.8 = f32[640,1024]{1,0:T(8,128)S(1)} fusion(bf16[1,3584,1024]{2,1,0:T(8,128)(2,1)} %param.12, bf16[640,7168]{1,0:T(8,128)(2,1)} %reshape.182), kind=kOutput, calls=%fused_computation.13 | convolution fusion | flops 4697620480 | bytes 14548992 | tf_op jit(solution)/shard_map/dot_general | solution.py:18
  170.2 0.0 copy-done
  170.2 7.6 %multiply_reduce_fusion.1 = (bf16[640]{0:T(1024)(128)(2,1)S(1)}, f32[640,1024]{1,0:T(8,128)S(1)}) fusion(f32[640,1024]{1,0:T(8,128)S(1)} %fusion.8, bf16[1,1024,3584]{2,1,0:T(8,128)(2,1)} %param.13, bf16[640,7168]{1,0:T(8,128)(2,1)S(1)} %copy-done), kind=kOutput, calls=%fused_computation.38 | convolution fusion | flops 4701552128 | bytes 17171712 | tf_op jit(solution)/shard_map/dot_general | solution.py:19
  177.9 10.1 %fusion.14 = bf16[640,3584]{1,0:T(8,128)(2,1)} fusion(bf16[1,3584,1024]{2,1,0:T(8,128)(2,1)} %param.12, f32[640,1024]{1,0:T(8,128)S(1)} %get-tuple-element.15, f32[640,1024]{1,0:T(8,128)S(1)} %fusion.8), kind=kOutput, calls=%fused_computation.19 | convolution fusion | flops 4705812480 | bytes 17170432 | tf_op jit(solution)/shard_map/dot_general | solution.py:24
  188.0 9.6 %reshape.183 = bf16[128,140,128]{2,1,0:T(8,128)(2,1)} reshape(bf16[640,3584]{1,0:T(8,128)(2,1)} %fusion.14) | data formatting | bytes 9175040 | tf_op jit(solution)/shard_map/reshape | solution.py:85
  197.6 0.2 convert_element_type.69
  197.9 5.0 %fusion.21 = bf16[128,144,128]{2,1,0:T(8,128)(2,1)} fusion(bf16[128,1,5]{2,1,0:T(2,128)(2,1)S(1)} %convert_element_type.69, bf16[128,140,128]{2,1,0:T(8,128)(2,1)} %reshape.183), kind=kLoop, calls=%fused_computation.23 | loop fusion | flops 14155776 | bytes 9307392 | tf_op jit(solution)/shard_map/concatenate | solution.py:83
  202.9 57.1 %all-to-all-done.2 = bf16[128,280,128]{2,1,0:T(8,128)(2,1)} async-done(((bf16[128,280,128]{2,1,0:T(8,128)(2,1)}), bf16[128,280,128]{2,1,0:T(8,128)(2,1)}, u32[]{:S(2)}, u32[]{:S(2)}) %all-to-all-start.2) | async-done | bytes 9175072 | tf_op jit(solution)/shard_map/all_to_all | solution.py:31
  259.9 9.8 %all-to-all-start.1 = ((bf16[128,144,128]{2,1,0:T(8,128)(2,1)}), bf16[128,144,128]{2,1,0:T(8,128)(2,1)}, u32[]{:S(2)}, u32[]{:S(2)}) async-start(bf16[128,144,128]{2,1,0:T(8,128)(2,1)} %fusion.21), calls=%async_computation.1 | async-start | bytes 9437184 | tf_op jit(solution)/shard_map/all_to_all | solution.py:31
  269.8 13.8 %reshape.186 = bf16[640,7168]{1,0:T(8,128)(2,1)} reshape(bf16[128,280,128]{2,1,0:T(8,128)(2,1)} %all-to-all-done.2) | data formatting | bytes 18350080 | tf_op jit(solution)/shard_map/reshape | solution.py:78
  283.6 0.0 copy-start.1
  283.6 8.6 %fusion.4 = f32[640,1024]{1,0:T(8,128)S(1)} fusion(bf16[1,3584,1024]{2,1,0:T(8,128)(2,1)} %param.12, bf16[640,7168]{1,0:T(8,128)(2,1)} %reshape.186), kind=kOutput, calls=%fused_computation.9 | convolution fusion | flops 4697620480 | bytes 14548992 | tf_op jit(solution)/shard_map/dot_general | solution.py:18
  292.2 0.0 copy-done.1
  292.2 7.6 %multiply_reduce_fusion = (bf16[640]{0:T(1024)(128)(2,1)S(1)}, f32[640,1024]{1,0:T(8,128)S(1)}) fusion(f32[640,1024]{1,0:T(8,128)S(1)} %fusion.4, bf16[1,1024,3584]{2,1,0:T(8,128)(2,1)} %param.13, bf16[640,7168]{1,0:T(8,128)(2,1)S(1)} %copy-done.1), kind=kOutput, calls=%fused_computation.32 | convolution fusion | flops 4701552128 | bytes 17171712 | tf_op jit(solution)/shard_map/dot_general | solution.py:19
  299.9 10.0 %fusion.17 = bf16[640,3584]{1,0:T(8,128)(2,1)} fusion(bf16[1,3584,1024]{2,1,0:T(8,128)(2,1)} %param.12, f32[640,1024]{1,0:T(8,128)S(1)} %get-tuple-element.17, f32[640,1024]{1,0:T(8,128)S(1)} %fusion.4), kind=kOutput, calls=%fused_computation.20 | convolution fusion | flops 4705812480 | bytes 17170432 | tf_op jit(solution)/shard_map/dot_general | solution.py:24
  309.9 9.7 %reshape.187 = bf16[128,140,128]{2,1,0:T(8,128)(2,1)} reshape(bf16[640,3584]{1,0:T(8,128)(2,1)} %fusion.17) | data formatting | bytes 9175040 | tf_op jit(solution)/shard_map/reshape | solution.py:85
  319.5 0.2 convert_element_type.70
  319.8 4.9 %fusion.22 = bf16[128,144,128]{2,1,0:T(8,128)(2,1)} fusion(bf16[128,1,5]{2,1,0:T(2,128)(2,1)S(1)} %convert_element_type.70, bf16[128,140,128]{2,1,0:T(8,128)(2,1)} %reshape.187), kind=kLoop, calls=%fused_computation.24 | loop fusion | flops 14155776 | bytes 9307392 | tf_op jit(solution)/shard_map/concatenate | solution.py:83
  324.7 0.0 copy-start.2
  324.7 0.0 copy-start.3
  324.7 3.5 all-to-all-done.1
  328.3 6.7 %all-to-all-start.3 = ((bf16[128,144,128]{2,1,0:T(8,128)(2,1)}), bf16[128,144,128]{2,1,0:T(8,128)(2,1)}, u32[]{:S(2)}, u32[]{:S(2)}) async-start(bf16[128,144,128]{2,1,0:T(8,128)(2,1)} %fusion.22), calls=%async_computation.3 | async-start | bytes 9437184 | tf_op jit(solution)/shard_map/all_to_all | solution.py:31
  334.9 0.0 copy-done.2
  335.0 0.0 copy-done.3
  335.0 0.1 copy.16
  335.1 0.1 copy.11
  335.2 0.1 copy.14
  335.3 0.6 fusion.32
  336.0 0.6 fusion.30
  336.6 9.1 %reshape.227 = bf16[640,3584,1]{1,0,2:T(8,128)(2,1)} reshape(bf16[128,140,128]{2,1,0:T(8,128)(2,1)} %bitcast.46) | data formatting | bytes 9175040 | tf_op jit(solution)/shard_map/reshape | solution.py:91
  345.7 1.2 slice_reduce_fusion.1
  346.9 0.2 reshape.228
  347.1 3.6 fusion.31
  350.7 0.1 copy.18
  350.8 5.7 %fusion.41 = f32[128,2,3584]{2,0,1:T(8,128)} fusion(bf16[640,3584,1]{1,0,2:T(8,128)(2,1)} %reshape.227, bf16[128,2,640]{2,1,0:T(2,128)(2,1)S(1)} %fusion.32), kind=kOutput, calls=%fused_computation.54 | convolution fusion | flops 1174405120 | bytes 8585216 | tf_op jit(solution)/shard_map/tpj,jd->tpd/dot_general | solution.py:101
  356.5 37.0 %all-to-all-done.3 = bf16[128,144,128]{2,1,0:T(8,128)(2,1)} async-done(((bf16[128,144,128]{2,1,0:T(8,128)(2,1)}), bf16[128,144,128]{2,1,0:T(8,128)(2,1)}, u32[]{:S(2)}, u32[]{:S(2)}) %all-to-all-start.3) | async-done | bytes 4718624 | tf_op jit(solution)/shard_map/all_to_all | solution.py:31
  393.4 1.2 slice_reduce_fusion
  394.6 0.2 reshape.231
  394.8 3.6 fusion.29
  398.4 0.1 copy.20
  398.5 9.1 %reshape.230 = bf16[640,3584,1]{1,0,2:T(8,128)(2,1)} reshape(bf16[128,140,128]{2,1,0:T(8,128)(2,1)} %bitcast.47) | data formatting | bytes 9175040 | tf_op jit(solution)/shard_map/reshape | solution.py:91
  407.6 0.6 fusion.50
  408.2 6.2 %fusion.34 = bf16[128,3584]{1,0:T(8,128)(2,1)} fusion(f32[128,2,3584]{2,0,1:T(8,128)} %fusion.41, bf16[640,3584,1]{1,0,2:T(8,128)(2,1)} %reshape.230, bf16[128,2,640]{2,1,0:T(2,128)(2,1)S(1)} %fusion.30), kind=kOutput, calls=%fused_computation.45 | convolution fusion | flops 1176698880 | bytes 9502720 | tf_op jit(solution)/shard_map/tpj,jd->tpd/dot_general | solution.py:101
  (9 shorter events, 0.1 us)
Async XLA Ops:
  14.7 124.6 %all-to-all-start = ((bf16[128,280,128]{2,1,0:T(8,128)(2,1)}), bf16[128,280,128]{2,1,0:T(8,128)(2,1)}, u32[]{:S(2)}, u32[]{:S(2)}) async-start(bf16[128,280,128]{2,1,0:T(8,128)(2,1)} %bitcast.49), calls=%async_computation | async-start | bytes 18350080 | tf_op jit(solution)/shard_map/all_to_all | solution.py:31
  139.3 120.6 %all-to-all-start.2 = ((bf16[128,280,128]{2,1,0:T(8,128)(2,1)}), bf16[128,280,128]{2,1,0:T(8,128)(2,1)}, u32[]{:S(2)}, u32[]{:S(2)}) async-start(bf16[128,280,128]{2,1,0:T(8,128)(2,1)} %bitcast.48), calls=%async_computation.2 | async-start | bytes 18350080 | tf_op jit(solution)/shard_map/all_to_all | solution.py:31
  161.6 8.6 %copy-start = (bf16[640,7168]{1,0:T(8,128)(2,1)S(1)}, bf16[640,7168]{1,0:T(8,128)(2,1)}, u32[]{:S(2)}) copy-start(bf16[640,7168]{1,0:T(8,128)(2,1)} %reshape.182) | copy-start | bytes 27525124
  259.9 68.3 %all-to-all-start.1 = ((bf16[128,144,128]{2,1,0:T(8,128)(2,1)}), bf16[128,144,128]{2,1,0:T(8,128)(2,1)}, u32[]{:S(2)}, u32[]{:S(2)}) async-start(bf16[128,144,128]{2,1,0:T(8,128)(2,1)} %fusion.21), calls=%async_computation.1 | async-start | bytes 9437184 | tf_op jit(solution)/shard_map/all_to_all | solution.py:31
  283.6 8.6 %copy-start.1 = (bf16[640,7168]{1,0:T(8,128)(2,1)S(1)}, bf16[640,7168]{1,0:T(8,128)(2,1)}, u32[]{:S(2)}) copy-start(bf16[640,7168]{1,0:T(8,128)(2,1)} %reshape.186) | copy-start | bytes 27525124
  324.7 10.2 %copy-start.2 = (s32[128,8]{0,1:T(8,128)S(1)}, s32[128,8]{0,1:T(8,128)}, u32[]{:S(2)}) copy-start(s32[128,8]{0,1:T(8,128)} %param.10) | copy-start | bytes 12292
  324.7 10.3 %copy-start.3 = (bf16[128,8]{0,1:T(8,128)(2,1)S(1)}, bf16[128,8]{0,1:T(8,128)(2,1)}, u32[]{:S(2)}) copy-start(bf16[128,8]{0,1:T(8,128)(2,1)} %param.9) | copy-start | bytes 6148
  328.3 65.2 %all-to-all-start.3 = ((bf16[128,144,128]{2,1,0:T(8,128)(2,1)}), bf16[128,144,128]{2,1,0:T(8,128)(2,1)}, u32[]{:S(2)}, u32[]{:S(2)}) async-start(bf16[128,144,128]{2,1,0:T(8,128)(2,1)} %fusion.22), calls=%async_computation.3 | async-start | bytes 9437184 | tf_op jit(solution)/shard_map/all_to_all | solution.py:31

commit v7 on v4

--- a/solution.py
+++ b/solution.py
@@ -52,14 +52,14 @@
     blocks = both // LANES
     part = capacity // CHUNKS
     part_rows = experts * part
-    joined = jnp.concatenate(
-        [jnp.concatenate([tokens, out_grad], axis=1), jnp.zeros((1, both), jnp.bfloat16)]
-    ).reshape(rows_dev + 1, blocks, LANES)
+    pair = jnp.concatenate([tokens, out_grad], axis=1).reshape(rows_dev, blocks, LANES)
     target = (expert_ids * capacity + slot_ids).reshape(-1)
-    slot_table = (
-        jnp.full((slots_all,), entries, jnp.int32)
-        .at[target]
-        .set(jnp.arange(entries, dtype=jnp.int32))
+    entry = jnp.arange(entries, dtype=jnp.int32)
+    slot_table = jnp.min(
+        jnp.where(
+            target[None, :] == jnp.arange(slots_all, dtype=jnp.int32)[:, None], entry[None, :], entries
+        ),
+        axis=1,
     ).reshape(experts, capacity)
     slot_flat = slot_ids.reshape(-1)
     expert_flat = expert_ids.reshape(-1)
@@ -70,7 +70,10 @@
     gate_sum = None
     for c in range(CHUNKS):
         table = slot_table[:, c * part:(c + 1) * part]
-        sent = joined[table // TOPK].reshape(experts, part * blocks, LANES)
+        anchor = table // TOPK
+        rows = pair[jnp.minimum(anchor, rows_dev - 1)]
+        sent = jnp.where((anchor < rows_dev)[:, :, None, None], rows.reshape(experts, part, blocks, LANES), 0)
+        sent = sent.astype(jnp.bfloat16).reshape(experts, part * blocks, LANES)
         arrived = exchange(sent)
         data = arrived.reshape(part_rows, both)
         contrib, gate_rows = expert_rows(

time: 412 us -> 418 us (1.015)
  other arithmetic: 13 us -> 31.6 us
  waiting for transfers between devices: 196 us -> 186 us
    select_n x2 -> x3, other arithmetic: 0.14 us -> 17.9 us  [the longest x2 17.7 us: layer(): jnp.where((anchor < rows_dev)[:, :, None, None], rows.reshape(experts, pa...]
    all_to_all x4, waiting for transfers between devices: 196 us -> 186 us  [exchange(): lax.all_to_all(x, ('group', 'dev'), split_axis=0, concat_axis=0, tiled=True)]
    scatter x1 -> x0, local copies, waits for them, and re-layouts: 4.32 us -> none  [layer(): slot_table = jnp.full((slots_all,), entries, jnp.int32).at[target].set(jn...]
  transfers between devices with their start and end apart: 4 -> 4, of which waited for: 4 -> 4; matrix products, arithmetic and copies ran while one was open for 33% -> 35% of each run, Pallas kernels for 0% -> 0%
where the time goes in v7:
time: 418 us; the launch traced here: 415 us
  waiting for transfers between devices  186 us (44%)
  local copies, waits for them, and re-layouts  80.9 us (19%)
  matrix products  73.1 us (17%)
  starting transfers between devices  42.5 us (10%)
  other arithmetic  31.6 us (8%)
    all_to_all x4, waiting for transfers between devices, exchange(): lax.all_to_all(x, ('group', 'dev'), split_axis=0, concat_axis=0, tiled=True)  186 us
    all_to_all x4, starting transfers between devices, exchange(): lax.all_to_all(x, ('group', 'dev'), split_axis=0, concat_axis=0, tiled=True)  42.5 us
    reshape x2, local copies, waits for them, and re-layouts, layer(): data = arrived.reshape(part_rows, both)  27.7 us
    dot_general x2, matrix products, expert_rows(): lax.dot_general(inner_grad, up_matrix, (((1,), (1,)), ((), ())), preferre...  20.2 us
    reshape x2, local copies, waits for them, and re-layouts, layer(): contrib.reshape(experts, back_blocks, LANES)  19.3 us
    reshape x2, local copies, waits for them, and re-layouts, layer(): rows_back = returned[:, :back_blocks, :].reshape(part_rows, features)  18.2 us
    select_n x2, other arithmetic, layer(): jnp.where((anchor < rows_dev)[:, :, None, None], rows.reshape(experts, pa...  17.7 us
    dot_general x2, matrix products, expert_rows(): raised = jnp.dot(token_rows, up_matrix, preferred_element_type=jnp.float32)  17.3 us
  transfers between devices with their start and end apart: 4, of which 4 were waited for; matrix products, arithmetic and copies ran while one was open for 35% of the time, Pallas kernels for 0%

profile of v7, /device:TPU:1, one launch (start us, length us, event | category | flops | bytes accessed | tf_op | source)
XLA Modules:
  0.0 415.5 jit_solution(12460028771239569200)
XLA Ops:
  0.6 0.7 add_select_fusion.5
  1.3 0.1 copy.22
  1.5 0.1 eq.70
  1.5 0.8 select_reduce_fusion
  2.3 0.1 reshape.86
  2.5 0.1 compare_select_fusion
  2.6 0.1 broadcast_compare_fusion
  2.7 0.2 reshape.96
  3.0 1.6 maximum_bitcast_fusion
  4.6 0.4 copy.35
  5.0 0.1 copy.23
  5.1 0.2 copy.24
  5.3 5.2 %gather_fusion = bf16[640,56,128]{2,1,0:T(8,128)(2,1)} fusion(bf16[128,56,128]{2,1,0:T(8,128)(2,1)S(1)} %bitcast.51, s32[1024]{0:T(1024)S(1)} %pad_clamp_fusion.1), kind=kCustom, calls=%fused_computation | custom fusion | bytes 18352640 | tf_op jit(solution)/shard_map/gather | solution.py:74
  10.5 8.9 %bitcast_select_fusion.1 = bf16[128,280,128]{2,1,0:T(8,128)(2,1)} fusion(pred[128,280]{1,0:T(8,128)(4,1)S(1)} %copy.24, bf16[128,280,128]{2,1,0:T(8,128)(2,1)} %bitcast.54), kind=kLoop, calls=%fused_computation.6 | loop fusion | flops 4587520 | bytes 18385920 | tf_op jit(solution)/shard_map/jit(_where)/select_n | solution.py:75
  19.4 11.9 %all-to-all-start = ((bf16[128,280,128]{2,1,0:T(8,128)(2,1)}), bf16[128,280,128]{2,1,0:T(8,128)(2,1)}, u32[]{:S(2)}, u32[]{:S(2)}) async-start(bf16[128,280,128]{2,1,0:T(8,128)(2,1)} %bitcast_select_fusion.1), calls=%async_computation | async-start | bytes 18350080 | tf_op jit(solution)/shard_map/all_to_all | solution.py:31
  31.3 0.2 reshape.104
  31.5 5.2 %gather_fusion.1 = bf16[640,56,128]{2,1,0:T(8,128)(2,1)} fusion(bf16[128,56,128]{2,1,0:T(8,128)(2,1)S(1)} %bitcast.52, s32[1024]{0:T(1024)S(1)} %pad_clamp_fusion), kind=kCustom, calls=%fused_computation.1 | custom fusion | bytes 18352640 | tf_op jit(solution)/shard_map/gather | solution.py:74
  36.7 0.1 copy.29
  36.8 0.2 copy.30
  37.0 8.9 %bitcast_select_fusion = bf16[128,280,128]{2,1,0:T(8,128)(2,1)} fusion(pred[128,280]{1,0:T(8,128)(4,1)S(1)} %copy.30, bf16[128,280,128]{2,1,0:T(8,128)(2,1)} %bitcast.53), kind=kLoop, calls=%fused_computation.5 | loop fusion | flops 4587520 | bytes 18385920 | tf_op jit(solution)/shard_map/jit(_where)/select_n | solution.py:75
  45.8 93.5 %all-to-all-done = bf16[128,280,128]{2,1,0:T(8,128)(2,1)} async-done(((bf16[128,280,128]{2,1,0:T(8,128)(2,1)}), bf16[128,280,128]{2,1,0:T(8,128)(2,1)}, u32[]{:S(2)}, u32[]{:S(2)}) %all-to-all-start) | async-done | bytes 9175072 | tf_op jit(solution)/shard_map/all_to_all | solution.py:31
  139.3 11.9 %all-to-all-start.2 = ((bf16[128,280,128]{2,1,0:T(8,128)(2,1)}), bf16[128,280,128]{2,1,0:T(8,128)(2,1)}, u32[]{:S(2)}, u32[]{:S(2)}) async-start(bf16[128,280,128]{2,1,0:T(8,128)(2,1)} %bitcast_select_fusion), calls=%async_computation.2 | async-start | bytes 18350080 | tf_op jit(solution)/shard_map/all_to_all | solution.py:31
  151.3 13.9 %reshape.88 = bf16[640,7168]{1,0:T(8,128)(2,1)} reshape(bf16[128,280,128]{2,1,0:T(8,128)(2,1)} %all-to-all-done) | data formatting | bytes 18350080 | tf_op jit(solution)/shard_map/reshape | solution.py:78
  165.1 0.0 copy-start
  165.1 8.6 %fusion.8 = f32[640,1024]{1,0:T(8,128)S(1)} fusion(bf16[1,3584,1024]{2,1,0:T(8,128)(2,1)} %param.12, bf16[640,7168]{1,0:T(8,128)(2,1)} %reshape.88), kind=kOutput, calls=%fused_computation.13 | convolution fusion | flops 4697620480 | bytes 14548992 | tf_op jit(solution)/shard_map/dot_general | solution.py:18
  173.8 0.0 copy-done
  173.8 7.6 %multiply_reduce_fusion.1 = (bf16[640]{0:T(1024)(128)(2,1)S(1)}, f32[640,1024]{1,0:T(8,128)S(1)}) fusion(f32[640,1024]{1,0:T(8,128)S(1)} %fusion.8, bf16[1,1024,3584]{2,1,0:T(8,128)(2,1)} %param.13, bf16[640,7168]{1,0:T(8,128)(2,1)S(1)} %copy-done), kind=kOutput, calls=%fused_computation.37 | convolution fusion | flops 4701552128 | bytes 17171712 | tf_op jit(solution)/shard_map/dot_general | solution.py:19
  181.4 10.1 %fusion.14 = bf16[640,3584]{1,0:T(8,128)(2,1)} fusion(bf16[1,3584,1024]{2,1,0:T(8,128)(2,1)} %param.12, f32[640,1024]{1,0:T(8,128)S(1)} %get-tuple-element.17, f32[640,1024]{1,0:T(8,128)S(1)} %fusion.8), kind=kOutput, calls=%fused_computation.19 | convolution fusion | flops 4705812480 | bytes 17170432 | tf_op jit(solution)/shard_map/dot_general | solution.py:24
  191.6 9.6 %reshape.89 = bf16[128,140,128]{2,1,0:T(8,128)(2,1)} reshape(bf16[640,3584]{1,0:T(8,128)(2,1)} %fusion.14) | data formatting | bytes 9175040 | tf_op jit(solution)/shard_map/reshape | solution.py:85
  201.2 0.2 convert_element_type.72
  201.4 5.0 %fusion.21 = bf16[128,144,128]{2,1,0:T(8,128)(2,1)} fusion(bf16[128,1,5]{2,1,0:T(2,128)(2,1)S(1)} %convert_element_type.72, bf16[128,140,128]{2,1,0:T(8,128)(2,1)} %reshape.89), kind=kLoop, calls=%fused_computation.25 | loop fusion | flops 14155776 | bytes 9307392 | tf_op jit(solution)/shard_map/concatenate | solution.py:83
  206.4 52.9 %all-to-all-done.2 = bf16[128,280,128]{2,1,0:T(8,128)(2,1)} async-done(((bf16[128,280,128]{2,1,0:T(8,128)(2,1)}), bf16[128,280,128]{2,1,0:T(8,128)(2,1)}, u32[]{:S(2)}, u32[]{:S(2)}) %all-to-all-start.2) | async-done | bytes 9175072 | tf_op jit(solution)/shard_map/all_to_all | solution.py:31
  259.3 11.8 %all-to-all-start.1 = ((bf16[128,144,128]{2,1,0:T(8,128)(2,1)}), bf16[128,144,128]{2,1,0:T(8,128)(2,1)}, u32[]{:S(2)}, u32[]{:S(2)}) async-start(bf16[128,144,128]{2,1,0:T(8,128)(2,1)} %fusion.21), calls=%async_computation.1 | async-start | bytes 9437184 | tf_op jit(solution)/shard_map/all_to_all | solution.py:31
  271.2 13.8 %reshape.91 = bf16[640,7168]{1,0:T(8,128)(2,1)} reshape(bf16[128,280,128]{2,1,0:T(8,128)(2,1)} %all-to-all-done.2) | data formatting | bytes 18350080 | tf_op jit(solution)/shard_map/reshape | solution.py:78
  285.0 0.0 copy-start.1
  285.0 8.6 %fusion.4 = f32[640,1024]{1,0:T(8,128)S(1)} fusion(bf16[1,3584,1024]{2,1,0:T(8,128)(2,1)} %param.12, bf16[640,7168]{1,0:T(8,128)(2,1)} %reshape.91), kind=kOutput, calls=%fused_computation.9 | convolution fusion | flops 4697620480 | bytes 14548992 | tf_op jit(solution)/shard_map/dot_general | solution.py:18
  293.6 0.0 copy-done.1
  293.6 7.6 %multiply_reduce_fusion = (bf16[640]{0:T(1024)(128)(2,1)S(1)}, f32[640,1024]{1,0:T(8,128)S(1)}) fusion(f32[640,1024]{1,0:T(8,128)S(1)} %fusion.4, bf16[1,1024,3584]{2,1,0:T(8,128)(2,1)} %param.13, bf16[640,7168]{1,0:T(8,128)(2,1)S(1)} %copy-done.1), kind=kOutput, calls=%fused_computation.31 | convolution fusion | flops 4701552128 | bytes 17171712 | tf_op jit(solution)/shard_map/dot_general | solution.py:19
  301.3 10.0 %fusion.17 = bf16[640,3584]{1,0:T(8,128)(2,1)} fusion(bf16[1,3584,1024]{2,1,0:T(8,128)(2,1)} %param.12, f32[640,1024]{1,0:T(8,128)S(1)} %get-tuple-element.19, f32[640,1024]{1,0:T(8,128)S(1)} %fusion.4), kind=kOutput, calls=%fused_computation.20 | convolution fusion | flops 4705812480 | bytes 17170432 | tf_op jit(solution)/shard_map/dot_general | solution.py:24
  311.3 9.7 %reshape.92 = bf16[128,140,128]{2,1,0:T(8,128)(2,1)} reshape(bf16[640,3584]{1,0:T(8,128)(2,1)} %fusion.17) | data formatting | bytes 9175040 | tf_op jit(solution)/shard_map/reshape | solution.py:85
  321.0 0.2 convert_element_type.73
  321.2 4.9 %fusion.22 = bf16[128,144,128]{2,1,0:T(8,128)(2,1)} fusion(bf16[128,1,5]{2,1,0:T(2,128)(2,1)S(1)} %convert_element_type.73, bf16[128,140,128]{2,1,0:T(8,128)(2,1)} %reshape.92), kind=kLoop, calls=%fused_computation.26 | loop fusion | flops 14155776 | bytes 9307392 | tf_op jit(solution)/shard_map/concatenate | solution.py:83
  326.2 3.3 all-to-all-done.1
  329.4 6.9 %all-to-all-start.3 = ((bf16[128,144,128]{2,1,0:T(8,128)(2,1)}), bf16[128,144,128]{2,1,0:T(8,128)(2,1)}, u32[]{:S(2)}, u32[]{:S(2)}) async-start(bf16[128,144,128]{2,1,0:T(8,128)(2,1)} %fusion.22), calls=%async_computation.3 | async-start | bytes 9437184 | tf_op jit(solution)/shard_map/all_to_all | solution.py:31
  336.3 0.0 copy-done.2
  336.4 0.1 copy.21
  336.5 0.1 copy.20
  336.6 0.1 copy.27
  336.7 0.6 fusion.38
  337.4 0.6 fusion.39
  338.0 9.1 %reshape.116 = bf16[640,3584,1]{1,0,2:T(8,128)(2,1)} reshape(bf16[128,140,128]{2,1,0:T(8,128)(2,1)} %bitcast.49) | data formatting | bytes 9175040 | tf_op jit(solution)/shard_map/reshape | solution.py:91
  347.1 1.2 slice_reduce_fusion.1
  348.3 0.2 reshape.117
  348.5 3.6 fusion.29
  352.1 0.1 copy.33
  352.2 5.7 %fusion.41 = f32[128,2,3584]{2,0,1:T(8,128)} fusion(bf16[640,3584,1]{1,0,2:T(8,128)(2,1)} %reshape.116, bf16[128,2,640]{2,1,0:T(2,128)(2,1)S(1)} %fusion.38), kind=kOutput, calls=%fused_computation.54 | convolution fusion | flops 1174405120 | bytes 8585216 | tf_op jit(solution)/shard_map/tpj,jd->tpd/dot_general | solution.py:101
  357.9 36.7 %all-to-all-done.3 = bf16[128,144,128]{2,1,0:T(8,128)(2,1)} async-done(((bf16[128,144,128]{2,1,0:T(8,128)(2,1)}), bf16[128,144,128]{2,1,0:T(8,128)(2,1)}, u32[]{:S(2)}, u32[]{:S(2)}) %all-to-all-start.3) | async-done | bytes 4718624 | tf_op jit(solution)/shard_map/all_to_all | solution.py:31
  394.6 1.2 slice_reduce_fusion
  395.7 0.2 reshape.120
  396.0 3.6 fusion.27
  399.6 0.1 copy.34
  399.6 9.1 %reshape.119 = bf16[640,3584,1]{1,0,2:T(8,128)(2,1)} reshape(bf16[128,140,128]{2,1,0:T(8,128)(2,1)} %bitcast.50) | data formatting | bytes 9175040 | tf_op jit(solution)/shard_map/reshape | solution.py:91
  408.7 0.6 fusion.48
  409.3 6.2 %fusion.31 = bf16[128,3584]{1,0:T(8,128)(2,1)} fusion(f32[128,2,3584]{2,0,1:T(8,128)} %fusion.41, bf16[640,3584,1]{1,0,2:T(8,128)(2,1)} %reshape.119, bf16[128,2,640]{2,1,0:T(2,128)(2,1)S(1)} %fusion.39), kind=kOutput, calls=%fused_computation.44 | convolution fusion | flops 1176698880 | bytes 9502720 | tf_op jit(solution)/shard_map/tpj,jd->tpd/dot_general | solution.py:101
  (8 shorter events, 0.1 us)
Async XLA Ops:
  19.4 120.0 %all-to-all-start = ((bf16[128,280,128]{2,1,0:T(8,128)(2,1)}), bf16[128,280,128]{2,1,0:T(8,128)(2,1)}, u32[]{:S(2)}, u32[]{:S(2)}) async-start(bf16[128,280,128]{2,1,0:T(8,128)(2,1)} %bitcast_select_fusion.1), calls=%async_computation | async-start | bytes 18350080 | tf_op jit(solution)/shard_map/all_to_all | solution.py:31
  139.3 120.0 %all-to-all-start.2 = ((bf16[128,280,128]{2,1,0:T(8,128)(2,1)}), bf16[128,280,128]{2,1,0:T(8,128)(2,1)}, u32[]{:S(2)}, u32[]{:S(2)}) async-start(bf16[128,280,128]{2,1,0:T(8,128)(2,1)} %bitcast_select_fusion), calls=%async_computation.2 | async-start | bytes 18350080 | tf_op jit(solution)/shard_map/all_to_all | solution.py:31
  165.1 8.6 %copy-start = (bf16[640,7168]{1,0:T(8,128)(2,1)S(1)}, bf16[640,7168]{1,0:T(8,128)(2,1)}, u32[]{:S(2)}) copy-start(bf16[640,7168]{1,0:T(8,128)(2,1)} %reshape.88) | copy-start | bytes 27525124
  259.3 70.1 %all-to-all-start.1 = ((bf16[128,144,128]{2,1,0:T(8,128)(2,1)}), bf16[128,144,128]{2,1,0:T(8,128)(2,1)}, u32[]{:S(2)}, u32[]{:S(2)}) async-start(bf16[128,144,128]{2,1,0:T(8,128)(2,1)} %fusion.21), calls=%async_computation.1 | async-start | bytes 9437184 | tf_op jit(solution)/shard_map/all_to_all | solution.py:31
  285.0 8.6 %copy-start.1 = (bf16[640,7168]{1,0:T(8,128)(2,1)S(1)}, bf16[640,7168]{1,0:T(8,128)(2,1)}, u32[]{:S(2)}) copy-start(bf16[640,7168]{1,0:T(8,128)(2,1)} %reshape.91) | copy-start | bytes 27525124
  326.1 10.2 %copy-start.2 = (bf16[128,8]{0,1:T(8,128)(2,1)S(1)}, bf16[128,8]{0,1:T(8,128)(2,1)}, u32[]{:S(2)}) copy-start(bf16[128,8]{0,1:T(8,128)(2,1)} %param.9) | copy-start | bytes 6148
  329.4 65.1 %all-to-all-start.3 = ((bf16[128,144,128]{2,1,0:T(8,128)(2,1)}), bf16[128,144,128]{2,1,0:T(8,128)(2,1)}, u32[]{:S(2)}, u32[]{:S(2)}) async-start(bf16[128,144,128]{2,1,0:T(8,128)(2,1)} %fusion.22), calls=%async_computation.3 | async-start | bytes 9437184 | tf_op jit(solution)/shard_map/all_to_all | solution.py:31

commit v8 on v7

--- a/solution.py
+++ b/solution.py
@@ -52,7 +52,9 @@
     blocks = both // LANES
     part = capacity // CHUNKS
     part_rows = experts * part
-    pair = jnp.concatenate([tokens, out_grad], axis=1).reshape(rows_dev, blocks, LANES)
+    joined = jnp.concatenate(
+        [jnp.concatenate([tokens, out_grad], axis=1), jnp.zeros((1, both), jnp.bfloat16)]
+    ).reshape(rows_dev + 1, blocks, LANES)
     target = (expert_ids * capacity + slot_ids).reshape(-1)
     entry = jnp.arange(entries, dtype=jnp.int32)
     slot_table = jnp.min(
@@ -70,10 +72,7 @@
     gate_sum = None
     for c in range(CHUNKS):
         table = slot_table[:, c * part:(c + 1) * part]
-        anchor = table // TOPK
-        rows = pair[jnp.minimum(anchor, rows_dev - 1)]
-        sent = jnp.where((anchor < rows_dev)[:, :, None, None], rows.reshape(experts, part, blocks, LANES), 0)
-        sent = sent.astype(jnp.bfloat16).reshape(experts, part * blocks, LANES)
+        sent = joined[table // TOPK].reshape(experts, part * blocks, LANES)
         arrived = exchange(sent)
         data = arrived.reshape(part_rows, both)
         contrib, gate_rows = expert_rows(
@@ -88,8 +87,6 @@
             axis=1,
         )
         returned = exchange(back)
-        rows_back = returned[:, :back_blocks, :].reshape(part_rows, features)
-        gates_back = returned[:, back_blocks, :part].reshape(part_rows)
         in_chunk = slot_flat // part == c
         spot = jnp.where(in_chunk, expert_flat * part + slot_flat - c * part, -1)
         onehot = (
@@ -98,6 +95,9 @@
         chooser = jnp.einsum(
             "tpk,tkj->tpj", pick, onehot, preferred_element_type=jnp.float32
         ).astype(jnp.bfloat16)
+        onehot, chooser = lax.optimization_barrier((onehot, chooser))
+        rows_back = returned[:, :back_blocks, :].reshape(part_rows, features)
+        gates_back = returned[:, back_blocks, :part].reshape(part_rows)
         partial = jnp.einsum("tpj,jd->tpd", chooser, rows_back, preferred_element_type=jnp.float32)
         gate_part = jnp.einsum("tkj,j->tk", onehot, gates_back, preferred_element_type=jnp.float32)
         if c < CHUNKS - 1:

time: 418 us -> 409 us (0.978)
  other arithmetic: 31.6 us -> 14.4 us
  waiting for transfers between devices: 186 us -> 195 us
    select_n x3 -> x1, other arithmetic: 17.9 us -> 0.13 us  [layer(): sent = joined[table // TOPK].reshape(experts, part * blocks, LANES)]
    all_to_all x4, waiting for transfers between devices: 186 us -> 195 us  [exchange(): lax.all_to_all(x, ('group', 'dev'), split_axis=0, concat_axis=0, tiled=True)]
  transfers between devices with their start and end apart: 4 -> 4, of which waited for: 4 -> 4; matrix products, arithmetic and copies ran while one was open for 35% -> 34% of each run, Pallas kernels for 0% -> 0%
where the time goes in v8:
time: 409 us; the launch traced here: 406 us
  waiting for transfers between devices  195 us (48%)
  local copies, waits for them, and re-layouts  80.7 us (20%)
  matrix products  72.9 us (18%)
  starting transfers between devices  42.5 us (10%)
  other arithmetic  14.4 us (4%)
    all_to_all x4, waiting for transfers between devices, exchange(): lax.all_to_all(x, ('group', 'dev'), split_axis=0, concat_axis=0, tiled=True)  195 us
    all_to_all x4, starting transfers between devices, exchange(): lax.all_to_all(x, ('group', 'dev'), split_axis=0, concat_axis=0, tiled=True)  42.5 us
    reshape x2, local copies, waits for them, and re-layouts, layer(): data = arrived.reshape(part_rows, both)  27.7 us
    dot_general x2, matrix products, expert_rows(): lax.dot_general(inner_grad, up_matrix, (((1,), (1,)), ((), ())), preferre...  20.1 us
    reshape x2, local copies, waits for them, and re-layouts, layer(): contrib.reshape(experts, back_blocks, LANES)  19.3 us
    reshape x2, local copies, waits for them, and re-layouts, layer(): rows_back = returned[:, :back_blocks, :].reshape(part_rows, features)  18.2 us
    dot_general x2, matrix products, expert_rows(): raised = jnp.dot(token_rows, up_matrix, preferred_element_type=jnp.float32)  17.3 us
    dot_general x2, matrix products, expert_rows(): lax.dot_general(grad_rows, down_matrix, (((1,), (1,)), ((), ())), preferr...  15.3 us
  transfers between devices with their start and end apart: 4, of which 4 were waited for; matrix products, arithmetic and copies ran while one was open for 34% of the time, Pallas kernels for 0%

profile of v8, /device:TPU:1, one launch (start us, length us, event | category | flops | bytes accessed | tf_op | source)
XLA Modules:
  0.0 406.4 jit_solution(17643156892539746898)
XLA Ops:
  0.6 0.7 add_select_fusion.5
  1.3 0.1 copy.26
  1.5 0.1 eq.70
  1.5 0.8 select_reduce_fusion
  2.3 0.1 reshape.85
  2.5 0.1 compare_select_fusion
  2.6 0.2 reshape.96
  2.8 1.6 fusion.33
  4.5 0.4 copy.35
  4.9 0.3 slice.58
  5.2 5.2 %gather_fusion = bf16[640,56,128]{2,1,0:T(8,128)(2,1)} fusion(bf16[129,56,128]{2,1,0:T(8,128)(2,1)S(1)} %slice.58, s32[1024]{0:T(1024)S(1)} %pad_clamp_fusion.1), kind=kCustom, calls=%fused_computation | custom fusion | bytes 18352640 | tf_op jit(solution)/shard_map/gather | solution.py:75
  10.4 11.9 %all-to-all-start = ((bf16[128,280,128]{2,1,0:T(8,128)(2,1)}), bf16[128,280,128]{2,1,0:T(8,128)(2,1)}, u32[]{:S(2)}, u32[]{:S(2)}) async-start(bf16[128,280,128]{2,1,0:T(8,128)(2,1)} %bitcast.48), calls=%async_computation | async-start | bytes 18350080 | tf_op jit(solution)/shard_map/all_to_all | solution.py:31
  22.3 0.2 reshape.104
  22.5 5.2 %gather_fusion.1 = bf16[640,56,128]{2,1,0:T(8,128)(2,1)} fusion(bf16[129,56,128]{2,1,0:T(8,128)(2,1)S(1)} %slice.58, s32[1024]{0:T(1024)S(1)} %pad_clamp_fusion), kind=kCustom, calls=%fused_computation.1 | custom fusion | bytes 18352640 | tf_op jit(solution)/shard_map/gather | solution.py:75
  27.8 102.6 %all-to-all-done = bf16[128,280,128]{2,1,0:T(8,128)(2,1)} async-done(((bf16[128,280,128]{2,1,0:T(8,128)(2,1)}), bf16[128,280,128]{2,1,0:T(8,128)(2,1)}, u32[]{:S(2)}, u32[]{:S(2)}) %all-to-all-start) | async-done | bytes 9175072 | tf_op jit(solution)/shard_map/all_to_all | solution.py:31
  130.4 11.9 %all-to-all-start.2 = ((bf16[128,280,128]{2,1,0:T(8,128)(2,1)}), bf16[128,280,128]{2,1,0:T(8,128)(2,1)}, u32[]{:S(2)}, u32[]{:S(2)}) async-start(bf16[128,280,128]{2,1,0:T(8,128)(2,1)} %bitcast.47), calls=%async_computation.2 | async-start | bytes 18350080 | tf_op jit(solution)/shard_map/all_to_all | solution.py:31
  142.3 13.9 %reshape.87 = bf16[640,7168]{1,0:T(8,128)(2,1)} reshape(bf16[128,280,128]{2,1,0:T(8,128)(2,1)} %all-to-all-done) | data formatting | bytes 18350080 | tf_op jit(solution)/shard_map/reshape | solution.py:77
  156.2 0.0 copy-start
  156.2 8.6 %fusion.8 = f32[640,1024]{1,0:T(8,128)S(1)} fusion(bf16[1,3584,1024]{2,1,0:T(8,128)(2,1)} %param.12, bf16[640,7168]{1,0:T(8,128)(2,1)} %reshape.87), kind=kOutput, calls=%fused_computation.11 | convolution fusion | flops 4697620480 | bytes 14548992 | tf_op jit(solution)/shard_map/dot_general | solution.py:18
  164.8 0.0 copy-done
  164.8 7.6 %multiply_reduce_fusion.1 = (bf16[640]{0:T(1024)(128)(2,1)S(1)}, f32[640,1024]{1,0:T(8,128)S(1)}) fusion(f32[640,1024]{1,0:T(8,128)S(1)} %fusion.8, bf16[1,1024,3584]{2,1,0:T(8,128)(2,1)} %param.13, bf16[640,7168]{1,0:T(8,128)(2,1)S(1)} %copy-done), kind=kOutput, calls=%fused_computation.38 | convolution fusion | flops 4701552128 | bytes 17171712 | tf_op jit(solution)/shard_map/dot_general | solution.py:19
  172.5 10.1 %fusion.14 = bf16[640,3584]{1,0:T(8,128)(2,1)} fusion(bf16[1,3584,1024]{2,1,0:T(8,128)(2,1)} %param.12, f32[640,1024]{1,0:T(8,128)S(1)} %get-tuple-element.23, f32[640,1024]{1,0:T(8,128)S(1)} %fusion.8), kind=kOutput, calls=%fused_computation.17 | convolution fusion | flops 4705812480 | bytes 17170432 | tf_op jit(solution)/shard_map/dot_general | solution.py:24
  182.6 9.6 %reshape.88 = bf16[128,140,128]{2,1,0:T(8,128)(2,1)} reshape(bf16[640,3584]{1,0:T(8,128)(2,1)} %fusion.14) | data formatting | bytes 9175040 | tf_op jit(solution)/shard_map/reshape | solution.py:84
  192.2 0.2 convert_element_type.75
  192.5 5.0 %fusion.21 = bf16[128,144,128]{2,1,0:T(8,128)(2,1)} fusion(bf16[128,1,5]{2,1,0:T(2,128)(2,1)S(1)} %convert_element_type.75, bf16[128,140,128]{2,1,0:T(8,128)(2,1)} %reshape.88), kind=kLoop, calls=%fused_computation.23 | loop fusion | flops 14155776 | bytes 9307392 | tf_op jit(solution)/shard_map/concatenate | solution.py:82
  197.5 52.9 %all-to-all-done.2 = bf16[128,280,128]{2,1,0:T(8,128)(2,1)} async-done(((bf16[128,280,128]{2,1,0:T(8,128)(2,1)}), bf16[128,280,128]{2,1,0:T(8,128)(2,1)}, u32[]{:S(2)}, u32[]{:S(2)}) %all-to-all-start.2) | async-done | bytes 9175072 | tf_op jit(solution)/shard_map/all_to_all | solution.py:31
  250.4 11.8 %all-to-all-start.1 = ((bf16[128,144,128]{2,1,0:T(8,128)(2,1)}), bf16[128,144,128]{2,1,0:T(8,128)(2,1)}, u32[]{:S(2)}, u32[]{:S(2)}) async-start(bf16[128,144,128]{2,1,0:T(8,128)(2,1)} %fusion.21), calls=%async_computation.1 | async-start | bytes 9437184 | tf_op jit(solution)/shard_map/all_to_all | solution.py:31
  262.2 13.8 %reshape.91 = bf16[640,7168]{1,0:T(8,128)(2,1)} reshape(bf16[128,280,128]{2,1,0:T(8,128)(2,1)} %all-to-all-done.2) | data formatting | bytes 18350080 | tf_op jit(solution)/shard_map/reshape | solution.py:77
  276.0 0.0 copy-start.1
  276.0 8.6 %fusion.4 = f32[640,1024]{1,0:T(8,128)S(1)} fusion(bf16[1,3584,1024]{2,1,0:T(8,128)(2,1)} %param.12, bf16[640,7168]{1,0:T(8,128)(2,1)} %reshape.91), kind=kOutput, calls=%fused_computation.7 | convolution fusion | flops 4697620480 | bytes 14548992 | tf_op jit(solution)/shard_map/dot_general | solution.py:18
  284.7 0.0 copy-done.1
  284.7 7.6 %multiply_reduce_fusion = (bf16[640]{0:T(1024)(128)(2,1)S(1)}, f32[640,1024]{1,0:T(8,128)S(1)}) fusion(f32[640,1024]{1,0:T(8,128)S(1)} %fusion.4, bf16[1,1024,3584]{2,1,0:T(8,128)(2,1)} %param.13, bf16[640,7168]{1,0:T(8,128)(2,1)S(1)} %copy-done.1), kind=kOutput, calls=%fused_computation.32 | convolution fusion | flops 4701552128 | bytes 17171712 | tf_op jit(solution)/shard_map/dot_general | solution.py:19
  292.3 10.0 %fusion.17 = bf16[640,3584]{1,0:T(8,128)(2,1)} fusion(bf16[1,3584,1024]{2,1,0:T(8,128)(2,1)} %param.12, f32[640,1024]{1,0:T(8,128)S(1)} %get-tuple-element.25, f32[640,1024]{1,0:T(8,128)S(1)} %fusion.4), kind=kOutput, calls=%fused_computation.18 | convolution fusion | flops 4705812480 | bytes 17170432 | tf_op jit(solution)/shard_map/dot_general | solution.py:24
  302.3 9.7 %reshape.92 = bf16[128,140,128]{2,1,0:T(8,128)(2,1)} reshape(bf16[640,3584]{1,0:T(8,128)(2,1)} %fusion.17) | data formatting | bytes 9175040 | tf_op jit(solution)/shard_map/reshape | solution.py:84
  312.0 0.2 convert_element_type.76
  312.2 4.9 %fusion.22 = bf16[128,144,128]{2,1,0:T(8,128)(2,1)} fusion(bf16[128,1,5]{2,1,0:T(2,128)(2,1)S(1)} %convert_element_type.76, bf16[128,140,128]{2,1,0:T(8,128)(2,1)} %reshape.92), kind=kLoop, calls=%fused_computation.24 | loop fusion | flops 14155776 | bytes 9307392 | tf_op jit(solution)/shard_map/concatenate | solution.py:82
  317.2 0.0 copy-start.2
  317.2 3.3 all-to-all-done.1
  320.5 6.9 %all-to-all-start.3 = ((bf16[128,144,128]{2,1,0:T(8,128)(2,1)}), bf16[128,144,128]{2,1,0:T(8,128)(2,1)}, u32[]{:S(2)}, u32[]{:S(2)}) async-start(bf16[128,144,128]{2,1,0:T(8,128)(2,1)} %fusion.22), calls=%async_computation.3 | async-start | bytes 9437184 | tf_op jit(solution)/shard_map/all_to_all | solution.py:31
  327.4 0.0 copy-done.2
  327.4 0.1 copy.25
  327.5 0.1 copy.24
  327.6 0.6 fusion.39
  328.3 0.3 fusion.32
  328.6 0.1 copy.29
  328.7 0.6 fusion.40
  329.3 0.3 fusion.30
  329.6 9.1 %reshape.116 = bf16[640,3584,1]{1,0,2:T(8,128)(2,1)} reshape(bf16[128,140,128]{2,1,0:T(8,128)(2,1)} %bitcast.45) | data formatting | bytes 9175040 | tf_op jit(solution)/shard_map/reshape | solution.py:99
  338.7 1.2 slice_reduce_fusion.1
  339.9 0.2 reshape.117
  340.1 3.5 fusion.54
  343.6 0.1 copy.33
  343.7 5.7 %fusion.42 = f32[128,2,3584]{2,0,1:T(8,128)} fusion(bf16[640,3584,1]{1,0,2:T(8,128)(2,1)} %reshape.116, bf16[128,2,640]{2,1,0:T(2,128)(2,1)S(1)} %fusion.39), kind=kOutput, calls=%fused_computation.53 | convolution fusion | flops 1174405120 | bytes 8585216 | tf_op jit(solution)/shard_map/tpj,jd->tpd/dot_general | solution.py:101
  349.4 36.2 %all-to-all-done.3 = bf16[128,144,128]{2,1,0:T(8,128)(2,1)} async-done(((bf16[128,144,128]{2,1,0:T(8,128)(2,1)}), bf16[128,144,128]{2,1,0:T(8,128)(2,1)}, u32[]{:S(2)}, u32[]{:S(2)}) %all-to-all-start.3) | async-done | bytes 4718624 | tf_op jit(solution)/shard_map/all_to_all | solution.py:31
  385.6 1.2 slice_reduce_fusion
  386.8 0.2 reshape.120
  387.0 3.5 fusion.55
  390.5 0.1 copy.34
  390.6 9.1 %reshape.119 = bf16[640,3584,1]{1,0,2:T(8,128)(2,1)} reshape(bf16[128,140,128]{2,1,0:T(8,128)(2,1)} %bitcast.46) | data formatting | bytes 9175040 | tf_op jit(solution)/shard_map/reshape | solution.py:99
  399.7 0.6 fusion.49
  400.3 6.2 %fusion.34 = bf16[128,3584]{1,0:T(8,128)(2,1)} fusion(f32[128,2,3584]{2,0,1:T(8,128)} %fusion.42, bf16[640,3584,1]{1,0,2:T(8,128)(2,1)} %reshape.119, bf16[128,2,640]{2,1,0:T(2,128)(2,1)S(1)} %fusion.40), kind=kOutput, calls=%fused_computation.45 | convolution fusion | flops 1176698880 | bytes 9502720 | tf_op jit(solution)/shard_map/tpj,jd->tpd/dot_general | solution.py:101
  (5 shorter events, 0.0 us)
Async XLA Ops:
  10.4 120.0 %all-to-all-start = ((bf16[128,280,128]{2,1,0:T(8,128)(2,1)}), bf16[128,280,128]{2,1,0:T(8,128)(2,1)}, u32[]{:S(2)}, u32[]{:S(2)}) async-start(bf16[128,280,128]{2,1,0:T(8,128)(2,1)} %bitcast.48), calls=%async_computation | async-start | bytes 18350080 | tf_op jit(solution)/shard_map/all_to_all | solution.py:31
  130.4 120.0 %all-to-all-start.2 = ((bf16[128,280,128]{2,1,0:T(8,128)(2,1)}), bf16[128,280,128]{2,1,0:T(8,128)(2,1)}, u32[]{:S(2)}, u32[]{:S(2)}) async-start(bf16[128,280,128]{2,1,0:T(8,128)(2,1)} %bitcast.47), calls=%async_computation.2 | async-start | bytes 18350080 | tf_op jit(solution)/shard_map/all_to_all | solution.py:31
  156.2 8.6 %copy-start = (bf16[640,7168]{1,0:T(8,128)(2,1)S(1)}, bf16[640,7168]{1,0:T(8,128)(2,1)}, u32[]{:S(2)}) copy-start(bf16[640,7168]{1,0:T(8,128)(2,1)} %reshape.87) | copy-start | bytes 27525124
  250.4 70.1 %all-to-all-start.1 = ((bf16[128,144,128]{2,1,0:T(8,128)(2,1)}), bf16[128,144,128]{2,1,0:T(8,128)(2,1)}, u32[]{:S(2)}, u32[]{:S(2)}) async-start(bf16[128,144,128]{2,1,0:T(8,128)(2,1)} %fusion.21), calls=%async_computation.1 | async-start | bytes 9437184 | tf_op jit(solution)/shard_map/all_to_all | solution.py:31
  276.0 8.6 %copy-start.1 = (bf16[640,7168]{1,0:T(8,128)(2,1)S(1)}, bf16[640,7168]{1,0:T(8,128)(2,1)}, u32[]{:S(2)}) copy-start(bf16[640,7168]{1,0:T(8,128)(2,1)} %reshape.91) | copy-start | bytes 27525124
  317.2 10.2 %copy-start.2 = (bf16[128,8]{0,1:T(8,128)(2,1)S(1)}, bf16[128,8]{0,1:T(8,128)(2,1)}, u32[]{:S(2)}) copy-start(bf16[128,8]{0,1:T(8,128)(2,1)} %param.9) | copy-start | bytes 6148
  320.5 65.1 %all-to-all-start.3 = ((bf16[128,144,128]{2,1,0:T(8,128)(2,1)}), bf16[128,144,128]{2,1,0:T(8,128)(2,1)}, u32[]{:S(2)}, u32[]{:S(2)}) async-start(bf16[128,144,128]{2,1,0:T(8,128)(2,1)} %fusion.22), calls=%async_computation.3 | async-start | bytes 9437184 | tf_op jit(solution)/shard_map/all_to_all | solution.py:31

commit v9 on v8

--- a/solution.py
+++ b/solution.py
@@ -87,6 +87,8 @@
             axis=1,
         )
         returned = exchange(back)
+        rows_back = returned[:, :back_blocks, :].reshape(part_rows, features)
+        gate_block = returned[:, back_blocks, :]
         in_chunk = slot_flat // part == c
         spot = jnp.where(in_chunk, expert_flat * part + slot_flat - c * part, -1)
         onehot = (
@@ -95,11 +97,13 @@
         chooser = jnp.einsum(
             "tpk,tkj->tpj", pick, onehot, preferred_element_type=jnp.float32
         ).astype(jnp.bfloat16)
-        onehot, chooser = lax.optimization_barrier((onehot, chooser))
-        rows_back = returned[:, :back_blocks, :].reshape(part_rows, features)
-        gates_back = returned[:, back_blocks, :part].reshape(part_rows)
         partial = jnp.einsum("tpj,jd->tpd", chooser, rows_back, preferred_element_type=jnp.float32)
-        gate_part = jnp.einsum("tkj,j->tk", onehot, gates_back, preferred_element_type=jnp.float32)
+        expert_hot = jnp.logical_and(
+            expert_flat[:, None] == jnp.arange(experts, dtype=jnp.int32), in_chunk[:, None]
+        ).astype(jnp.bfloat16)
+        gate_rows_of = jnp.dot(expert_hot, gate_block, preferred_element_type=jnp.float32)
+        lane = (slot_flat - c * part)[:, None] == jnp.arange(LANES, dtype=jnp.int32)
+        gate_part = jnp.sum(jnp.where(lane, gate_rows_of, 0.0), axis=1).reshape(rows_dev, TOPK)
         if c < CHUNKS - 1:
             partial, gate_part = lax.optimization_barrier((partial, gate_part))
         summed = partial if summed is None else summed + partial

time: 409 us -> 405 us (level)
  matrix products: 72.9 us -> 67 us
    dot_general x2, matrix products: 7.07 us -> 1.11 us  [layer(): jnp.dot(expert_hot, gate_block, preferred_element_type=jnp.float32)]
  transfers between devices with their start and end apart: 4 -> 4, of which waited for: 4 -> 4; matrix products, arithmetic and copies ran while one was open for 34% -> 33% of each run, Pallas kernels for 0% -> 0%
where the time goes in v9:
time: 405 us; the launch traced here: 403 us
  waiting for transfers between devices  199 us (49%)
  local copies, waits for them, and re-layouts  81 us (20%)
  matrix products  67 us (17%)
  starting transfers between devices  42.5 us (10%)
  other arithmetic  13.2 us (3%)
    all_to_all x4, waiting for transfers between devices, exchange(): lax.all_to_all(x, ('group', 'dev'), split_axis=0, concat_axis=0, tiled=True)  199 us
    all_to_all x4, starting transfers between devices, exchange(): lax.all_to_all(x, ('group', 'dev'), split_axis=0, concat_axis=0, tiled=True)  42.5 us
    reshape x2, local copies, waits for them, and re-layouts, layer(): data = arrived.reshape(part_rows, both)  27.6 us
    dot_general x2, matrix products, expert_rows(): lax.dot_general(inner_grad, up_matrix, (((1,), (1,)), ((), ())), preferre...  20.2 us
    reshape x2, local copies, waits for them, and re-layouts, layer(): contrib.reshape(experts, back_blocks, LANES)  19.2 us
    reshape x2, local copies, waits for them, and re-layouts, layer(): rows_back = returned[:, :back_blocks, :].reshape(part_rows, features)  18.1 us
    dot_general x2, matrix products, expert_rows(): raised = jnp.dot(token_rows, up_matrix, preferred_element_type=jnp.float32)  17.3 us
    dot_general x2, matrix products, expert_rows(): lax.dot_general(grad_rows, down_matrix, (((1,), (1,)), ((), ())), preferr...  15.3 us
  transfers between devices with their start and end apart: 4, of which 4 were waited for; matrix products, arithmetic and copies ran while one was open for 33% of the time, Pallas kernels for 0%

profile of v9, /device:TPU:1, one launch (start us, length us, event | category | flops | bytes accessed | tf_op | source)
XLA Modules:
  0.0 403.2 jit_solution(16166319599670686154)
XLA Ops:
  0.6 0.7 add_select_fusion.6
  1.4 0.1 copy.21
  1.5 0.1 eq.132
  1.5 0.8 select_reduce_fusion
  2.3 0.1 reshape.125
  2.5 0.1 compare_select_fusion
  2.6 0.2 reshape.138
  2.8 1.6 fusion.31
  4.5 0.4 copy.33
  4.9 0.3 slice.58
  5.2 5.2 %gather_fusion = bf16[640,56,128]{2,1,0:T(8,128)(2,1)} fusion(bf16[129,56,128]{2,1,0:T(8,128)(2,1)S(1)} %slice.58, s32[1024]{0:T(1024)S(1)} %pad_clamp_fusion.1), kind=kCustom, calls=%fused_computation | custom fusion | bytes 18352640 | tf_op jit(solution)/shard_map/gather | solution.py:75
  10.4 11.9 %all-to-all-start = ((bf16[128,280,128]{2,1,0:T(8,128)(2,1)}), bf16[128,280,128]{2,1,0:T(8,128)(2,1)}, u32[]{:S(2)}, u32[]{:S(2)}) async-start(bf16[128,280,128]{2,1,0:T(8,128)(2,1)} %bitcast.45), calls=%async_computation | async-start | bytes 18350080 | tf_op jit(solution)/shard_map/all_to_all | solution.py:31
  22.3 0.2 reshape.146
  22.5 5.3 %gather_fusion.1 = bf16[640,56,128]{2,1,0:T(8,128)(2,1)} fusion(bf16[129,56,128]{2,1,0:T(8,128)(2,1)S(1)} %slice.58, s32[1024]{0:T(1024)S(1)} %pad_clamp_fusion), kind=kCustom, calls=%fused_computation.1 | custom fusion | bytes 18352640 | tf_op jit(solution)/shard_map/gather | solution.py:75
  27.8 102.6 %all-to-all-done = bf16[128,280,128]{2,1,0:T(8,128)(2,1)} async-done(((bf16[128,280,128]{2,1,0:T(8,128)(2,1)}), bf16[128,280,128]{2,1,0:T(8,128)(2,1)}, u32[]{:S(2)}, u32[]{:S(2)}) %all-to-all-start) | async-done | bytes 9175072 | tf_op jit(solution)/shard_map/all_to_all | solution.py:31
  130.4 11.9 %all-to-all-start.2 = ((bf16[128,280,128]{2,1,0:T(8,128)(2,1)}), bf16[128,280,128]{2,1,0:T(8,128)(2,1)}, u32[]{:S(2)}, u32[]{:S(2)}) async-start(bf16[128,280,128]{2,1,0:T(8,128)(2,1)} %bitcast.44), calls=%async_computation.2 | async-start | bytes 18350080 | tf_op jit(solution)/shard_map/all_to_all | solution.py:31
  142.3 13.8 %reshape.127 = bf16[640,7168]{1,0:T(8,128)(2,1)} reshape(bf16[128,280,128]{2,1,0:T(8,128)(2,1)} %all-to-all-done) | data formatting | bytes 18350080 | tf_op jit(solution)/shard_map/reshape | solution.py:77
  156.2 0.0 copy-start
  156.2 8.6 %fusion.8 = f32[640,1024]{1,0:T(8,128)S(1)} fusion(bf16[1,3584,1024]{2,1,0:T(8,128)(2,1)} %param.12, bf16[640,7168]{1,0:T(8,128)(2,1)} %reshape.127), kind=kOutput, calls=%fused_computation.11 | convolution fusion | flops 4697620480 | bytes 14548992 | tf_op jit(solution)/shard_map/dot_general | solution.py:18
  164.8 0.0 copy-done
  164.8 7.6 %multiply_reduce_fusion.1 = (bf16[640]{0:T(1024)(128)(2,1)S(1)}, f32[640,1024]{1,0:T(8,128)S(1)}) fusion(f32[640,1024]{1,0:T(8,128)S(1)} %fusion.8, bf16[1,1024,3584]{2,1,0:T(8,128)(2,1)} %param.13, bf16[640,7168]{1,0:T(8,128)(2,1)S(1)} %copy-done), kind=kOutput, calls=%fused_computation.36 | convolution fusion | flops 4701552128 | bytes 17171712 | tf_op jit(solution)/shard_map/dot_general | solution.py:19
  172.5 10.1 %fusion.14 = bf16[640,3584]{1,0:T(8,128)(2,1)} fusion(bf16[1,3584,1024]{2,1,0:T(8,128)(2,1)} %param.12, f32[640,1024]{1,0:T(8,128)S(1)} %get-tuple-element.21, f32[640,1024]{1,0:T(8,128)S(1)} %fusion.8), kind=kOutput, calls=%fused_computation.17 | convolution fusion | flops 4705812480 | bytes 17170432 | tf_op jit(solution)/shard_map/dot_general | solution.py:24
  182.6 9.6 %reshape.128 = bf16[128,140,128]{2,1,0:T(8,128)(2,1)} reshape(bf16[640,3584]{1,0:T(8,128)(2,1)} %fusion.14) | data formatting | bytes 9175040 | tf_op jit(solution)/shard_map/reshape | solution.py:84
  192.2 0.2 convert_element_type.71
  192.4 5.0 %fusion.21 = bf16[128,144,128]{2,1,0:T(8,128)(2,1)} fusion(bf16[128,1,5]{2,1,0:T(2,128)(2,1)S(1)} %convert_element_type.71, bf16[128,140,128]{2,1,0:T(8,128)(2,1)} %reshape.128), kind=kLoop, calls=%fused_computation.23 | loop fusion | flops 14155776 | bytes 9307392 | tf_op jit(solution)/shard_map/concatenate | solution.py:82
  197.4 53.0 %all-to-all-done.2 = bf16[128,280,128]{2,1,0:T(8,128)(2,1)} async-done(((bf16[128,280,128]{2,1,0:T(8,128)(2,1)}), bf16[128,280,128]{2,1,0:T(8,128)(2,1)}, u32[]{:S(2)}, u32[]{:S(2)}) %all-to-all-start.2) | async-done | bytes 9175072 | tf_op jit(solution)/shard_map/all_to_all | solution.py:31
  250.4 11.8 %all-to-all-start.1 = ((bf16[128,144,128]{2,1,0:T(8,128)(2,1)}), bf16[128,144,128]{2,1,0:T(8,128)(2,1)}, u32[]{:S(2)}, u32[]{:S(2)}) async-start(bf16[128,144,128]{2,1,0:T(8,128)(2,1)} %fusion.21), calls=%async_computation.1 | async-start | bytes 9437184 | tf_op jit(solution)/shard_map/all_to_all | solution.py:31
  262.2 13.8 %reshape.132 = bf16[640,7168]{1,0:T(8,128)(2,1)} reshape(bf16[128,280,128]{2,1,0:T(8,128)(2,1)} %all-to-all-done.2) | data formatting | bytes 18350080 | tf_op jit(solution)/shard_map/reshape | solution.py:77
  276.0 0.0 copy-start.1
  276.0 8.6 %fusion.4 = f32[640,1024]{1,0:T(8,128)S(1)} fusion(bf16[1,3584,1024]{2,1,0:T(8,128)(2,1)} %param.12, bf16[640,7168]{1,0:T(8,128)(2,1)} %reshape.132), kind=kOutput, calls=%fused_computation.7 | convolution fusion | flops 4697620480 | bytes 14548992 | tf_op jit(solution)/shard_map/dot_general | solution.py:18
  284.7 0.0 copy-done.1
  284.7 7.6 %multiply_reduce_fusion = (bf16[640]{0:T(1024)(128)(2,1)S(1)}, f32[640,1024]{1,0:T(8,128)S(1)}) fusion(f32[640,1024]{1,0:T(8,128)S(1)} %fusion.4, bf16[1,1024,3584]{2,1,0:T(8,128)(2,1)} %param.13, bf16[640,7168]{1,0:T(8,128)(2,1)S(1)} %copy-done.1), kind=kOutput, calls=%fused_computation.32 | convolution fusion | flops 4701552128 | bytes 17171712 | tf_op jit(solution)/shard_map/dot_general | solution.py:19
  292.3 10.0 %fusion.17 = bf16[640,3584]{1,0:T(8,128)(2,1)} fusion(bf16[1,3584,1024]{2,1,0:T(8,128)(2,1)} %param.12, f32[640,1024]{1,0:T(8,128)S(1)} %get-tuple-element.23, f32[640,1024]{1,0:T(8,128)S(1)} %fusion.4), kind=kOutput, calls=%fused_computation.18 | convolution fusion | flops 4705812480 | bytes 17170432 | tf_op jit(solution)/shard_map/dot_general | solution.py:24
  302.4 9.6 %reshape.133 = bf16[128,140,128]{2,1,0:T(8,128)(2,1)} reshape(bf16[640,3584]{1,0:T(8,128)(2,1)} %fusion.17) | data formatting | bytes 9175040 | tf_op jit(solution)/shard_map/reshape | solution.py:84
  312.0 0.2 convert_element_type.72
  312.3 4.9 %fusion.22 = bf16[128,144,128]{2,1,0:T(8,128)(2,1)} fusion(bf16[128,1,5]{2,1,0:T(2,128)(2,1)S(1)} %convert_element_type.72, bf16[128,140,128]{2,1,0:T(8,128)(2,1)} %reshape.133), kind=kLoop, calls=%fused_computation.24 | loop fusion | flops 14155776 | bytes 9307392 | tf_op jit(solution)/shard_map/concatenate | solution.py:82
  317.2 0.0 copy-start.2
  317.2 0.0 copy-start.3
  317.2 3.3 all-to-all-done.1
  320.5 6.9 %all-to-all-start.3 = ((bf16[128,144,128]{2,1,0:T(8,128)(2,1)}), bf16[128,144,128]{2,1,0:T(8,128)(2,1)}, u32[]{:S(2)}, u32[]{:S(2)}) async-start(bf16[128,144,128]{2,1,0:T(8,128)(2,1)} %fusion.22), calls=%async_computation.3 | async-start | bytes 9437184 | tf_op jit(solution)/shard_map/all_to_all | solution.py:31
  327.3 0.0 copy-done.2
  327.4 0.1 copy.24
  327.5 0.0 copy-done.3
  327.5 0.1 copy.25
  327.6 0.0 copy-done.4
  327.6 0.1 copy.20
  327.7 0.1 copy.19
  327.8 0.1 eq.136
  327.9 0.1 eq.140
  328.0 0.1 copy.26
  328.2 0.6 fusion.38
  328.8 0.6 fusion.37
  329.5 9.1 %reshape.158 = bf16[640,3584,1]{1,0,2:T(8,128)(2,1)} reshape(bf16[128,140,128]{2,1,0:T(8,128)(2,1)} %bitcast.42) | data formatting | bytes 9175040 | tf_op jit(solution)/shard_map/reshape | solution.py:90
  338.5 1.0 slice.52
  339.5 0.6 fusion.39
  340.1 0.1 reshape.130
  340.2 5.7 %fusion.46 = f32[128,2,3584]{2,0,1:T(8,128)} fusion(bf16[640,3584,1]{1,0,2:T(8,128)(2,1)} %reshape.158, bf16[128,2,640]{2,1,0:T(2,128)(2,1)S(1)} %fusion.38), kind=kOutput, calls=%fused_computation.60 | convolution fusion | flops 1174405120 | bytes 8585216 | tf_op jit(solution)/shard_map/tpj,jd->tpd/dot_general | solution.py:100
  345.9 39.7 %all-to-all-done.3 = bf16[128,144,128]{2,1,0:T(8,128)(2,1)} async-done(((bf16[128,144,128]{2,1,0:T(8,128)(2,1)}), bf16[128,144,128]{2,1,0:T(8,128)(2,1)}, u32[]{:S(2)}, u32[]{:S(2)}) %all-to-all-start.3) | async-done | bytes 4718624 | tf_op jit(solution)/shard_map/all_to_all | solution.py:31
  385.6 1.0 slice.57
  386.6 0.6 fusion.40
  387.2 0.1 reshape.135
  387.3 0.7 copy.30
  387.9 9.0 %reshape.159 = bf16[640,3584,1]{1,0,2:T(8,128)(2,1)} reshape(bf16[128,140,128]{2,1,0:T(8,128)(2,1)} %bitcast.43) | data formatting | bytes 9175040 | tf_op jit(solution)/shard_map/reshape | solution.py:90
  397.0 6.2 %fusion.32 = bf16[128,3584]{1,0:T(8,128)(2,1)} fusion(f32[128,2,3584]{2,0,1:T(8,128)} %fusion.46, bf16[640,3584,1]{1,0,2:T(8,128)(2,1)} %reshape.159, bf16[128,2,640]{2,1,0:T(2,128)(2,1)S(1)} %fusion.37), kind=kOutput, calls=%fused_computation.43 | convolution fusion | flops 1176698880 | bytes 9502720 | tf_op jit(solution)/shard_map/tpj,jd->tpd/dot_general | solution.py:100
  (9 shorter events, 0.1 us)
Async XLA Ops:
  10.4 120.0 %all-to-all-start = ((bf16[128,280,128]{2,1,0:T(8,128)(2,1)}), bf16[128,280,128]{2,1,0:T(8,128)(2,1)}, u32[]{:S(2)}, u32[]{:S(2)}) async-start(bf16[128,280,128]{2,1,0:T(8,128)(2,1)} %bitcast.45), calls=%async_computation | async-start | bytes 18350080 | tf_op jit(solution)/shard_map/all_to_all | solution.py:31
  130.4 120.0 %all-to-all-start.2 = ((bf16[128,280,128]{2,1,0:T(8,128)(2,1)}), bf16[128,280,128]{2,1,0:T(8,128)(2,1)}, u32[]{:S(2)}, u32[]{:S(2)}) async-start(bf16[128,280,128]{2,1,0:T(8,128)(2,1)} %bitcast.44), calls=%async_computation.2 | async-start | bytes 18350080 | tf_op jit(solution)/shard_map/all_to_all | solution.py:31
  156.2 8.6 %copy-start = (bf16[640,7168]{1,0:T(8,128)(2,1)S(1)}, bf16[640,7168]{1,0:T(8,128)(2,1)}, u32[]{:S(2)}) copy-start(bf16[640,7168]{1,0:T(8,128)(2,1)} %reshape.127) | copy-start | bytes 27525124
  250.4 70.1 %all-to-all-start.1 = ((bf16[128,144,128]{2,1,0:T(8,128)(2,1)}), bf16[128,144,128]{2,1,0:T(8,128)(2,1)}, u32[]{:S(2)}, u32[]{:S(2)}) async-start(bf16[128,144,128]{2,1,0:T(8,128)(2,1)} %fusion.21), calls=%async_computation.1 | async-start | bytes 9437184 | tf_op jit(solution)/shard_map/all_to_all | solution.py:31
  276.0 8.6 %copy-start.1 = (bf16[640,7168]{1,0:T(8,128)(2,1)S(1)}, bf16[640,7168]{1,0:T(8,128)(2,1)}, u32[]{:S(2)}) copy-start(bf16[640,7168]{1,0:T(8,128)(2,1)} %reshape.132) | copy-start | bytes 27525124
  317.2 10.2 %copy-start.2 = (s32[128,8]{0,1:T(8,128)S(1)}, s32[128,8]{0,1:T(8,128)}, u32[]{:S(2)}) copy-start(s32[128,8]{0,1:T(8,128)} %param.11) | copy-start | bytes 12292
  317.2 10.3 %copy-start.3 = (s32[128,8]{0,1:T(8,128)S(1)}, s32[128,8]{0,1:T(8,128)}, u32[]{:S(2)}) copy-start(s32[128,8]{0,1:T(8,128)} %param.10) | copy-start | bytes 12292
  317.2 10.4 %copy-start.4 = (bf16[128,8]{0,1:T(8,128)(2,1)S(1)}, bf16[128,8]{0,1:T(8,128)(2,1)}, u32[]{:S(2)}) copy-start(bf16[128,8]{0,1:T(8,128)(2,1)} %param.9) | copy-start | bytes 6148
  320.5 65.1 %all-to-all-start.3 = ((bf16[128,144,128]{2,1,0:T(8,128)(2,1)}), bf16[128,144,128]{2,1,0:T(8,128)(2,1)}, u32[]{:S(2)}, u32[]{:S(2)}) async-start(bf16[128,144,128]{2,1,0:T(8,128)(2,1)} %fusion.22), calls=%async_computation.3 | async-start | bytes 9437184 | tf_op jit(solution)/shard_map/all_to_all | solution.py:31
